TPU v7x, 512 devices: a whole 4x4x16 slice. The times are simulated.
512 devices in a mesh: dp: 4 (over y), seq: 16 (over z), section: 8 (over x, core).
Axes of the slice: x: 4, y: 4, z: 16, core: 2. Of those that a mesh axis runs over, the one named last changes fastest.
Arguments:
- signal: bfloat16 [4, 10240, 1280], P('dp', 'seq'), may hold values from -6 to 6
- kernel: bfloat16 [1536, 5, 1280], P('section'), may hold values from -0.078125 to 0.078125
- trunk_grad: bfloat16 [4, 5120, 1536], P('dp', ('seq', 'section')), may hold values from -24 to 24
Outputs:
- weight_grad: float32 [1536, 5, 1280], P(('section', 'seq'))
- input_grad: bfloat16 [4, 1280, 10240], P('dp', 'section', 'seq')
All inputs are finite; a program needn't handle non-finite values.
Results may differ from a plain program's by a relative error of at most 0.019.
Values may be sent and summed in bfloat16 or wider, within the bound.
No kernel may reach another device: no remote copies, remote signals or barrier semaphores. Data moves between devices by JAX's collectives and lax.ppermute only.
A program may use at most 64 MiB of HBM per device.

v0:
```python
import jax
import jax.numpy as jnp
from jax import lax
from jax.sharding import PartitionSpec as P


def extended(block, sides, width):
    for axis, dim in sides:
        count = lax.axis_size(axis)
        forward = [(i, i + 1) for i in range(count - 1)]
        backward = [(target, source) for source, target in forward]
        low = lax.ppermute(
            lax.slice_in_dim(block, block.shape[dim] - width, None, axis=dim), axis, forward
        )
        high = lax.ppermute(lax.slice_in_dim(block, 0, width, axis=dim), axis, backward)
        block = jnp.concatenate([low, block, high], axis=dim)
    return block


def gelu_slope(values):
    normal_cdf = 0.5 * (1.0 + jax.scipy.special.erf(values * 0.7071067811865476))
    density = jnp.exp(-0.5 * values * values) * 0.3989422804014327
    return normal_cdf + values * density


def convolve(padded, kernel, out_rows):
    linear = jnp.einsum(
        "lc,oc->lo", padded[0:out_rows], kernel[:, 0, :], preferred_element_type=jnp.float32
    )
    for offset in range(1, kernel.shape[1]):
        linear = linear + jnp.einsum(
            "lc,oc->lo",
            padded[offset : offset + out_rows],
            kernel[:, offset, :],
            preferred_element_type=jnp.float32,
        )
    return linear


def shards(signal, kernel, trunk_grad):
    local_signal = signal[0]
    length = local_signal.shape[0]
    taps_count = kernel.shape[1]
    pooled = lax.all_to_all(trunk_grad, "section", split_axis=2, concat_axis=1, tiled=True)[0]
    padded = extended(local_signal, (("seq", 0),), 2)
    linear = convolve(padded, kernel, length)
    grad_hidden = 0.5 * jnp.repeat(pooled.astype(jnp.float32), 2, axis=0)
    grad_pre = (grad_hidden * gelu_slope(linear)).astype(jnp.bfloat16)
    grad_ext = extended(grad_pre, (("seq", 0),), 2)
    grad_middle = grad_ext[2 : 2 + length]
    taps = []
    for offset in range(taps_count):
        taps.append(
            jnp.einsum(
                "lo,lc->oc",
                grad_middle,
                padded[offset : offset + length],
                preferred_element_type=jnp.float32,
            )
        )
    weight_rows = lax.psum_scatter(
        jnp.stack(taps, axis=1).astype(jnp.bfloat16), "seq", scatter_dimension=0, tiled=True
    )
    weight_grad = lax.psum(weight_rows, "dp").astype(jnp.float32)
    summed = jnp.einsum(
        "lo,oc->cl", grad_ext[4 : 4 + length], kernel[:, 0, :], preferred_element_type=jnp.float32
    )
    for offset in range(1, taps_count):
        summed = summed + jnp.einsum(
            "lo,oc->cl",
            grad_ext[4 - offset : 4 - offset + length],
            kernel[:, offset, :],
            preferred_element_type=jnp.float32,
        )
    input_rows = lax.psum_scatter(
        summed.astype(jnp.bfloat16), "section", scatter_dimension=0, tiled=True
    )
    return (weight_grad, input_rows[None])


def solution(mesh):
    return jax.shard_map(
        shards,
        mesh=mesh,
        in_specs=(
            P("dp", "seq", None),
            P("section", None, None),
            P("dp", ("seq", "section"), None),
        ),
        out_specs=(P(("section", "seq"), None, None), P("dp", "section", "seq")),
        check_vma=False,
    )
```

profile of v0, /device:TPU:6, one launch (start us, length us, event | category | flops | bytes accessed | tf_op | source)
XLA Modules:
  0.0 269.3 jit_solution(15086313837585822264)
XLA Ops:
  8.0 0.9 slice_bitcast_fusion.1
  8.9 3.8 %collective-permute-start = (bf16[2,1280]{1,0:T(2,128)(2,1)S(1)}, bf16[2,1280]{1,0:T(2,128)(2,1)S(1)}, u32[]{:S(2)}, u32[]{:S(2)}) collective-permute-start(bf16[2,1280]{1,0:T(2,128)(2,1)S(1)} %get-tuple-element.8), channel_id=1, source_target_pairs={{0,8},{8,16},{16,24},{24,32},{32,40},{40,48},{48,56},{56,64},{64,7... | collective-permute-start | bytes 15368 | tf_op jit(solution)/shard_map/ppermute | solution.py:12
  12.7 1.3 collective-permute-start.1
  14.0 1.9 copy.9
  16.5 9.6 %reduce = bf16[1536,40]{1,0:T(8,128)(2,1)} reduce(bf16[1536,1,40]{2,1,0:T(2,128)(2,1)S(1)} %bitcast.76, bf16[]{:T(256)} %broadcast.19), dimensions={1}, to_apply=%bitcast.67.reduce_sub_computation | reduce | bytes 245762
  26.0 2.2 reshape.21
  28.3 6.6 %all-to-all-start = ((bf16[8,2,3840]{2,1,0:T(2,128)(2,1)}), bf16[8,2,3840]{2,1,0:T(2,128)(2,1)S(1)}, u32[]{:S(2)}, u32[]{:S(2)}) async-start(bf16[8,2,3840]{2,1,0:T(2,128)(2,1)} %reshape.21), calls=%async_computation | async-start | bytes 245760 | tf_op jit(solution)/shard_map/all_to_all | solution.py:44
  34.9 2.2 fusion.33
  37.2 0.7 fusion.18
  37.9 1.5 fusion.16
  39.4 1.5 fusion.19
  40.9 1.2 reshape.22
  42.1 0.9 convert_multiply_fusion
  44.4 2.3 fusion.25
  46.7 0.6 fusion.5
  47.4 0.6 fusion.7
  49.8 1.4 copy-done
  51.4 1.3 dynamic-slice
  53.4 1.3 collective-permute-start.2
  54.7 1.7 fusion.31
  56.3 5.2 %collective-permute-start.3 = (bf16[2,192]{0,1:T(8,128)(2,1)S(1)}, bf16[2,192]{0,1:T(8,128)(2,1)S(1)}, u32[]{:S(2)}, u32[]{:S(2)}) collective-permute-start(bf16[2,192]{0,1:T(8,128)(2,1)S(1)} %get-tuple-element.11), channel_id=1, source_target_pairs={{0,8},{8,16},{16,24},{24,32},{32,40},{40,48},{48,56},{56,64},{64,7... | collective-permute-start | bytes 2312 | tf_op jit(solution)/shard_map/ppermute | solution.py:12
  61.5 1.8 fusion.35
  64.0 1.8 fusion.26
  65.7 3.5 %fusion.1 = f32[640,1280]{1,0:T(8,128)} fusion(f32[640,1280]{1,0:T(8,128)S(1)} %fusion.31, f32[640,1280]{1,0:T(8,128)S(1)} %fusion.35, bf16[192,5,1280]{2,0,1:T(8,128)(2,1)} %param.4, bf16[640,192]{0,1:T(8,128)(2,1)S(1)} %fusion.25, bf16[2,192]{0,1:T(8,128)(2,1)S(1)} %collective-permute-done.2), kind=kOutput, calls=%fused_computation.3 | convolution fusion | flops 316702720 | bytes 10568448 | tf_op jit(solution)/shard_map/lo,oc->cl/dot_general | solution.py:65
  69.2 133.3 %all-reduce.6.cloned.1.call-done = bf16[192,5,1280]{2,0,1:T(8,128)(2,1)} async-done(((bf16[192,5,1280]{2,0,1:T(8,128)(2,1)}), bf16[192,5,1280]{2,0,1:T(8,128)(2,1)}) %all-reduce.6.cloned.1.call-update) | async-done | bytes 2457616
  202.5 1.7 constant_dynamic-slice_fusion
  204.3 4.1 %fusion.3 = bf16[1280,640]{0,1:T(8,128)(2,1)} fusion(f32[640,1280]{1,0:T(8,128)S(1)} %fusion.26, f32[640,1280]{1,0:T(8,128)} %fusion.1, bf16[192,5,1280]{2,0,1:T(8,128)(2,1)} %param.4, bf16[2,192]{0,1:T(8,128)(2,1)} %copy-done.5, bf16[640,192]{0,1:T(8,128)(2,1)S(1)} %fusion.25), kind=kOutput, calls=%fused_computation.5 | convolution fusion | flops 317521920 | bytes 8978432 | tf_op jit(solution)/shard_map/lo,oc->cl/dot_general | solution.py:69
  208.4 3.5 %copy.15 = bf16[1280,640]{1,0:T(8,128)(2,1)} copy(bf16[1280,640]{0,1:T(8,128)(2,1)} %fusion.3) | data formatting | bytes 3276800
  211.9 46.3 %all-reduce.4.cloned.1.call-done = bf16[12,5,1280]{2,0,1:T(8,128)(2,1)} async-done(((bf16[12,5,1280]{2,0,1:T(8,128)(2,1)}), bf16[12,5,1280]{2,0,1:T(8,128)(2,1)}) %all-reduce.4.cloned.1.call-update) | async-done | bytes 153616 | tf_op jit(solution)/shard_map/psum | solution.py:64
  258.2 1.7 convert_element_type.16
  259.9 1.1 copy.16
  261.0 0.8 copy.12
  (32 shorter events, 4.6 us)
Async XLA Ops:
  8.0 26.9 %copy-start.1 = (bf16[192,5,1280]{2,0,1:T(8,128)(2,1)S(1)}, bf16[192,5,1280]{2,0,1:T(8,128)(2,1)}, u32[]{:S(2)}) copy-start(bf16[192,5,1280]{2,0,1:T(8,128)(2,1)} %param.4) | copy-start | bytes 7372804
  8.9 28.2 %collective-permute-start = (bf16[2,1280]{1,0:T(2,128)(2,1)S(1)}, bf16[2,1280]{1,0:T(2,128)(2,1)S(1)}, u32[]{:S(2)}, u32[]{:S(2)}) collective-permute-start(bf16[2,1280]{1,0:T(2,128)(2,1)S(1)} %get-tuple-element.8), channel_id=1, source_target_pairs={{0,8},{8,16},{16,24},{24,32},{32,40},{40,48},{48,56},{56,64},{64,7... | collective-permute-start | bytes 15368 | tf_op jit(solution)/shard_map/ppermute | solution.py:12
  12.7 26.7 %collective-permute-start.1 = (bf16[2,1280]{1,0:T(2,128)(2,1)S(1)}, bf16[2,1280]{1,0:T(2,128)(2,1)S(1)}, u32[]{:S(2)}, u32[]{:S(2)}) collective-permute-start(bf16[2,1280]{1,0:T(2,128)(2,1)S(1)} %get-tuple-element.9), channel_id=1, source_target_pairs={{8,0},{16,8},{24,16},{32,24},{40,32},{48,40},{56,48},{64,56},{72,6... | collective-permute-start | bytes 15368 | tf_op jit(solution)/shard_map/ppermute | solution.py:15
  28.3 12.6 %all-to-all-start = ((bf16[8,2,3840]{2,1,0:T(2,128)(2,1)}), bf16[8,2,3840]{2,1,0:T(2,128)(2,1)S(1)}, u32[]{:S(2)}, u32[]{:S(2)}) async-start(bf16[8,2,3840]{2,1,0:T(2,128)(2,1)} %reshape.21), calls=%async_computation | async-start | bytes 245760 | tf_op jit(solution)/shard_map/all_to_all | solution.py:44
  34.9 167.7 %all-reduce.6.cloned.1.call-start = ((), (), s32[]{:S(2)}) async-start(), calls=%async_computation.4 | async-start | bytes 4915200
  34.9 2.3 copy-start.2
  42.9 1.4 copy-start.3
  44.4 2.3 copy-start.4
  49.8 1.5 copy-start
  51.3 206.9 %all-reduce.4.cloned.1.call-start = ((), (), s32[]{:S(2)}) async-start(), calls=%async_computation.2 | async-start | bytes 409600 | tf_op jit(solution)/shard_map/psum | solution.py:64
  53.4 8.2 %collective-permute-start.2 = (bf16[2,192]{0,1:T(8,128)(2,1)S(1)}, bf16[2,192]{0,1:T(8,128)(2,1)S(1)}, u32[]{:S(2)}, u32[]{:S(2)}) collective-permute-start(bf16[2,192]{0,1:T(8,128)(2,1)S(1)} %get-tuple-element.10), channel_id=1, source_target_pairs={{8,0},{16,8},{24,16},{32,24},{40,32},{48,40},{56,48},{64,56},{72,6... | collective-permute-start | bytes 2312 | tf_op jit(solution)/shard_map/ppermute | solution.py:15
  56.3 7.0 %collective-permute-start.3 = (bf16[2,192]{0,1:T(8,128)(2,1)S(1)}, bf16[2,192]{0,1:T(8,128)(2,1)S(1)}, u32[]{:S(2)}, u32[]{:S(2)}) collective-permute-start(bf16[2,192]{0,1:T(8,128)(2,1)S(1)} %get-tuple-element.11), channel_id=1, source_target_pairs={{0,8},{8,16},{16,24},{24,32},{32,40},{40,48},{48,56},{56,64},{64,7... | collective-permute-start | bytes 2312 | tf_op jit(solution)/shard_map/ppermute | solution.py:12
  63.3 0.6 copy-start.5
  204.3 55.7 %reduce-scatter.5.cloned.1.call-start = ((), (), s32[]{:S(2)}) async-start(), calls=%async_computation.3 | async-start | bytes 1843200
Sparse Core Ops, SparseCore 0:
  51.4 151.0 all-reduce.5
  205.4 52.7 all-reduce.3
Sparse Core Ops, SparseCore 1:
  212.0 33.1 reduce-scatter.4
where the time goes:
time: 270 us; the launch traced here: 269 us
  waiting for transfers between devices  180 us (67%)
  matrix products  24.2 us (9%)
  local copies, waits for them, and re-layouts  18.7 us (7%)
  starting transfers between devices  18.3 us (7%)
  between operations  16.4 us (6%)
  other arithmetic  12.1 us (4%)
    unnamed x5, waiting for transfers between devices  133 us
    psum x1, waiting for transfers between devices, shards(): weight_grad = lax.psum(weight_rows, 'dp').astype(jnp.float32)  46.3 us
    unnamed x21, local copies, waits for them, and re-layouts  16.5 us
    unnamed x1, other arithmetic  9.56 us
    dot_general x4, matrix products, shards(): jnp.einsum('lo,oc->cl', grad_ext[4 - offset:4 - offset + length], kernel[...  9.3 us
    ppermute x2, starting transfers between devices, extended(): lax.ppermute(lax.slice_in_dim(block, block.shape[dim] - width, None, axis...  8.99 us
    dot_general x4, matrix products, convolve(): jnp.einsum('lc,oc->lo', padded[offset:offset + out_rows], kernel[:, offse...  6.77 us
    all_to_all x1, starting transfers between devices, shards(): lax.all_to_all(trunk_grad, 'section', split_axis=2, concat_axis=1, tiled=...  6.63 us
  transfers between devices with their start and end apart: 8, of which 2 were waited for; matrix products, arithmetic and copies ran while one was open for 15% of the time, Pallas kernels for 0%

commit v1 on v0

--- a/solution.py
+++ b/solution.py
@@ -41,7 +41,12 @@
     local_signal = signal[0]
     length = local_signal.shape[0]
     taps_count = kernel.shape[1]
-    pooled = lax.all_to_all(trunk_grad, "section", split_axis=2, concat_axis=1, tiled=True)[0]
+    out_ch = kernel.shape[0]
+    in_ch = kernel.shape[2]
+    n_section = lax.axis_size("section")
+    rows = trunk_grad.shape[1]
+    grouped = trunk_grad[0].reshape(rows, n_section, out_ch).transpose(1, 0, 2)
+    pooled = lax.all_to_all(grouped, "section", 0, 0, tiled=True).reshape(rows * n_section, out_ch)
     padded = extended(local_signal, (("seq", 0),), 2)
     linear = convolve(padded, kernel, length)
     grad_hidden = 0.5 * jnp.repeat(pooled.astype(jnp.float32), 2, axis=0)
@@ -56,12 +61,13 @@
                 grad_middle,
                 padded[offset : offset + length],
                 preferred_element_type=jnp.float32,
-            )
+            ).astype(jnp.bfloat16)
         )
-    weight_rows = lax.psum_scatter(
-        jnp.stack(taps, axis=1).astype(jnp.bfloat16), "seq", scatter_dimension=0, tiled=True
-    )
-    weight_grad = lax.psum(weight_rows, "dp").astype(jnp.float32)
+    n_seq = lax.axis_size("seq")
+    partial = jnp.stack(taps, axis=1).reshape(n_seq, -1, 128)
+    weight_part = lax.psum_scatter(partial, "seq", scatter_dimension=0, tiled=True)
+    weight_rows = lax.psum(weight_part, "dp")
+    weight_grad = weight_rows.reshape(-1, taps_count, in_ch).astype(jnp.float32)
     summed = jnp.einsum(
         "lo,oc->cl", grad_ext[4 : 4 + length], kernel[:, 0, :], preferred_element_type=jnp.float32
     )

time: 270 us -> 235 us (0.87)
  waiting for transfers between devices: 180 us -> 163 us
  other arithmetic: 12.1 us -> 0.02 us
  matrix products: 24.2 us -> 17.4 us
  local copies, waits for them, and re-layouts: 18.7 us -> 21.7 us
    unnamed x5, waiting for transfers between devices: 133 us -> 102 us
    psum x1, waiting for transfers between devices: 46.3 us -> 60.3 us  [shards(): weight_rows = lax.psum(weight_part, 'dp')]
    unnamed x21 -> x12, local copies, waits for them, and re-layouts: 16.5 us -> 6.46 us
    unnamed x1 -> x0, other arithmetic: 9.56 us -> none
    reshape x0 -> x1, local copies, waits for them, and re-layouts: none -> 6.51 us  [shards(): partial = jnp.stack(taps, axis=1).reshape(n_seq, -1, 128)]
    dot_general x4, matrix products: 9.3 us -> 3.95 us  [shards(): jnp.einsum('lo,oc->cl', grad_ext[4 - offset:4 - offset + length], kernel[...]
    another operation x0 -> x3, local copies, waits for them, and re-layouts: none -> 5.09 us  [the longest x1 3.31 us: shards(): partial = jnp.stack(taps, axis=1).reshape(n_seq, -1, 128)]
    dot_general x1, matrix products: 3.49 us -> 0.78 us  [shards(): jnp.einsum('lo,oc->cl', grad_ext[4:4 + length], kernel[:, 0, :], preferre...]
  transfers between devices with their start and end apart: 8 -> 8, of which waited for: 2 -> 4; matrix products, arithmetic and copies ran while one was open for 15% -> 9% of each run, Pallas kernels for 0% -> 0%
where the time goes in v1:
time: 235 us
  waiting for transfers between devices  163 us (69%)
  local copies, waits for them, and re-layouts  21.7 us (9%)
  starting transfers between devices  18.5 us (8%)
  matrix products  17.4 us (7%)
  between operations  13.9 us (6%)
    unnamed x5, waiting for transfers between devices  102 us
    psum x1, waiting for transfers between devices, shards(): weight_rows = lax.psum(weight_part, 'dp')  60.3 us
    ppermute x2, starting transfers between devices, extended(): lax.ppermute(lax.slice_in_dim(block, block.shape[dim] - width, None, axis...  9.09 us
    dot_general x4, matrix products, convolve(): jnp.einsum('lc,oc->lo', padded[offset:offset + out_rows], kernel[:, offse...  8.17 us
    all_to_all x1, starting transfers between devices, shards(): lax.all_to_all(grouped, 'section', 0, 0, tiled=True)  6.64 us
    reshape x1, local copies, waits for them, and re-layouts, shards(): partial = jnp.stack(taps, axis=1).reshape(n_seq, -1, 128)  6.51 us
    unnamed x12, local copies, waits for them, and re-layouts  6.46 us
  transfers between devices with their start and end apart: 8, of which 4 were waited for; matrix products, arithmetic and copies ran while one was open for 9% of the time, Pallas kernels for 0%

profile of v1, /device:TPU:6, one launch (start us, length us, event | category | flops | bytes accessed | tf_op | source)
XLA Modules:
  0.0 234.7 jit_solution(15794759697085680820)
XLA Ops:
  7.2 0.9 slice_bitcast_fusion.1
  8.1 3.8 %collective-permute-start = (bf16[2,1280]{1,0:T(2,128)(2,1)S(1)}, bf16[2,1280]{1,0:T(2,128)(2,1)S(1)}, u32[]{:S(2)}, u32[]{:S(2)}) collective-permute-start(bf16[2,1280]{1,0:T(2,128)(2,1)S(1)} %get-tuple-element.8), channel_id=1, source_target_pairs={{0,8},{8,16},{16,24},{24,32},{32,40},{40,48},{48,56},{56,64},{64,7... | collective-permute-start | bytes 15368 | tf_op jit(solution)/shard_map/ppermute | solution.py:12
  11.9 1.3 collective-permute-start.1
  13.2 1.1 reshape_squeeze.3
  14.3 0.7 copy.19
  15.0 6.6 %all-to-all-start = ((bf16[8,40,192]{2,1,0:T(8,128)(2,1)}), bf16[8,40,192]{2,1,0:T(8,128)(2,1)S(1)}, u32[]{:S(2)}, u32[]{:S(2)}) async-start(bf16[8,40,192]{2,1,0:T(8,128)(2,1)} %bitcast.70), calls=%async_computation | async-start | bytes 327680 | tf_op jit(solution)/shard_map/all_to_all | solution.py:49
  21.6 2.2 fusion.33
  23.9 2.3 fusion.18
  26.2 1.5 fusion.16
  27.7 1.5 fusion.19
  30.6 2.2 fusion.25
  33.4 0.6 fusion.7
  34.6 0.6 fusion.11
  35.2 0.6 fusion.13
  35.8 3.3 %copy.13 = bf16[192,5,1280]{2,1,0:T(8,128)(2,1)} copy(bf16[192,5,1280]{2,0,1:T(8,128)(2,1)S(1)} %fusion.13) | data formatting | bytes 4915200 | tf_op jit(solution)/shard_map/stack | solution.py:67
  39.1 6.5 %reshape.19 = bf16[16,600,128]{2,1,0:T(8,128)(2,1)} reshape(bf16[192,5,1280]{2,1,0:T(8,128)(2,1)} %copy.13) | data formatting | bytes 4915200 | tf_op jit(solution)/shard_map/reshape | solution.py:67
  45.8 1.4 collective-permute-start.2
  47.3 0.6 fusion.31
  48.0 5.3 %collective-permute-start.3 = (bf16[2,192]{0,1:T(8,128)(2,1)S(1)}, bf16[2,192]{0,1:T(8,128)(2,1)S(1)}, u32[]{:S(2)}, u32[]{:S(2)}) collective-permute-start(bf16[2,192]{0,1:T(8,128)(2,1)S(1)} %get-tuple-element.11), channel_id=1, source_target_pairs={{0,8},{8,16},{16,24},{24,32},{32,40},{40,48},{48,56},{56,64},{64,7... | collective-permute-start | bytes 2312 | tf_op jit(solution)/shard_map/ppermute | solution.py:12
  53.3 0.8 fusion.35
  54.0 0.8 collective-permute-done.3
  54.8 0.7 fusion.26
  55.5 0.8 fusion.1
  56.3 1.8 fusion.3
  58.1 2.2 copy.16
  60.4 66.0 %reduce-scatter.9.cloned.1.call-done = bf16[1,600,128]{2,1,0:T(8,128)(2,1)} async-done(((bf16[16,600,128]{2,1,0:T(8,128)(2,1)}), bf16[1,600,128]{2,1,0:T(8,128)(2,1)}) %reduce-scatter.9.cloned.1.call-update) | async-done | bytes 153616
  126.4 1.8 convert_element_type.36
  128.2 36.0 %reduce-scatter.7.cloned.1.call-done = bf16[160,640]{1,0:T(8,128)(2,1)} async-done(((bf16[1280,640]{1,0:T(8,128)(2,1)}), bf16[160,640]{1,0:T(8,128)(2,1)}) %reduce-scatter.7.cloned.1.call-update) | async-done | bytes 204816
  164.2 1.1 copy.17
  165.3 0.8 copy.15
  166.2 60.3 %all-reduce.3.cloned.1.call-done = bf16[12,5,1280]{2,1,0:T(8,128)(2,1)} async-done(((bf16[12,5,1280]{2,1,0:T(8,128)(2,1)}), bf16[12,5,1280]{2,1,0:T(8,128)(2,1)}) %all-reduce.3.cloned.1.call-update) | async-done | bytes 153616 | tf_op jit(solution)/shard_map/psum | solution.py:69
  226.4 1.7 copy.14
  (25 shorter events, 2.9 us)
Async XLA Ops:
  7.2 16.7 %copy-start = (bf16[192,5,1280]{2,0,1:T(8,128)(2,1)S(1)}, bf16[192,5,1280]{2,0,1:T(8,128)(2,1)}, u32[]{:S(2)}) copy-start(bf16[192,5,1280]{2,0,1:T(8,128)(2,1)} %param.4) | copy-start | bytes 7372804
  8.1 15.8 %collective-permute-start = (bf16[2,1280]{1,0:T(2,128)(2,1)S(1)}, bf16[2,1280]{1,0:T(2,128)(2,1)S(1)}, u32[]{:S(2)}, u32[]{:S(2)}) collective-permute-start(bf16[2,1280]{1,0:T(2,128)(2,1)S(1)} %get-tuple-element.8), channel_id=1, source_target_pairs={{0,8},{8,16},{16,24},{24,32},{32,40},{40,48},{48,56},{56,64},{64,7... | collective-permute-start | bytes 15368 | tf_op jit(solution)/shard_map/ppermute | solution.py:12
  11.9 15.8 %collective-permute-start.1 = (bf16[2,1280]{1,0:T(2,128)(2,1)S(1)}, bf16[2,1280]{1,0:T(2,128)(2,1)S(1)}, u32[]{:S(2)}, u32[]{:S(2)}) collective-permute-start(bf16[2,1280]{1,0:T(2,128)(2,1)S(1)} %get-tuple-element.9), channel_id=1, source_target_pairs={{8,0},{16,8},{24,16},{32,24},{40,32},{48,40},{56,48},{64,56},{72,6... | collective-permute-start | bytes 15368 | tf_op jit(solution)/shard_map/ppermute | solution.py:15
  15.0 14.2 %all-to-all-start = ((bf16[8,40,192]{2,1,0:T(8,128)(2,1)}), bf16[8,40,192]{2,1,0:T(8,128)(2,1)S(1)}, u32[]{:S(2)}, u32[]{:S(2)}) async-start(bf16[8,40,192]{2,1,0:T(8,128)(2,1)} %bitcast.70), calls=%async_computation | async-start | bytes 327680 | tf_op jit(solution)/shard_map/all_to_all | solution.py:49
  21.6 104.7 %reduce-scatter.9.cloned.1.call-start = ((), (), s32[]{:S(2)}) async-start(), calls=%async_computation.5 | async-start | bytes 2611200
  23.9 2.3 copy-start.2
  29.2 1.4 copy-start.3
  45.6 1.7 copy-start.1
  45.7 118.6 %reduce-scatter.7.cloned.1.call-start = ((), (), s32[]{:S(2)}) async-start(), calls=%async_computation.4 | async-start | bytes 1843200
  45.8 7.4 %collective-permute-start.2 = (bf16[2,192]{0,1:T(8,128)(2,1)S(1)}, bf16[2,192]{0,1:T(8,128)(2,1)S(1)}, u32[]{:S(2)}, u32[]{:S(2)}) collective-permute-start(bf16[2,192]{0,1:T(8,128)(2,1)S(1)} %get-tuple-element.10), channel_id=1, source_target_pairs={{8,0},{16,8},{24,16},{32,24},{40,32},{48,40},{56,48},{64,56},{72,6... | collective-permute-start | bytes 2312 | tf_op jit(solution)/shard_map/ppermute | solution.py:15
  48.0 6.8 %collective-permute-start.3 = (bf16[2,192]{0,1:T(8,128)(2,1)S(1)}, bf16[2,192]{0,1:T(8,128)(2,1)S(1)}, u32[]{:S(2)}, u32[]{:S(2)}) collective-permute-start(bf16[2,192]{0,1:T(8,128)(2,1)S(1)} %get-tuple-element.11), channel_id=1, source_target_pairs={{0,8},{8,16},{16,24},{24,32},{32,40},{40,48},{48,56},{56,64},{64,7... | collective-permute-start | bytes 2312 | tf_op jit(solution)/shard_map/ppermute | solution.py:12
  60.4 166.0 %all-reduce.3.cloned.1.call-start = ((), (), s32[]{:S(2)}) async-start(), calls=%async_computation.3 | async-start | bytes 491520 | tf_op jit(solution)/shard_map/psum | solution.py:69
Sparse Core Ops, SparseCore 0:
  45.8 80.5 reduce-scatter.8
  129.2 34.9 reduce-scatter.6
  167.1 59.2 all-reduce.2

commit v2 on v1

--- a/solution.py
+++ b/solution.py
@@ -37,6 +37,19 @@
     return linear
 
 
+def butterfly_sum(block, axis):
+    count = lax.axis_size(axis)
+    if count & (count - 1):
+        return lax.psum(block.astype(jnp.float32), axis)
+    total = block.astype(jnp.float32)
+    step = 1
+    while step < count:
+        other = lax.ppermute(block if step == 1 else total, axis, [(i, i ^ step) for i in range(count)])
+        total = total + other.astype(jnp.float32)
+        step *= 2
+    return total
+
+
 def shards(signal, kernel, trunk_grad):
     local_signal = signal[0]
     length = local_signal.shape[0]
@@ -66,8 +79,8 @@
     n_seq = lax.axis_size("seq")
     partial = jnp.stack(taps, axis=1).reshape(n_seq, -1, 128)
     weight_part = lax.psum_scatter(partial, "seq", scatter_dimension=0, tiled=True)
-    weight_rows = lax.psum(weight_part, "dp")
-    weight_grad = weight_rows.reshape(-1, taps_count, in_ch).astype(jnp.float32)
+    weight_rows = butterfly_sum(weight_part, "dp")
+    weight_grad = weight_rows.reshape(-1, taps_count, in_ch)
     summed = jnp.einsum(
         "lo,oc->cl", grad_ext[4 : 4 + length], kernel[:, 0, :], preferred_element_type=jnp.float32
     )
@@ -78,9 +91,9 @@
             kernel[:, offset, :],
             preferred_element_type=jnp.float32,
         )
-    input_rows = lax.psum_scatter(
-        summed.astype(jnp.bfloat16), "section", scatter_dimension=0, tiled=True
-    )
+    groups = summed.astype(jnp.bfloat16).reshape(n_section, -1, length)
+    received = lax.all_to_all(groups, "section", 0, 0, tiled=True)
+    input_rows = jnp.sum(received.astype(jnp.float32), axis=0).astype(jnp.bfloat16)
     return (weight_grad, input_rows[None])
 
 

time: 235 us -> 155 us (0.66)
  waiting for transfers between devices: 163 us -> 72.1 us
  starting transfers between devices: 18.5 us -> 30.7 us
  local copies, waits for them, and re-layouts: 21.7 us -> 17.2 us
    psum x1 -> x0, waiting for transfers between devices: 60.3 us -> none  [shards(): weight_rows = lax.psum(weight_part, 'dp')]
    unnamed x5 -> x2, waiting for transfers between devices: 102 us -> 61.3 us
    ppermute x0 -> x2, waiting for transfers between devices: none -> 9.97 us  [butterfly_sum(): lax.ppermute(block if step == 1 else total, axis, [(i, i ^ step) for i in...]
    ppermute x0 -> x2, starting transfers between devices: none -> 7.49 us  [butterfly_sum(): lax.ppermute(block if step == 1 else total, axis, [(i, i ^ step) for i in...]
    unnamed x12 -> x11, local copies, waits for them, and re-layouts: 6.46 us -> 1.5 us
    all_to_all x0 -> x1, starting transfers between devices: none -> 4.8 us  [shards(): received = lax.all_to_all(groups, 'section', 0, 0, tiled=True)]
  transfers between devices with their start and end apart: 8 -> 9, of which waited for: 4 -> 4; matrix products, arithmetic and copies ran while one was open for 9% -> 12% of each run, Pallas kernels for 0% -> 0%
where the time goes in v2:
time: 155 us; the launch traced here: 154 us
  waiting for transfers between devices  72.1 us (47%)
  starting transfers between devices  30.7 us (20%)
  matrix products  17.3 us (11%)
  local copies, waits for them, and re-layouts  17.2 us (11%)
  between operations  14.3 us (9%)
  other arithmetic  1.96 us (1%)
    unnamed x2, waiting for transfers between devices  61.3 us
    ppermute x2, waiting for transfers between devices, butterfly_sum(): lax.ppermute(block if step == 1 else total, axis, [(i, i ^ step) for i in...  9.97 us
    ppermute x2, starting transfers between devices, extended(): lax.ppermute(lax.slice_in_dim(block, block.shape[dim] - width, None, axis...  9.04 us
    dot_general x4, matrix products, convolve(): jnp.einsum('lc,oc->lo', padded[offset:offset + out_rows], kernel[:, offse...  8.17 us
    ppermute x2, starting transfers between devices, butterfly_sum(): lax.ppermute(block if step == 1 else total, axis, [(i, i ^ step) for i in...  7.49 us
    all_to_all x1, starting transfers between devices, shards(): lax.all_to_all(grouped, 'section', 0, 0, tiled=True)  6.64 us
    reshape x1, local copies, waits for them, and re-layouts, shards(): partial = jnp.stack(taps, axis=1).reshape(n_seq, -1, 128)  6.5 us
    all_to_all x1, starting transfers between devices, shards(): received = lax.all_to_all(groups, 'section', 0, 0, tiled=True)  4.8 us
  transfers between devices with their start and end apart: 9, of which 4 were waited for; matrix products, arithmetic and copies ran while one was open for 12% of the time, Pallas kernels for 0%

profile of v2, /device:TPU:6, one launch (start us, length us, event | category | flops | bytes accessed | tf_op | source)
XLA Modules:
  0.0 153.5 jit_solution(2902892211606074665)
XLA Ops:
  7.2 0.9 slice_bitcast_fusion.1
  8.1 3.8 %collective-permute-start = (bf16[2,1280]{1,0:T(2,128)(2,1)S(1)}, bf16[2,1280]{1,0:T(2,128)(2,1)S(1)}, u32[]{:S(2)}, u32[]{:S(2)}) collective-permute-start(bf16[2,1280]{1,0:T(2,128)(2,1)S(1)} %get-tuple-element.6), channel_id=1, source_target_pairs={{0,8},{8,16},{16,24},{24,32},{32,40},{40,48},{48,56},{56,64},{64,7... | collective-permute-start | bytes 15368 | tf_op jit(solution)/shard_map/ppermute | solution.py:12
  11.9 1.3 collective-permute-start.1
  13.2 1.1 reshape_squeeze.3
  14.3 0.7 copy.16
  15.0 6.6 %all-to-all-start = ((bf16[8,40,192]{2,1,0:T(8,128)(2,1)}), bf16[8,40,192]{2,1,0:T(8,128)(2,1)S(1)}, u32[]{:S(2)}, u32[]{:S(2)}) async-start(bf16[8,40,192]{2,1,0:T(8,128)(2,1)} %bitcast.70), calls=%async_computation | async-start | bytes 327680 | tf_op jit(solution)/shard_map/all_to_all | solution.py:62
  21.6 2.2 %fusion.33 = f32[640,192]{0,1:T(8,128)S(1)} fusion(bf16[192,5,1280]{2,0,1:T(8,128)(2,1)} %param.4, bf16[1,640,1280]{2,1,0:T(8,128)(2,1)} %param.3), kind=kOutput, calls=%fused_computation.49 | convolution fusion | flops 314572800 | bytes 2621440 | tf_op jit(solution)/shard_map/lc,oc->lo/dot_general | solution.py:31
  23.9 2.3 %fusion.18 = f32[640,192]{0,1:T(8,128)S(1)} fusion(bf16[640,1280]{1,0:T(8,128)(2,1)} %bitcast.71, bf16[2,1280]{1,0:T(2,128)(2,1)S(1)} %collective-permute-done, bf16[192,5,1280]{2,0,1:T(8,128)(2,1)S(1)} %copy-done), kind=kOutput, calls=%fused_computation.33 | convolution fusion | flops 317849600 | bytes 2626560 | tf_op jit(solution)/shard_map/lc,oc->lo/dot_general | solution.py:31
  26.2 1.5 fusion.16
  27.7 1.5 fusion.19
  30.6 2.2 %fusion.25 = bf16[640,192]{0,1:T(8,128)(2,1)S(1)} fusion(f32[640,192]{0,1:T(8,128)S(1)} %copy.11, f32[640,192]{0,1:T(8,128)} %fusion.19, f32[640,192]{0,1:T(8,128)} %fusion.16, bf16[192,5,1280]{2,0,1:T(8,128)(2,1)} %param.4, bf16[640,1280]{1,0:T(8,128)(2,1)S(1)} %bitcast.74, bf16[2,1280]{1,0:T(2,128)(2,1)S(1)} %collective-permute-done.1), kind=kOutput, calls=%fused_computation.41 | convolution fusion | flops 319324160 | bytes 3855360 | tf_op jit(solution)/shard_map/lc,oc->lo/dot_general | solution.py:31
  33.4 0.6 fusion.7
  35.8 3.3 %copy.12 = bf16[192,5,1280]{2,1,0:T(8,128)(2,1)} copy(bf16[192,5,1280]{2,0,1:T(8,128)(2,1)S(1)} %fusion.13) | data formatting | bytes 4915200 | tf_op jit(solution)/shard_map/stack | solution.py:80
  39.1 6.5 %reshape.22 = bf16[16,600,128]{2,1,0:T(8,128)(2,1)} reshape(bf16[192,5,1280]{2,1,0:T(8,128)(2,1)} %copy.12) | data formatting | bytes 4915200 | tf_op jit(solution)/shard_map/reshape | solution.py:80
  45.7 1.4 collective-permute-start.4
  47.3 0.6 fusion.31
  47.9 5.2 %collective-permute-start.5 = (bf16[2,192]{0,1:T(8,128)(2,1)S(1)}, bf16[2,192]{0,1:T(8,128)(2,1)S(1)}, u32[]{:S(2)}, u32[]{:S(2)}) collective-permute-start(bf16[2,192]{0,1:T(8,128)(2,1)S(1)} %get-tuple-element.9), channel_id=1, source_target_pairs={{0,8},{8,16},{16,24},{24,32},{32,40},{40,48},{48,56},{56,64},{64,7... | collective-permute-start | bytes 2312 | tf_op jit(solution)/shard_map/ppermute | solution.py:12
  53.2 0.8 fusion.35
  53.9 0.8 collective-permute-done.5
  54.7 0.7 fusion.26
  55.5 0.8 fusion.1
  56.2 1.8 %fusion.3 = bf16[1280,640]{0,1:T(8,128)(2,1)S(1)} fusion(f32[640,1280]{1,0:T(8,128)S(1)} %fusion.26, f32[640,1280]{1,0:T(8,128)S(1)} %fusion.1, bf16[192,5,1280]{2,0,1:T(8,128)(2,1)} %param.4, bf16[2,192]{0,1:T(8,128)(2,1)S(1)} %collective-permute-done.5, bf16[640,192]{0,1:T(8,128)(2,1)S(1)} %fusion.25), kind=kOutput, calls=%fused_computation.5 | convolution fusion | flops 317521920 | bytes 8930048 | tf_op jit(solution)/shard_map/lo,oc->cl/dot_general | solution.py:88
  58.1 2.2 %copy.13 = bf16[1280,640]{1,0:T(8,128)(2,1)} copy(bf16[1280,640]{0,1:T(8,128)(2,1)S(1)} %fusion.3) | data formatting | bytes 3276800 | tf_op jit(solution)/shard_map/add | solution.py:88
  60.3 4.8 %all-to-all-start.1 = ((bf16[8,160,640]{2,1,0:T(8,128)(2,1)}), bf16[8,160,640]{2,1,0:T(8,128)(2,1)S(1)}, u32[]{:S(2)}, u32[]{:S(2)}) async-start(bf16[8,160,640]{2,1,0:T(8,128)(2,1)} %bitcast.16), calls=%async_computation.1 | async-start | bytes 3276800 | tf_op jit(solution)/shard_map/all_to_all | solution.py:95
  65.0 61.3 %reduce-scatter.4.cloned.1.call-done = bf16[1,600,128]{2,1,0:T(8,128)(2,1)} async-done(((bf16[16,600,128]{2,1,0:T(8,128)(2,1)}), bf16[1,600,128]{2,1,0:T(8,128)(2,1)}) %reduce-scatter.4.cloned.1.call-update) | async-done | bytes 153616
  126.3 3.5 %collective-permute-start.2 = (bf16[1,600,128]{2,1,0:T(8,128)(2,1)}, bf16[1,600,128]{2,1,0:T(8,128)(2,1)S(1)}, u32[]{:S(2)}, u32[]{:S(2)}) collective-permute-start(bf16[1,600,128]{2,1,0:T(8,128)(2,1)} %reduce-scatter.4.cloned.1.call-done), channel_id=1, source_target_pairs={{0,128},{128,0},{256,384},{384,256},{1,129},{129,1},{257,385},{385... | collective-permute-start | bytes 460808 | tf_op jit(solution)/shard_map/ppermute | solution.py:47
  129.8 4.7 %collective-permute-done.2 = bf16[1,600,128]{2,1,0:T(8,128)(2,1)S(1)} collective-permute-done((bf16[1,600,128]{2,1,0:T(8,128)(2,1)}, bf16[1,600,128]{2,1,0:T(8,128)(2,1)S(1)}, u32[]{:S(2)}, u32[]{:S(2)}) %collective-permute-start.2) | collective-permute-done | bytes 153632 | tf_op jit(solution)/shard_map/ppermute | solution.py:47
  134.5 0.9 convert_add_fusion
  135.5 4.0 %collective-permute-start.3 = (f32[1,600,128]{2,1,0:T(8,128)S(1)}, f32[1,600,128]{2,1,0:T(8,128)S(1)}, u32[]{:S(2)}, u32[]{:S(2)}) collective-permute-start(f32[1,600,128]{2,1,0:T(8,128)S(1)} %convert_add_fusion), channel_id=1, source_target_pairs={{0,256},{128,384},{256,0},{384,128},{1,257},{129,385},{257,1},{385... | collective-permute-start | bytes 921608 | tf_op jit(solution)/shard_map/ppermute | solution.py:47
  139.5 0.9 reduce_sum.12
  140.5 5.3 %collective-permute-done.3 = f32[1,600,128]{2,1,0:T(8,128)S(1)} collective-permute-done((f32[1,600,128]{2,1,0:T(8,128)S(1)}, f32[1,600,128]{2,1,0:T(8,128)S(1)}, u32[]{:S(2)}, u32[]{:S(2)}) %collective-permute-start.3) | collective-permute-done | bytes 307232 | tf_op jit(solution)/shard_map/ppermute | solution.py:47
  145.8 0.9 copy.14
  (28 shorter events, 4.1 us)
Async XLA Ops:
  7.2 16.7 %copy-start = (bf16[192,5,1280]{2,0,1:T(8,128)(2,1)S(1)}, bf16[192,5,1280]{2,0,1:T(8,128)(2,1)}, u32[]{:S(2)}) copy-start(bf16[192,5,1280]{2,0,1:T(8,128)(2,1)} %param.4) | copy-start | bytes 7372804
  8.1 15.8 %collective-permute-start = (bf16[2,1280]{1,0:T(2,128)(2,1)S(1)}, bf16[2,1280]{1,0:T(2,128)(2,1)S(1)}, u32[]{:S(2)}, u32[]{:S(2)}) collective-permute-start(bf16[2,1280]{1,0:T(2,128)(2,1)S(1)} %get-tuple-element.6), channel_id=1, source_target_pairs={{0,8},{8,16},{16,24},{24,32},{32,40},{40,48},{48,56},{56,64},{64,7... | collective-permute-start | bytes 15368 | tf_op jit(solution)/shard_map/ppermute | solution.py:12
  11.9 15.7 %collective-permute-start.1 = (bf16[2,1280]{1,0:T(2,128)(2,1)S(1)}, bf16[2,1280]{1,0:T(2,128)(2,1)S(1)}, u32[]{:S(2)}, u32[]{:S(2)}) collective-permute-start(bf16[2,1280]{1,0:T(2,128)(2,1)S(1)} %get-tuple-element.7), channel_id=1, source_target_pairs={{8,0},{16,8},{24,16},{32,24},{40,32},{48,40},{56,48},{64,56},{72,6... | collective-permute-start | bytes 15368 | tf_op jit(solution)/shard_map/ppermute | solution.py:15
  15.0 14.2 %all-to-all-start = ((bf16[8,40,192]{2,1,0:T(8,128)(2,1)}), bf16[8,40,192]{2,1,0:T(8,128)(2,1)S(1)}, u32[]{:S(2)}, u32[]{:S(2)}) async-start(bf16[8,40,192]{2,1,0:T(8,128)(2,1)} %bitcast.70), calls=%async_computation | async-start | bytes 327680 | tf_op jit(solution)/shard_map/all_to_all | solution.py:62
  21.6 104.7 %reduce-scatter.4.cloned.1.call-start = ((), (), s32[]{:S(2)}) async-start(), calls=%async_computation.3 | async-start | bytes 2611200
  23.9 2.3 %copy-start.2 = (bf16[1,640,1280]{2,1,0:T(8,128)(2,1)S(1)}, bf16[1,640,1280]{2,1,0:T(8,128)(2,1)}, u32[]{:S(2)}) copy-start(bf16[1,640,1280]{2,1,0:T(8,128)(2,1)} %param.3) | copy-start | bytes 4915204
  29.2 1.4 copy-start.3
  45.6 1.7 %copy-start.1 = (bf16[192,5,1280]{2,0,1:T(8,128)(2,1)S(1)}, bf16[192,5,1280]{2,0,1:T(8,128)(2,1)}, u32[]{:S(2)}) copy-start(bf16[192,5,1280]{2,0,1:T(8,128)(2,1)} %param.4) | copy-start | bytes 7372804
  45.7 7.4 %collective-permute-start.4 = (bf16[2,192]{0,1:T(8,128)(2,1)S(1)}, bf16[2,192]{0,1:T(8,128)(2,1)S(1)}, u32[]{:S(2)}, u32[]{:S(2)}) collective-permute-start(bf16[2,192]{0,1:T(8,128)(2,1)S(1)} %get-tuple-element.8), channel_id=1, source_target_pairs={{8,0},{16,8},{24,16},{32,24},{40,32},{48,40},{56,48},{64,56},{72,6... | collective-permute-start | bytes 2312 | tf_op jit(solution)/shard_map/ppermute | solution.py:15
  47.9 6.8 %collective-permute-start.5 = (bf16[2,192]{0,1:T(8,128)(2,1)S(1)}, bf16[2,192]{0,1:T(8,128)(2,1)S(1)}, u32[]{:S(2)}, u32[]{:S(2)}) collective-permute-start(bf16[2,192]{0,1:T(8,128)(2,1)S(1)} %get-tuple-element.9), channel_id=1, source_target_pairs={{0,8},{8,16},{16,24},{24,32},{32,40},{40,48},{48,56},{56,64},{64,7... | collective-permute-start | bytes 2312 | tf_op jit(solution)/shard_map/ppermute | solution.py:12
  60.3 79.3 %all-to-all-start.1 = ((bf16[8,160,640]{2,1,0:T(8,128)(2,1)}), bf16[8,160,640]{2,1,0:T(8,128)(2,1)S(1)}, u32[]{:S(2)}, u32[]{:S(2)}) async-start(bf16[8,160,640]{2,1,0:T(8,128)(2,1)} %bitcast.16), calls=%async_computation.1 | async-start | bytes 3276800 | tf_op jit(solution)/shard_map/all_to_all | solution.py:95
  126.3 19.4 %copy-start.4 = (bf16[1,600,128]{2,1,0:T(8,128)(2,1)S(1)}, bf16[1,600,128]{2,1,0:T(8,128)(2,1)}, u32[]{:S(2)}) copy-start(bf16[1,600,128]{2,1,0:T(8,128)(2,1)} %reduce-scatter.4.cloned.1.call-done) | copy-start | bytes 460804
  126.3 8.2 %collective-permute-start.2 = (bf16[1,600,128]{2,1,0:T(8,128)(2,1)}, bf16[1,600,128]{2,1,0:T(8,128)(2,1)S(1)}, u32[]{:S(2)}, u32[]{:S(2)}) collective-permute-start(bf16[1,600,128]{2,1,0:T(8,128)(2,1)} %reduce-scatter.4.cloned.1.call-done), channel_id=1, source_target_pairs={{0,128},{128,0},{256,384},{384,256},{1,129},{129,1},{257,385},{385... | collective-permute-start | bytes 460808 | tf_op jit(solution)/shard_map/ppermute | solution.py:47
  135.5 10.3 %collective-permute-start.3 = (f32[1,600,128]{2,1,0:T(8,128)S(1)}, f32[1,600,128]{2,1,0:T(8,128)S(1)}, u32[]{:S(2)}, u32[]{:S(2)}) collective-permute-start(f32[1,600,128]{2,1,0:T(8,128)S(1)} %convert_add_fusion), channel_id=1, source_target_pairs={{0,256},{128,384},{256,0},{384,128},{1,257},{129,385},{257,1},{385... | collective-permute-start | bytes 921608 | tf_op jit(solution)/shard_map/ppermute | solution.py:47
Sparse Core Ops, SparseCore 0:
  45.7 80.5 reduce-scatter.3

commit v3 on v2

--- a/solution.py
+++ b/solution.py
@@ -79,7 +79,7 @@
     n_seq = lax.axis_size("seq")
     partial = jnp.stack(taps, axis=1).reshape(n_seq, -1, 128)
     weight_part = lax.psum_scatter(partial, "seq", scatter_dimension=0, tiled=True)
-    weight_rows = butterfly_sum(weight_part, "dp")
+    weight_rows = jnp.sum(lax.all_gather(weight_part, "dp", axis=0, tiled=False).astype(jnp.float32), axis=0)
     weight_grad = weight_rows.reshape(-1, taps_count, in_ch)
     summed = jnp.einsum(
         "lo,oc->cl", grad_ext[4 : 4 + length], kernel[:, 0, :], preferred_element_type=jnp.float32

time: 155 us -> 148 us (0.955)
  blocking collectives: 0 us -> 38.5 us
  waiting for transfers between devices: 72.1 us -> 41.7 us
  starting transfers between devices: 30.7 us -> 18.4 us
    all_to_all x0 -> x1, blocking collectives: none -> 25 us  [shards(): received = lax.all_to_all(groups, 'section', 0, 0, tiled=True)]
    unnamed x2, waiting for transfers between devices: 61.3 us -> 40.9 us
    all_gather x0 -> x1, blocking collectives: none -> 13.5 us  [shards(): lax.all_gather(weight_part, 'dp', axis=0, tiled=False).astype(jnp.float32)]
    ppermute x2 -> x0, waiting for transfers between devices: 9.97 us -> none  [butterfly_sum(): lax.ppermute(block if step == 1 else total, axis, [(i, i ^ step) for i in...]
    ppermute x2 -> x0, starting transfers between devices: 7.49 us -> none  [butterfly_sum(): lax.ppermute(block if step == 1 else total, axis, [(i, i ^ step) for i in...]
    all_to_all x1 -> x0, starting transfers between devices: 4.8 us -> none  [shards(): received = lax.all_to_all(groups, 'section', 0, 0, tiled=True)]
  transfers between devices with their start and end apart: 9 -> 6, of which waited for: 4 -> 2; matrix products, arithmetic and copies ran while one was open for 12% -> 11% of each run, Pallas kernels for 0% -> 0%
where the time goes in v3:
time: 148 us
  waiting for transfers between devices  41.7 us (28%)
  blocking collectives  38.5 us (26%)
  starting transfers between devices  18.4 us (12%)
  matrix products  17.3 us (12%)
  local copies, waits for them, and re-layouts  16.3 us (11%)
  between operations  14.2 us (10%)
    unnamed x2, waiting for transfers between devices  40.9 us
    all_to_all x1, blocking collectives, shards(): received = lax.all_to_all(groups, 'section', 0, 0, tiled=True)  25 us
    all_gather x1, blocking collectives, shards(): lax.all_gather(weight_part, 'dp', axis=0, tiled=False).astype(jnp.float32)  13.5 us
    ppermute x2, starting transfers between devices, extended(): lax.ppermute(lax.slice_in_dim(block, block.shape[dim] - width, None, axis...  9.04 us
    dot_general x4, matrix products, convolve(): jnp.einsum('lc,oc->lo', padded[offset:offset + out_rows], kernel[:, offse...  8.16 us
    all_to_all x1, starting transfers between devices, shards(): lax.all_to_all(grouped, 'section', 0, 0, tiled=True)  6.64 us
    reshape x1, local copies, waits for them, and re-layouts, shards(): partial = jnp.stack(taps, axis=1).reshape(n_seq, -1, 128)  6.47 us
    dot_general x4, matrix products, shards(): jnp.einsum('lo,oc->cl', grad_ext[4 - offset:4 - offset + length], kernel[...  3.95 us
  transfers between devices with their start and end apart: 6, of which 2 were waited for; matrix products, arithmetic and copies ran while one was open for 11% of the time, Pallas kernels for 0%

profile of v3, /device:TPU:6, one launch (start us, length us, event | category | flops | bytes accessed | tf_op | source)
XLA Modules:
  0.0 147.5 jit_solution(16046514797513972056)
XLA Ops:
  7.2 0.9 slice_bitcast_fusion.1
  8.1 3.8 %collective-permute-start = (bf16[2,1280]{1,0:T(2,128)(2,1)S(1)}, bf16[2,1280]{1,0:T(2,128)(2,1)S(1)}, u32[]{:S(2)}, u32[]{:S(2)}) collective-permute-start(bf16[2,1280]{1,0:T(2,128)(2,1)S(1)} %get-tuple-element.6), channel_id=1, source_target_pairs={{0,8},{8,16},{16,24},{24,32},{32,40},{40,48},{48,56},{56,64},{64,7... | collective-permute-start | bytes 15368 | tf_op jit(solution)/shard_map/ppermute | solution.py:12
  11.9 1.3 collective-permute-start.1
  13.2 1.1 reshape_squeeze.3
  14.3 0.7 copy.16
  15.0 6.6 %all-to-all-start = ((bf16[8,40,192]{2,1,0:T(8,128)(2,1)}), bf16[8,40,192]{2,1,0:T(8,128)(2,1)S(1)}, u32[]{:S(2)}, u32[]{:S(2)}) async-start(bf16[8,40,192]{2,1,0:T(8,128)(2,1)} %bitcast.70), calls=%async_computation | async-start | bytes 327680 | tf_op jit(solution)/shard_map/all_to_all | solution.py:62
  21.6 2.2 %fusion.33 = f32[640,192]{0,1:T(8,128)S(1)} fusion(bf16[192,5,1280]{2,0,1:T(8,128)(2,1)} %param.4, bf16[1,640,1280]{2,1,0:T(8,128)(2,1)} %param.3), kind=kOutput, calls=%fused_computation.50 | convolution fusion | flops 314572800 | bytes 2621440 | tf_op jit(solution)/shard_map/lc,oc->lo/dot_general | solution.py:31
  23.9 2.3 %fusion.18 = f32[640,192]{0,1:T(8,128)S(1)} fusion(bf16[640,1280]{1,0:T(8,128)(2,1)} %bitcast.72, bf16[2,1280]{1,0:T(2,128)(2,1)S(1)} %collective-permute-done, bf16[192,5,1280]{2,0,1:T(8,128)(2,1)S(1)} %copy-done), kind=kOutput, calls=%fused_computation.34 | convolution fusion | flops 317849600 | bytes 2626560 | tf_op jit(solution)/shard_map/lc,oc->lo/dot_general | solution.py:31
  26.2 1.5 %fusion.16 = f32[640,192]{0,1:T(8,128)} fusion(f32[640,192]{0,1:T(8,128)S(1)} %fusion.33, f32[640,192]{0,1:T(8,128)S(1)} %fusion.18, bf16[192,5,1280]{2,0,1:T(8,128)(2,1)S(1)} %copy-done, bf16[2,1280]{1,0:T(2,128)(2,1)S(1)} %collective-permute-done, bf16[640,1280]{1,0:T(8,128)(2,1)S(1)} %bitcast.73), kind=kOutput, calls=%fused_computation.32 | convolution fusion | flops 318095360 | bytes 3609600 | tf_op jit(solution)/shard_map/lc,oc->lo/dot_general | solution.py:27
  27.7 1.5 %fusion.19 = f32[640,192]{0,1:T(8,128)} fusion(bf16[2,1280]{1,0:T(2,128)(2,1)S(1)} %collective-permute-done.1, bf16[640,1280]{1,0:T(8,128)(2,1)S(1)} %bitcast.74, bf16[192,5,1280]{2,0,1:T(8,128)(2,1)S(1)} %copy-done), kind=kOutput, calls=%fused_computation.35 | convolution fusion | flops 317849600 | bytes 2626560 | tf_op jit(solution)/shard_map/lc,oc->lo/dot_general | solution.py:31
  30.6 2.2 %fusion.25 = bf16[640,192]{0,1:T(8,128)(2,1)S(1)} fusion(f32[640,192]{0,1:T(8,128)S(1)} %copy.11, f32[640,192]{0,1:T(8,128)} %fusion.19, f32[640,192]{0,1:T(8,128)} %fusion.16, bf16[192,5,1280]{2,0,1:T(8,128)(2,1)} %param.4, bf16[640,1280]{1,0:T(8,128)(2,1)S(1)} %bitcast.75, bf16[2,1280]{1,0:T(2,128)(2,1)S(1)} %collective-permute-done.1), kind=kOutput, calls=%fused_computation.42 | convolution fusion | flops 319324160 | bytes 3855360 | tf_op jit(solution)/shard_map/lc,oc->lo/dot_general | solution.py:31
  32.8 0.6 fusion.5
  33.4 0.6 fusion.7
  34.0 0.6 fusion.9
  34.6 0.6 fusion.11
  35.2 0.6 fusion.13
  35.8 3.3 %copy.12 = bf16[192,5,1280]{2,1,0:T(8,128)(2,1)} copy(bf16[192,5,1280]{2,0,1:T(8,128)(2,1)S(1)} %fusion.13) | data formatting | bytes 4915200 | tf_op jit(solution)/shard_map/stack | solution.py:80
  39.1 6.5 %reshape.24 = bf16[16,600,128]{2,1,0:T(8,128)(2,1)} reshape(bf16[192,5,1280]{2,1,0:T(8,128)(2,1)} %copy.12) | data formatting | bytes 4915200 | tf_op jit(solution)/shard_map/reshape | solution.py:80
  45.7 1.4 collective-permute-start.2
  47.3 0.6 fusion.31
  47.9 5.2 %collective-permute-start.3 = (bf16[2,192]{0,1:T(8,128)(2,1)S(1)}, bf16[2,192]{0,1:T(8,128)(2,1)S(1)}, u32[]{:S(2)}, u32[]{:S(2)}) collective-permute-start(bf16[2,192]{0,1:T(8,128)(2,1)S(1)} %get-tuple-element.9), channel_id=1, source_target_pairs={{0,8},{8,16},{16,24},{24,32},{32,40},{40,48},{48,56},{56,64},{64,7... | collective-permute-start | bytes 2312 | tf_op jit(solution)/shard_map/ppermute | solution.py:12
  53.2 0.8 fusion.35
  53.9 0.8 collective-permute-done.3
  54.7 0.7 fusion.26
  55.5 0.8 fusion.1
  56.2 1.8 %fusion.3 = bf16[1280,640]{0,1:T(8,128)(2,1)S(1)} fusion(f32[640,1280]{1,0:T(8,128)S(1)} %fusion.26, f32[640,1280]{1,0:T(8,128)S(1)} %fusion.1, bf16[192,5,1280]{2,0,1:T(8,128)(2,1)} %param.4, bf16[2,192]{0,1:T(8,128)(2,1)S(1)} %collective-permute-done.3, bf16[640,192]{0,1:T(8,128)(2,1)S(1)} %fusion.25), kind=kOutput, calls=%fused_computation.5 | convolution fusion | flops 317521920 | bytes 8930048 | tf_op jit(solution)/shard_map/lo,oc->cl/dot_general | solution.py:88
  58.1 1.3 copy.13
  59.4 25.0 %all_to_all.10 = bf16[8,160,640]{2,1,0:T(8,128)(2,1)S(1)} all-to-all(bf16[8,160,640]{2,1,0:T(8,128)(2,1)S(1)} %bitcast.71), channel_id=1, replica_groups=mesh['dp'=4,'seq'=16,'section'=8] {'section'}, dimensions={0} | all-to-all | bytes 3276800 | tf_op jit(solution)/shard_map/all_to_all | solution.py:95
  84.4 0.9 reduce_sum.22
  85.3 40.8 %reduce-scatter.4.cloned.1.call-done = bf16[1,600,128]{2,1,0:T(8,128)(2,1)} async-done(((bf16[16,600,128]{2,1,0:T(8,128)(2,1)}), bf16[1,600,128]{2,1,0:T(8,128)(2,1)}) %reduce-scatter.4.cloned.1.call-update) | async-done | bytes 153616
  126.2 13.5 %all-gather = bf16[4,600,128]{2,1,0:T(8,128)(2,1)S(1)} all-gather(bf16[1,600,128]{2,1,0:T(8,128)(2,1)} %reduce-scatter.4.cloned.1.call-done), channel_id=2, replica_groups=mesh['dp'=4,'seq'=16,'section'=8] {'dp'}, dimensions={0}, use_global_device_ids=true | all-gather | bytes 768000 | tf_op jit(solution)/shard_map/all_gather | solution.py:82
  139.8 0.9 copy.14
  (21 shorter events, 1.8 us)
Async XLA Ops:
  7.2 16.7 %copy-start = (bf16[192,5,1280]{2,0,1:T(8,128)(2,1)S(1)}, bf16[192,5,1280]{2,0,1:T(8,128)(2,1)}, u32[]{:S(2)}) copy-start(bf16[192,5,1280]{2,0,1:T(8,128)(2,1)} %param.4) | copy-start | bytes 7372804
  8.1 15.8 %collective-permute-start = (bf16[2,1280]{1,0:T(2,128)(2,1)S(1)}, bf16[2,1280]{1,0:T(2,128)(2,1)S(1)}, u32[]{:S(2)}, u32[]{:S(2)}) collective-permute-start(bf16[2,1280]{1,0:T(2,128)(2,1)S(1)} %get-tuple-element.6), channel_id=1, source_target_pairs={{0,8},{8,16},{16,24},{24,32},{32,40},{40,48},{48,56},{56,64},{64,7... | collective-permute-start | bytes 15368 | tf_op jit(solution)/shard_map/ppermute | solution.py:12
  11.9 15.8 %collective-permute-start.1 = (bf16[2,1280]{1,0:T(2,128)(2,1)S(1)}, bf16[2,1280]{1,0:T(2,128)(2,1)S(1)}, u32[]{:S(2)}, u32[]{:S(2)}) collective-permute-start(bf16[2,1280]{1,0:T(2,128)(2,1)S(1)} %get-tuple-element.7), channel_id=1, source_target_pairs={{8,0},{16,8},{24,16},{32,24},{40,32},{48,40},{56,48},{64,56},{72,6... | collective-permute-start | bytes 15368 | tf_op jit(solution)/shard_map/ppermute | solution.py:15
  15.0 14.2 %all-to-all-start = ((bf16[8,40,192]{2,1,0:T(8,128)(2,1)}), bf16[8,40,192]{2,1,0:T(8,128)(2,1)S(1)}, u32[]{:S(2)}, u32[]{:S(2)}) async-start(bf16[8,40,192]{2,1,0:T(8,128)(2,1)} %bitcast.70), calls=%async_computation | async-start | bytes 327680 | tf_op jit(solution)/shard_map/all_to_all | solution.py:62
  21.6 104.6 %reduce-scatter.4.cloned.1.call-start = ((), (), s32[]{:S(2)}) async-start(), calls=%async_computation.3 | async-start | bytes 2611200
  23.9 2.3 %copy-start.2 = (bf16[1,640,1280]{2,1,0:T(8,128)(2,1)S(1)}, bf16[1,640,1280]{2,1,0:T(8,128)(2,1)}, u32[]{:S(2)}) copy-start(bf16[1,640,1280]{2,1,0:T(8,128)(2,1)} %param.3) | copy-start | bytes 4915204
  29.2 1.4 copy-start.3
  45.6 1.7 %copy-start.1 = (bf16[192,5,1280]{2,0,1:T(8,128)(2,1)S(1)}, bf16[192,5,1280]{2,0,1:T(8,128)(2,1)}, u32[]{:S(2)}) copy-start(bf16[192,5,1280]{2,0,1:T(8,128)(2,1)} %param.4) | copy-start | bytes 7372804
  45.7 7.4 %collective-permute-start.2 = (bf16[2,192]{0,1:T(8,128)(2,1)S(1)}, bf16[2,192]{0,1:T(8,128)(2,1)S(1)}, u32[]{:S(2)}, u32[]{:S(2)}) collective-permute-start(bf16[2,192]{0,1:T(8,128)(2,1)S(1)} %get-tuple-element.8), channel_id=1, source_target_pairs={{8,0},{16,8},{24,16},{32,24},{40,32},{48,40},{56,48},{64,56},{72,6... | collective-permute-start | bytes 2312 | tf_op jit(solution)/shard_map/ppermute | solution.py:15
  47.9 6.8 %collective-permute-start.3 = (bf16[2,192]{0,1:T(8,128)(2,1)S(1)}, bf16[2,192]{0,1:T(8,128)(2,1)S(1)}, u32[]{:S(2)}, u32[]{:S(2)}) collective-permute-start(bf16[2,192]{0,1:T(8,128)(2,1)S(1)} %get-tuple-element.9), channel_id=1, source_target_pairs={{0,8},{8,16},{16,24},{24,32},{32,40},{40,48},{48,56},{56,64},{64,7... | collective-permute-start | bytes 2312 | tf_op jit(solution)/shard_map/ppermute | solution.py:12
Sparse Core Ops, SparseCore 0:
  45.7 80.4 reduce-scatter.3

commit v4 on v3

--- a/solution.py
+++ b/solution.py
@@ -50,6 +50,19 @@
     return total
 
 
+def symmetric_sum(block, axis):
+    count = lax.axis_size(axis)
+    if count & (count - 1):
+        return lax.psum(block.astype(jnp.float32), axis)
+    parts = [block] + [
+        lax.ppermute(block, axis, [(i, i ^ step) for i in range(count)]) for step in range(1, count)
+    ]
+    parts = [part.astype(jnp.float32) for part in parts]
+    while len(parts) > 1:
+        parts = [parts[i] + parts[i + 1] for i in range(0, len(parts), 2)]
+    return parts[0]
+
+
 def shards(signal, kernel, trunk_grad):
     local_signal = signal[0]
     length = local_signal.shape[0]
@@ -66,21 +79,21 @@
     grad_pre = (grad_hidden * gelu_slope(linear)).astype(jnp.bfloat16)
     grad_ext = extended(grad_pre, (("seq", 0),), 2)
     grad_middle = grad_ext[2 : 2 + length]
-    taps = []
-    for offset in range(taps_count):
-        taps.append(
-            jnp.einsum(
-                "lo,lc->oc",
-                grad_middle,
-                padded[offset : offset + length],
-                preferred_element_type=jnp.float32,
-            ).astype(jnp.bfloat16)
-        )
     n_seq = lax.axis_size("seq")
-    partial = jnp.stack(taps, axis=1).reshape(n_seq, -1, 128)
-    weight_part = lax.psum_scatter(partial, "seq", scatter_dimension=0, tiled=True)
-    weight_rows = jnp.sum(lax.all_gather(weight_part, "dp", axis=0, tiled=False).astype(jnp.float32), axis=0)
-    weight_grad = weight_rows.reshape(-1, taps_count, in_ch)
+    chunk = out_ch // n_seq * taps_count
+    chunk_rows = -(-chunk // 16) * 16
+    shifted = jnp.stack(
+        [jnp.pad(grad_middle.T, ((0, 0), (k, taps_count - 1 - k))) for k in range(taps_count)],
+        axis=1,
+    ).reshape(n_seq, chunk, length + taps_count - 1)
+    banded = jnp.pad(shifted, ((0, 0), (0, chunk_rows - chunk), (0, 0))).reshape(
+        n_seq * chunk_rows, length + taps_count - 1
+    )
+    partial = jnp.dot(banded, padded, preferred_element_type=jnp.float32).astype(jnp.bfloat16)
+    weight_part = lax.psum_scatter(
+        partial.reshape(n_seq, chunk_rows, in_ch), "seq", scatter_dimension=0, tiled=True
+    )[0, :chunk]
+    weight_grad = symmetric_sum(weight_part, "dp").reshape(-1, taps_count, in_ch)
     summed = jnp.einsum(
         "lo,oc->cl", grad_ext[4 : 4 + length], kernel[:, 0, :], preferred_element_type=jnp.float32
     )

time: 148 us -> 148 us (level)
  blocking collectives: 38.5 us -> 0 us
  waiting for transfers between devices: 41.7 us -> 61.9 us
  starting transfers between devices: 18.4 us -> 36.4 us
  matrix products: 17.3 us -> 20.1 us
  local copies, waits for them, and re-layouts: 16.3 us -> 13.6 us
    reduce_scatter x0 -> x1, waiting for transfers between devices: none -> 56.1 us  [shards(): lax.psum_scatter(partial.reshape(n_seq, chunk_rows, in_ch), 'seq', scatte...]
    unnamed x2 -> x1, waiting for transfers between devices: 40.9 us -> 0.02 us
    all_to_all x1 -> x0, blocking collectives: 25 us -> none  [shards(): received = lax.all_to_all(groups, 'section', 0, 0, tiled=True)]
    all_gather x1 -> x0, blocking collectives: 13.5 us -> none  [shards(): lax.all_gather(weight_part, 'dp', axis=0, tiled=False).astype(jnp.float32)]
    ppermute x0 -> x3, starting transfers between devices: none -> 10.4 us  [symmetric_sum(): lax.ppermute(block, axis, [(i, i ^ step) for i in range(count)])]
    ppermute x0 -> x3, waiting for transfers between devices: none -> 5.06 us  [symmetric_sum(): lax.ppermute(block, axis, [(i, i ^ step) for i in range(count)])]
    all_to_all x0 -> x1, starting transfers between devices: none -> 4.79 us  [shards(): received = lax.all_to_all(groups, 'section', 0, 0, tiled=True)]
    reshape x2, local copies, waits for them, and re-layouts: 6.53 us -> 2.01 us  [the longest x1 1.96 us: shards(): shifted = jnp.stack([jnp.pad(grad_middle.T, ((0, 0), (k, taps_count - 1 -...]
  transfers between devices with their start and end apart: 6 -> 10, of which waited for: 2 -> 4; matrix products, arithmetic and copies ran while one was open for 11% -> 13% of each run, Pallas kernels for 0% -> 0%
where the time goes in v4:
time: 148 us; the launch traced here: 147 us
  waiting for transfers between devices  61.9 us (42%)
  starting transfers between devices  36.4 us (25%)
  matrix products  20.1 us (14%)
  between operations  14.3 us (10%)
  local copies, waits for them, and re-layouts  13.6 us (9%)
    reduce_scatter x1, waiting for transfers between devices, shards(): lax.psum_scatter(partial.reshape(n_seq, chunk_rows, in_ch), 'seq', scatte...  56.1 us
    ppermute x3, starting transfers between devices, symmetric_sum(): lax.ppermute(block, axis, [(i, i ^ step) for i in range(count)])  10.4 us
    all_to_all x1, starting transfers between devices, shards(): lax.all_to_all(grouped, 'section', 0, 0, tiled=True)  9.3 us
    ppermute x2, starting transfers between devices, extended(): lax.ppermute(lax.slice_in_dim(block, block.shape[dim] - width, None, axis...  9.14 us
    dot_general x4, matrix products, convolve(): jnp.einsum('lc,oc->lo', padded[offset:offset + out_rows], kernel[:, offse...  9.07 us
    ppermute x3, waiting for transfers between devices, symmetric_sum(): lax.ppermute(block, axis, [(i, i ^ step) for i in range(count)])  5.06 us
    all_to_all x1, starting transfers between devices, shards(): received = lax.all_to_all(groups, 'section', 0, 0, tiled=True)  4.79 us
    dot_general x4, matrix products, shards(): jnp.einsum('lo,oc->cl', grad_ext[4 - offset:4 - offset + length], kernel[...  3.95 us
  transfers between devices with their start and end apart: 10, of which 4 were waited for; matrix products, arithmetic and copies ran while one was open for 13% of the time, Pallas kernels for 0%

profile of v4, /device:TPU:6, one launch (start us, length us, event | category | flops | bytes accessed | tf_op | source)
XLA Modules:
  0.0 147.3 jit_solution(13428328092210946671)
XLA Ops:
  7.2 0.8 slice_bitcast_fusion.2
  7.9 1.3 collective-permute-start.1
  9.2 4.5 %collective-permute-start = (bf16[2,1280]{1,0:T(2,128)(2,1)S(1)}, bf16[2,1280]{1,0:T(2,128)(2,1)S(1)}, u32[]{:S(2)}, u32[]{:S(2)}) collective-permute-start(bf16[2,1280]{1,0:T(2,128)(2,1)S(1)} %get-tuple-element.4), channel_id=1, source_target_pairs={{0,8},{8,16},{16,24},{24,32},{32,40},{40,48},{48,56},{56,64},{64,7... | collective-permute-start | bytes 15368 | tf_op jit(solution)/shard_map/ppermute | solution.py:12
  13.8 1.1 reshape_squeeze.3
  14.9 0.7 copy.11
  15.6 9.3 %all-to-all-start = ((bf16[8,40,192]{2,1,0:T(8,128)(2,1)}), bf16[8,40,192]{2,1,0:T(8,128)(2,1)S(1)}, u32[]{:S(2)}, u32[]{:S(2)}) async-start(bf16[8,40,192]{2,1,0:T(8,128)(2,1)} %bitcast.60), calls=%async_computation | async-start | bytes 327680 | tf_op jit(solution)/shard_map/all_to_all | solution.py:75
  24.9 3.0 %fusion.44 = f32[640,192]{0,1:T(8,128)} fusion(bf16[192,5,1280]{2,0,1:T(8,128)(2,1)} %param.4, bf16[1,640,1280]{2,1,0:T(8,128)(2,1)} %param.3), kind=kOutput, calls=%fused_computation.44 | convolution fusion | flops 314572800 | bytes 2621440 | tf_op jit(solution)/shard_map/lc,oc->lo/dot_general | solution.py:31
  27.9 3.0 %fusion.10 = f32[640,192]{0,1:T(8,128)} fusion(bf16[640,1280]{1,0:T(8,128)(2,1)} %bitcast.70, bf16[2,1280]{1,0:T(2,128)(2,1)S(1)} %collective-permute-done.1, bf16[192,5,1280]{2,0,1:T(8,128)(2,1)S(1)} %copy-done), kind=kOutput, calls=%fused_computation.17 | convolution fusion | flops 317849600 | bytes 2626560 | tf_op jit(solution)/shard_map/lc,oc->lo/dot_general | solution.py:31
  31.0 1.5 %fusion.15 = f32[640,192]{0,1:T(8,128)} fusion(bf16[2,1280]{1,0:T(2,128)(2,1)S(1)} %collective-permute-done.1, bf16[640,1280]{1,0:T(8,128)(2,1)S(1)} %bitcast.71, bf16[192,5,1280]{2,0,1:T(8,128)(2,1)S(1)} %copy-done), kind=kOutput, calls=%fused_computation.21 | convolution fusion | flops 317849600 | bytes 2626560 | tf_op jit(solution)/shard_map/lc,oc->lo/dot_general | solution.py:31
  32.5 1.5 %fusion.17 = f32[640,192]{0,1:T(8,128)} fusion(bf16[640,1280]{1,0:T(8,128)(2,1)S(1)} %bitcast.72, bf16[2,1280]{1,0:T(2,128)(2,1)S(1)} %collective-permute-done, bf16[192,5,1280]{2,0,1:T(8,128)(2,1)S(1)} %copy-done), kind=kOutput, calls=%fused_computation.24 | convolution fusion | flops 317849600 | bytes 2626560 | tf_op jit(solution)/shard_map/lc,oc->lo/dot_general | solution.py:31
  35.4 2.5 %fusion.36 = bf16[640,192]{0,1:T(8,128)(2,1)S(1)} fusion(f32[640,192]{0,1:T(8,128)S(1)} %copy.6, f32[640,192]{0,1:T(8,128)} %fusion.15, f32[640,192]{0,1:T(8,128)} %fusion.10, f32[640,192]{0,1:T(8,128)} %fusion.44, f32[640,192]{0,1:T(8,128)} %fusion.17, bf16[2,1280]{1,0:T(2,128)(2,1)S(1)} %collective-permute-done, bf16[640,1280]{1,0:T(8,128)(2,1)S(1)} %bitcast.73, ...), kind=kOutput, calls=%fused_computation.36 | convolution fusion | flops 319569920 | bytes 4838400 | tf_op jit(solution)/shard_map/lc,oc->lo/dot_general | solution.py:27
  38.6 0.9 copy.7
  39.5 2.0 %reshape.28 = bf16[16,60,644]{2,1,0:T(8,128)(2,1)} reshape(bf16[192,5,644]{2,1,0:T(8,128)(2,1)S(1)} %copy.7) | data formatting | bytes 2472960 | tf_op jit(solution)/shard_map/reshape | solution.py:88
  41.5 1.7 %pad.29 = bf16[16,64,644]{2,1,0:T(8,128)(2,1)S(1)} pad(bf16[16,60,644]{2,1,0:T(8,128)(2,1)} %reshape.28, bf16[]{:T(256)} %constant.14.clone.1), padding=0_0x0_4x0_0 | pad | bytes 2555394 | tf_op jit(solution)/shard_map/jit(_pad)/pad | solution.py:89
  43.4 3.7 %convolution_convert_fusion = bf16[1024,1280]{1,0:T(8,128)(2,1)} fusion(bf16[1024,644]{1,0:T(8,128)(2,1)S(1)} %bitcast.67, bf16[2,1280]{1,0:T(2,128)(2,1)S(1)} %collective-permute-done.1, bf16[640,1280]{1,0:T(8,128)(2,1)S(1)} %bitcast.74, bf16[2,1280]{1,0:T(2,128)(2,1)S(1)} %collective-permute-done), kind=kOutput, calls=%fused_computation | convolution fusion | flops 1694464000 | bytes 5588992 | tf_op jit(solution)/shard_map/dot_general | solution.py:92
  47.2 1.4 collective-permute-start.5
  49.4 4.6 %collective-permute-start.6 = (bf16[2,192]{0,1:T(8,128)(2,1)S(1)}, bf16[2,192]{0,1:T(8,128)(2,1)S(1)}, u32[]{:S(2)}, u32[]{:S(2)}) collective-permute-start(bf16[2,192]{0,1:T(8,128)(2,1)S(1)} %get-tuple-element.7), channel_id=1, source_target_pairs={{0,8},{8,16},{16,24},{24,32},{32,40},{40,48},{48,56},{56,64},{64,7... | collective-permute-start | bytes 2312 | tf_op jit(solution)/shard_map/ppermute | solution.py:12
  54.1 0.8 fusion.46
  54.8 0.8 collective-permute-done.6
  55.6 0.7 fusion.37
  56.3 0.8 fusion.1
  57.1 1.8 %fusion.3 = bf16[1280,640]{0,1:T(8,128)(2,1)S(1)} fusion(f32[640,1280]{1,0:T(8,128)S(1)} %fusion.37, f32[640,1280]{1,0:T(8,128)S(1)} %fusion.1, bf16[192,5,1280]{2,0,1:T(8,128)(2,1)} %param.4, bf16[2,192]{0,1:T(8,128)(2,1)S(1)} %collective-permute-done.6, bf16[640,192]{0,1:T(8,128)(2,1)S(1)} %fusion.36), kind=kOutput, calls=%fused_computation.6 | convolution fusion | flops 317521920 | bytes 8930048 | tf_op jit(solution)/shard_map/lo,oc->cl/dot_general | solution.py:101
  59.0 2.2 %copy.8 = bf16[1280,640]{1,0:T(8,128)(2,1)} copy(bf16[1280,640]{0,1:T(8,128)(2,1)S(1)} %fusion.3) | data formatting | bytes 3276800 | tf_op jit(solution)/shard_map/add | solution.py:101
  61.1 4.8 %all-to-all-start.1 = ((bf16[8,160,640]{2,1,0:T(8,128)(2,1)}), bf16[8,160,640]{2,1,0:T(8,128)(2,1)S(1)}, u32[]{:S(2)}, u32[]{:S(2)}) async-start(bf16[8,160,640]{2,1,0:T(8,128)(2,1)} %bitcast.20), calls=%async_computation.2 | async-start | bytes 3276800 | tf_op jit(solution)/shard_map/all_to_all | solution.py:108
  65.9 56.1 %reduce-scatter.2.cloned.1.call-done = bf16[1,64,1280]{2,1,0:T(8,128)(2,1)} async-done(((bf16[16,64,1280]{2,1,0:T(8,128)(2,1)}), bf16[1,64,1280]{2,1,0:T(8,128)(2,1)}) %reduce-scatter.2.cloned.1.call-update) | async-done | bytes 163856 | tf_op jit(solution)/shard_map/reduce_scatter | solution.py:93
  122.0 1.0 slice_bitcast_fusion
  123.0 3.2 %collective-permute-start.2 = (bf16[60,1280]{1,0:T(8,128)(2,1)S(1)}, bf16[60,1280]{1,0:T(8,128)(2,1)S(1)}, u32[]{:S(2)}, u32[]{:S(2)}) collective-permute-start(bf16[60,1280]{1,0:T(8,128)(2,1)S(1)} %slice_bitcast_fusion), channel_id=1, source_target_pairs={{0,128},{128,0},{256,384},{384,256},{1,129},{129,1},{257,385},{385... | collective-permute-start | bytes 460808 | tf_op jit(solution)/shard_map/ppermute | solution.py:58
  126.3 4.8 %collective-permute-start.3 = (bf16[60,1280]{1,0:T(8,128)(2,1)S(1)}, bf16[60,1280]{1,0:T(8,128)(2,1)S(1)}, u32[]{:S(2)}, u32[]{:S(2)}) collective-permute-start(bf16[60,1280]{1,0:T(8,128)(2,1)S(1)} %slice_bitcast_fusion), channel_id=1, source_target_pairs={{0,256},{128,384},{256,0},{384,128},{1,257},{129,385},{257,1},{385... | collective-permute-start | bytes 460808 | tf_op jit(solution)/shard_map/ppermute | solution.py:58
  131.0 2.4 %collective-permute-start.4 = (bf16[60,1280]{1,0:T(8,128)(2,1)S(1)}, bf16[60,1280]{1,0:T(8,128)(2,1)S(1)}, u32[]{:S(2)}, u32[]{:S(2)}) collective-permute-start(bf16[60,1280]{1,0:T(8,128)(2,1)S(1)} %slice_bitcast_fusion), channel_id=1, source_target_pairs={{0,384},{128,256},{256,128},{384,0},{1,385},{129,257},{257,129},{3... | collective-permute-start | bytes 460808 | tf_op jit(solution)/shard_map/ppermute | solution.py:58
  133.5 0.9 reduce_sum.12
  135.0 4.5 %collective-permute-done.4 = bf16[60,1280]{1,0:T(8,128)(2,1)S(1)} collective-permute-done((bf16[60,1280]{1,0:T(8,128)(2,1)S(1)}, bf16[60,1280]{1,0:T(8,128)(2,1)S(1)}, u32[]{:S(2)}, u32[]{:S(2)}) %collective-permute-start.4) | collective-permute-done | bytes 153632 | tf_op jit(solution)/shard_map/ppermute | solution.py:58
  139.6 0.9 copy.9
  (34 shorter events, 3.8 us)
Async XLA Ops:
  7.9 20.0 %collective-permute-start.1 = (bf16[2,1280]{1,0:T(2,128)(2,1)S(1)}, bf16[2,1280]{1,0:T(2,128)(2,1)S(1)}, u32[]{:S(2)}, u32[]{:S(2)}) collective-permute-start(bf16[2,1280]{1,0:T(2,128)(2,1)S(1)} %get-tuple-element.5), channel_id=1, source_target_pairs={{8,0},{16,8},{24,16},{32,24},{40,32},{48,40},{56,48},{64,56},{72,6... | collective-permute-start | bytes 15368 | tf_op jit(solution)/shard_map/ppermute | solution.py:15
  9.2 23.3 %collective-permute-start = (bf16[2,1280]{1,0:T(2,128)(2,1)S(1)}, bf16[2,1280]{1,0:T(2,128)(2,1)S(1)}, u32[]{:S(2)}, u32[]{:S(2)}) collective-permute-start(bf16[2,1280]{1,0:T(2,128)(2,1)S(1)} %get-tuple-element.4), channel_id=1, source_target_pairs={{0,8},{8,16},{16,24},{24,32},{32,40},{40,48},{48,56},{56,64},{64,7... | collective-permute-start | bytes 15368 | tf_op jit(solution)/shard_map/ppermute | solution.py:12
  14.9 13.1 %copy-start = (bf16[192,5,1280]{2,0,1:T(8,128)(2,1)S(1)}, bf16[192,5,1280]{2,0,1:T(8,128)(2,1)}, u32[]{:S(2)}) copy-start(bf16[192,5,1280]{2,0,1:T(8,128)(2,1)} %param.4) | copy-start | bytes 7372804
  15.6 18.4 %all-to-all-start = ((bf16[8,40,192]{2,1,0:T(8,128)(2,1)}), bf16[8,40,192]{2,1,0:T(8,128)(2,1)S(1)}, u32[]{:S(2)}, u32[]{:S(2)}) async-start(bf16[8,40,192]{2,1,0:T(8,128)(2,1)} %bitcast.60), calls=%async_computation | async-start | bytes 327680 | tf_op jit(solution)/shard_map/all_to_all | solution.py:75
  24.9 97.1 %reduce-scatter.2.cloned.1.call-start = ((), (), s32[]{:S(2)}) async-start(), calls=%async_computation.3 | async-start | bytes 2785280 | tf_op jit(solution)/shard_map/reduce_scatter | solution.py:93
  27.9 3.1 %copy-start.3 = (bf16[1,640,1280]{2,1,0:T(8,128)(2,1)S(1)}, bf16[1,640,1280]{2,1,0:T(8,128)(2,1)}, u32[]{:S(2)}) copy-start(bf16[1,640,1280]{2,1,0:T(8,128)(2,1)} %param.3) | copy-start | bytes 4915204
  34.0 1.4 copy-start.4
  41.5 1.9 %copy-start.5 = (bf16[1,640,1280]{2,1,0:T(8,128)(2,1)S(1)}, bf16[1,640,1280]{2,1,0:T(8,128)(2,1)}, u32[]{:S(2)}) copy-start(bf16[1,640,1280]{2,1,0:T(8,128)(2,1)} %param.3) | copy-start | bytes 4915204
  47.1 1.7 %copy-start.1 = (bf16[192,5,1280]{2,0,1:T(8,128)(2,1)S(1)}, bf16[192,5,1280]{2,0,1:T(8,128)(2,1)}, u32[]{:S(2)}) copy-start(bf16[192,5,1280]{2,0,1:T(8,128)(2,1)} %param.4) | copy-start | bytes 7372804
  47.2 6.8 %collective-permute-start.5 = (bf16[2,192]{0,1:T(8,128)(2,1)S(1)}, bf16[2,192]{0,1:T(8,128)(2,1)S(1)}, u32[]{:S(2)}, u32[]{:S(2)}) collective-permute-start(bf16[2,192]{0,1:T(8,128)(2,1)S(1)} %get-tuple-element.6), channel_id=1, source_target_pairs={{8,0},{16,8},{24,16},{32,24},{40,32},{48,40},{56,48},{64,56},{72,6... | collective-permute-start | bytes 2312 | tf_op jit(solution)/shard_map/ppermute | solution.py:15
  49.4 6.2 %collective-permute-start.6 = (bf16[2,192]{0,1:T(8,128)(2,1)S(1)}, bf16[2,192]{0,1:T(8,128)(2,1)S(1)}, u32[]{:S(2)}, u32[]{:S(2)}) collective-permute-start(bf16[2,192]{0,1:T(8,128)(2,1)S(1)} %get-tuple-element.7), channel_id=1, source_target_pairs={{0,8},{8,16},{16,24},{24,32},{32,40},{40,48},{48,56},{56,64},{64,7... | collective-permute-start | bytes 2312 | tf_op jit(solution)/shard_map/ppermute | solution.py:12
  61.1 72.3 %all-to-all-start.1 = ((bf16[8,160,640]{2,1,0:T(8,128)(2,1)}), bf16[8,160,640]{2,1,0:T(8,128)(2,1)S(1)}, u32[]{:S(2)}, u32[]{:S(2)}) async-start(bf16[8,160,640]{2,1,0:T(8,128)(2,1)} %bitcast.20), calls=%async_computation.2 | async-start | bytes 3276800 | tf_op jit(solution)/shard_map/all_to_all | solution.py:108
  122.0 17.5 %copy-start.2 = (bf16[1,64,1280]{2,1,0:T(8,128)(2,1)S(1)}, bf16[1,64,1280]{2,1,0:T(8,128)(2,1)}, u32[]{:S(2)}) copy-start(bf16[1,64,1280]{2,1,0:T(8,128)(2,1)} %reduce-scatter.2.cloned.1.call-done) | copy-start | bytes 491524
  123.0 11.4 %collective-permute-start.2 = (bf16[60,1280]{1,0:T(8,128)(2,1)S(1)}, bf16[60,1280]{1,0:T(8,128)(2,1)S(1)}, u32[]{:S(2)}, u32[]{:S(2)}) collective-permute-start(bf16[60,1280]{1,0:T(8,128)(2,1)S(1)} %slice_bitcast_fusion), channel_id=1, source_target_pairs={{0,128},{128,0},{256,384},{384,256},{1,129},{129,1},{257,385},{385... | collective-permute-start | bytes 460808 | tf_op jit(solution)/shard_map/ppermute | solution.py:58
  126.3 8.7 %collective-permute-start.3 = (bf16[60,1280]{1,0:T(8,128)(2,1)S(1)}, bf16[60,1280]{1,0:T(8,128)(2,1)S(1)}, u32[]{:S(2)}, u32[]{:S(2)}) collective-permute-start(bf16[60,1280]{1,0:T(8,128)(2,1)S(1)} %slice_bitcast_fusion), channel_id=1, source_target_pairs={{0,256},{128,384},{256,0},{384,128},{1,257},{129,385},{257,1},{385... | collective-permute-start | bytes 460808 | tf_op jit(solution)/shard_map/ppermute | solution.py:58
  131.0 8.4 %collective-permute-start.4 = (bf16[60,1280]{1,0:T(8,128)(2,1)S(1)}, bf16[60,1280]{1,0:T(8,128)(2,1)S(1)}, u32[]{:S(2)}, u32[]{:S(2)}) collective-permute-start(bf16[60,1280]{1,0:T(8,128)(2,1)S(1)} %slice_bitcast_fusion), channel_id=1, source_target_pairs={{0,384},{128,256},{256,128},{384,0},{1,385},{129,257},{257,129},{3... | collective-permute-start | bytes 460808 | tf_op jit(solution)/shard_map/ppermute | solution.py:58
Sparse Core Ops, SparseCore 0:
  47.3 74.7 reduce-scatter.1

commit v5 on v4

--- a/solution.py
+++ b/solution.py
@@ -74,7 +74,11 @@
     grouped = trunk_grad[0].reshape(rows, n_section, out_ch).transpose(1, 0, 2)
     pooled = lax.all_to_all(grouped, "section", 0, 0, tiled=True).reshape(rows * n_section, out_ch)
     padded = extended(local_signal, (("seq", 0),), 2)
-    linear = convolve(padded, kernel, length)
+    stacked = kernel.transpose(1, 0, 2).reshape(taps_count * out_ch, in_ch)
+    per_tap = jnp.einsum("tc,jc->tj", padded, stacked, preferred_element_type=jnp.float32)
+    linear = per_tap[0:length, 0:out_ch]
+    for k in range(1, taps_count):
+        linear = linear + per_tap[k : k + length, k * out_ch : (k + 1) * out_ch]
     grad_hidden = 0.5 * jnp.repeat(pooled.astype(jnp.float32), 2, axis=0)
     grad_pre = (grad_hidden * gelu_slope(linear)).astype(jnp.bfloat16)
     grad_ext = extended(grad_pre, (("seq", 0),), 2)
@@ -93,7 +97,14 @@
     weight_part = lax.psum_scatter(
         partial.reshape(n_seq, chunk_rows, in_ch), "seq", scatter_dimension=0, tiled=True
     )[0, :chunk]
-    weight_grad = symmetric_sum(weight_part, "dp").reshape(-1, taps_count, in_ch)
+    n_dp = lax.axis_size("dp")
+    copies = lax.all_to_all(
+        jnp.broadcast_to(weight_part[None], (n_dp,) + weight_part.shape), "dp", 0, 0, tiled=True
+    ).astype(jnp.float32)
+    total = copies[0]
+    for j in range(1, n_dp):
+        total = total + copies[j]
+    weight_grad = total.reshape(-1, taps_count, in_ch)
     summed = jnp.einsum(
         "lo,oc->cl", grad_ext[4 : 4 + length], kernel[:, 0, :], preferred_element_type=jnp.float32
     )

time: 148 us -> 149 us (level)
  local copies, waits for them, and re-layouts: 13.6 us -> 22.5 us
  starting transfers between devices: 36.4 us -> 27.8 us
  matrix products: 20.1 us -> 11.9 us
  waiting for transfers between devices: 61.9 us -> 68.7 us
  other arithmetic: 1.04 us -> 2.86 us
    ppermute x3 -> x0, starting transfers between devices: 10.4 us -> none  [symmetric_sum(): lax.ppermute(block, axis, [(i, i ^ step) for i in range(count)])]
    all_to_all x0 -> x1, waiting for transfers between devices: none -> 7.85 us  [shards(): lax.all_to_all(jnp.broadcast_to(weight_part[None], (n_dp,) + weight_part....]
    dot_general x5 -> x1, matrix products: 11.6 us -> 4.11 us  [shards(): jnp.einsum('tc,jc->tj', padded, stacked, preferred_element_type=jnp.float32)]
    ppermute x3 -> x0, waiting for transfers between devices: 5.06 us -> none  [symmetric_sum(): lax.ppermute(block, axis, [(i, i ^ step) for i in range(count)])]
    all_to_all x0 -> x1, starting transfers between devices: none -> 4.08 us  [shards(): lax.all_to_all(jnp.broadcast_to(weight_part[None], (n_dp,) + weight_part....]
    reduce_scatter x1, waiting for transfers between devices: 56.1 us -> 59.8 us  [shards(): lax.psum_scatter(partial.reshape(n_seq, chunk_rows, in_ch), 'seq', scatte...]
    another operation x2, local copies, waits for them, and re-layouts: 1.03 us -> 4.27 us  [shards(): jnp.stack([jnp.pad(grad_middle.T, ((0, 0), (k, taps_count - 1 - k))) for...]
    all_to_all x1, starting transfers between devices: 9.3 us -> 6.64 us  [shards(): lax.all_to_all(grouped, 'section', 0, 0, tiled=True)]
  transfers between devices with their start and end apart: 10 -> 8, of which waited for: 4 -> 4; matrix products, arithmetic and copies ran while one was open for 13% -> 9% of each run, Pallas kernels for 0% -> 0%
where the time goes in v5:
time: 149 us; the launch traced here: 148 us
  waiting for transfers between devices  68.7 us (46%)
  starting transfers between devices  27.8 us (19%)
  local copies, waits for them, and re-layouts  22.5 us (15%)
  between operations  14.2 us (10%)
  matrix products  11.9 us (8%)
  other arithmetic  2.86 us (2%)
    reduce_scatter x1, waiting for transfers between devices, shards(): lax.psum_scatter(partial.reshape(n_seq, chunk_rows, in_ch), 'seq', scatte...  59.8 us
    ppermute x2, starting transfers between devices, extended(): lax.ppermute(lax.slice_in_dim(block, block.shape[dim] - width, None, axis...  8.79 us
    all_to_all x1, waiting for transfers between devices, shards(): lax.all_to_all(jnp.broadcast_to(weight_part[None], (n_dp,) + weight_part....  7.85 us
    all_to_all x1, starting transfers between devices, shards(): lax.all_to_all(grouped, 'section', 0, 0, tiled=True)  6.64 us
    all_to_all x1, starting transfers between devices, shards(): received = lax.all_to_all(groups, 'section', 0, 0, tiled=True)  5.6 us
    unnamed x9, local copies, waits for them, and re-layouts  4.49 us
    another operation x2, local copies, waits for them, and re-layouts, shards(): jnp.stack([jnp.pad(grad_middle.T, ((0, 0), (k, taps_count - 1 - k))) for...  4.27 us
    dot_general x1, matrix products, shards(): jnp.einsum('tc,jc->tj', padded, stacked, preferred_element_type=jnp.float32)  4.11 us
  transfers between devices with their start and end apart: 8, of which 4 were waited for; matrix products, arithmetic and copies ran while one was open for 9% of the time, Pallas kernels for 0%

profile of v5, /device:TPU:6, one launch (start us, length us, event | category | flops | bytes accessed | tf_op | source)
XLA Modules:
  0.0 147.9 jit_solution(11343286712628284015)
XLA Ops:
  7.2 0.8 slice_bitcast_fusion.2
  7.9 3.8 %collective-permute-start = (bf16[2,1280]{1,0:T(2,128)(2,1)S(1)}, bf16[2,1280]{1,0:T(2,128)(2,1)S(1)}, u32[]{:S(2)}, u32[]{:S(2)}) collective-permute-start(bf16[2,1280]{1,0:T(2,128)(2,1)S(1)} %get-tuple-element.4), channel_id=1, source_target_pairs={{0,8},{8,16},{16,24},{24,32},{32,40},{40,48},{48,56},{56,64},{64,7... | collective-permute-start | bytes 15368 | tf_op jit(solution)/shard_map/ppermute | solution.py:12
  11.8 1.3 collective-permute-start.1
  13.1 1.1 reshape_squeeze.3
  14.1 0.7 copy.10
  14.8 6.6 %all-to-all-start = ((bf16[8,40,192]{2,1,0:T(8,128)(2,1)}), bf16[8,40,192]{2,1,0:T(8,128)(2,1)S(1)}, u32[]{:S(2)}, u32[]{:S(2)}) async-start(bf16[8,40,192]{2,1,0:T(8,128)(2,1)} %bitcast.48), calls=%async_computation | async-start | bytes 327680 | tf_op jit(solution)/shard_map/all_to_all | solution.py:75
  21.5 4.1 %fusion.4 = f32[644,960]{1,0:T(8,128)S(1)} fusion(bf16[960,1280]{1,0:T(8,128)(2,1)} %bitcast.56, bf16[2,1280]{1,0:T(2,128)(2,1)S(1)} %collective-permute-done.1, bf16[640,1280]{1,0:T(8,128)(2,1)} %bitcast.60, bf16[2,1280]{1,0:T(2,128)(2,1)S(1)} %collective-permute-done), kind=kOutput, calls=%fused_computation.9 | convolution fusion | flops 1587640320 | bytes 6579200 | tf_op jit(solution)/shard_map/tc,jc->tj/dot_general | solution.py:78
  25.9 1.1 broadcast_in_dim.13
  27.0 2.4 %mul.42 = f32[640,192]{1,0:T(8,128)} reshape(f32[320,2,192]{2,1,0:T(2,128)} %broadcast_in_dim.13) | data formatting | bytes 983040 | tf_op jit(solution)/shard_map/mul | solution.py:82
  29.4 1.7 %fusion.10 = bf16[640,192]{1,0:T(8,128)(2,1)S(1)} fusion(f32[640,192]{1,0:T(8,128)} %mul.42, f32[644,960]{1,0:T(8,128)S(1)} %fusion.4), kind=kLoop, calls=%fused_computation.15 | loop fusion | flops 1720320 | bytes 3194880 | tf_op jit(solution)/shard_map/convert_element_type | solution.py:83
  31.1 0.8 bitcast_dynamic-update-slice_fusion.4
  31.9 0.8 bitcast_dynamic-update-slice_fusion.3
  32.7 0.8 bitcast_dynamic-update-slice_fusion.2
  33.5 0.8 bitcast_dynamic-update-slice_fusion.1
  34.3 0.8 bitcast_dynamic-update-slice_fusion
  35.2 3.5 %copy.6 = bf16[192,5,644]{2,1,0:T(8,128)(2,1)S(1)} copy(bf16[192,5,644]{0,2,1:T(8,128)(2,1)} %bitcast_dynamic-update-slice_fusion) | data formatting | bytes 2472960 | tf_op jit(solution)/shard_map/stack | solution.py:89
  38.6 2.0 %reshape.37 = bf16[16,60,644]{2,1,0:T(8,128)(2,1)} reshape(bf16[192,5,644]{2,1,0:T(8,128)(2,1)S(1)} %copy.6) | data formatting | bytes 2472960 | tf_op jit(solution)/shard_map/reshape | solution.py:92
  40.6 1.7 %pad.29 = bf16[16,64,644]{2,1,0:T(8,128)(2,1)S(1)} pad(bf16[16,60,644]{2,1,0:T(8,128)(2,1)} %reshape.37, bf16[]{:T(256)} %constant.14.clone.1), padding=0_0x0_4x0_0 | pad | bytes 2555394 | tf_op jit(solution)/shard_map/jit(_pad)/pad | solution.py:93
  42.5 3.8 %convolution_convert_fusion = bf16[1024,1280]{1,0:T(8,128)(2,1)} fusion(bf16[1024,644]{1,0:T(8,128)(2,1)S(1)} %bitcast.57, bf16[2,1280]{1,0:T(2,128)(2,1)S(1)} %collective-permute-done.1, bf16[640,1280]{1,0:T(8,128)(2,1)S(1)} %bitcast.61, bf16[2,1280]{1,0:T(2,128)(2,1)S(1)} %collective-permute-done), kind=kOutput, calls=%fused_computation | convolution fusion | flops 1694464000 | bytes 5588992 | tf_op jit(solution)/shard_map/dot_general | solution.py:96
  46.3 1.4 collective-permute-start.2
  48.5 5.0 %collective-permute-start.3 = (bf16[2,192]{1,0:T(2,128)(2,1)S(1)}, bf16[2,192]{1,0:T(2,128)(2,1)S(1)}, u32[]{:S(2)}, u32[]{:S(2)}) collective-permute-start(bf16[2,192]{1,0:T(2,128)(2,1)S(1)} %get-tuple-element.7), channel_id=1, source_target_pairs={{0,8},{8,16},{16,24},{24,32},{32,40},{40,48},{48,56},{56,64},{64,7... | collective-permute-start | bytes 2312 | tf_op jit(solution)/shard_map/ppermute | solution.py:12
  54.1 0.7 collective-permute-done.3
  56.0 1.7 %fusion.3 = bf16[1280,640]{0,1:T(8,128)(2,1)S(1)} fusion(f32[640,1280]{1,0:T(8,128)S(1)} %fusion.11, f32[640,1280]{1,0:T(8,128)S(1)} %fusion.1, bf16[192,5,1280]{2,0,1:T(8,128)(2,1)} %param.4, bf16[2,192]{1,0:T(2,128)(2,1)S(1)} %collective-permute-done.3, bf16[640,192]{1,0:T(8,128)(2,1)S(1)} %fusion.10), kind=kOutput, calls=%fused_computation.6 | convolution fusion | flops 317521920 | bytes 8930048 | tf_op jit(solution)/shard_map/lo,oc->cl/dot_general | solution.py:112
  57.6 2.2 %copy.7 = bf16[1280,640]{1,0:T(8,128)(2,1)} copy(bf16[1280,640]{0,1:T(8,128)(2,1)S(1)} %fusion.3) | data formatting | bytes 3276800 | tf_op jit(solution)/shard_map/add | solution.py:112
  59.8 5.6 %all-to-all-start.2 = ((bf16[8,160,640]{2,1,0:T(8,128)(2,1)}), bf16[8,160,640]{2,1,0:T(8,128)(2,1)S(1)}, u32[]{:S(2)}, u32[]{:S(2)}) async-start(bf16[8,160,640]{2,1,0:T(8,128)(2,1)} %bitcast.54), calls=%async_computation.3 | async-start | bytes 3276800 | tf_op jit(solution)/shard_map/all_to_all | solution.py:119
  65.4 59.8 %reduce-scatter.2.cloned.1.call-done = bf16[1,64,1280]{2,1,0:T(8,128)(2,1)} async-done(((bf16[16,64,1280]{2,1,0:T(8,128)(2,1)}), bf16[1,64,1280]{2,1,0:T(8,128)(2,1)}) %reduce-scatter.2.cloned.1.call-update) | async-done | bytes 163856 | tf_op jit(solution)/shard_map/reduce_scatter | solution.py:97
  125.3 0.9 slice_bitcast_fusion
  126.2 0.9 broadcast_in_dim.15
  127.1 4.1 %all-to-all-start.1 = ((bf16[4,60,1280]{2,1,0:T(8,128)(2,1)}), bf16[4,60,1280]{2,1,0:T(8,128)(2,1)S(1)}, u32[]{:S(2)}, u32[]{:S(2)}) async-start(bf16[4,60,1280]{2,1,0:T(8,128)(2,1)} %broadcast_in_dim.15), calls=%async_computation.2 | async-start | bytes 1310720 | tf_op jit(solution)/shard_map/all_to_all | solution.py:101
  131.2 0.9 reduce_sum.12
  132.1 7.8 %all-to-all-done.1 = bf16[4,60,1280]{2,1,0:T(8,128)(2,1)S(1)} async-done(((bf16[4,60,1280]{2,1,0:T(8,128)(2,1)}), bf16[4,60,1280]{2,1,0:T(8,128)(2,1)S(1)}, u32[]{:S(2)}, u32[]{:S(2)}) %all-to-all-start.1) | async-done | bytes 614432 | tf_op jit(solution)/shard_map/all_to_all | solution.py:101
  140.2 0.9 copy.8
  (20 shorter events, 3.3 us)
Async XLA Ops:
  7.9 13.6 %collective-permute-start = (bf16[2,1280]{1,0:T(2,128)(2,1)S(1)}, bf16[2,1280]{1,0:T(2,128)(2,1)S(1)}, u32[]{:S(2)}, u32[]{:S(2)}) collective-permute-start(bf16[2,1280]{1,0:T(2,128)(2,1)S(1)} %get-tuple-element.4), channel_id=1, source_target_pairs={{0,8},{8,16},{16,24},{24,32},{32,40},{40,48},{48,56},{56,64},{64,7... | collective-permute-start | bytes 15368 | tf_op jit(solution)/shard_map/ppermute | solution.py:12
  11.8 9.7 %collective-permute-start.1 = (bf16[2,1280]{1,0:T(2,128)(2,1)S(1)}, bf16[2,1280]{1,0:T(2,128)(2,1)S(1)}, u32[]{:S(2)}, u32[]{:S(2)}) collective-permute-start(bf16[2,1280]{1,0:T(2,128)(2,1)S(1)} %get-tuple-element.5), channel_id=1, source_target_pairs={{8,0},{16,8},{24,16},{32,24},{40,32},{48,40},{56,48},{64,56},{72,6... | collective-permute-start | bytes 15368 | tf_op jit(solution)/shard_map/ppermute | solution.py:15
  14.8 11.0 %all-to-all-start = ((bf16[8,40,192]{2,1,0:T(8,128)(2,1)}), bf16[8,40,192]{2,1,0:T(8,128)(2,1)S(1)}, u32[]{:S(2)}, u32[]{:S(2)}) async-start(bf16[8,40,192]{2,1,0:T(8,128)(2,1)} %bitcast.48), calls=%async_computation | async-start | bytes 327680 | tf_op jit(solution)/shard_map/all_to_all | solution.py:75
  21.5 103.8 %reduce-scatter.2.cloned.1.call-start = ((), (), s32[]{:S(2)}) async-start(), calls=%async_computation.4 | async-start | bytes 2785280 | tf_op jit(solution)/shard_map/reduce_scatter | solution.py:97
  40.6 1.9 %copy-start.1 = (bf16[1,640,1280]{2,1,0:T(8,128)(2,1)S(1)}, bf16[1,640,1280]{2,1,0:T(8,128)(2,1)}, u32[]{:S(2)}) copy-start(bf16[1,640,1280]{2,1,0:T(8,128)(2,1)} %param.3) | copy-start | bytes 4915204
  46.2 1.7 %copy-start = (bf16[192,5,1280]{2,0,1:T(8,128)(2,1)S(1)}, bf16[192,5,1280]{2,0,1:T(8,128)(2,1)}, u32[]{:S(2)}) copy-start(bf16[192,5,1280]{2,0,1:T(8,128)(2,1)} %param.4) | copy-start | bytes 7372804
  46.3 7.2 %collective-permute-start.2 = (bf16[2,192]{1,0:T(2,128)(2,1)S(1)}, bf16[2,192]{1,0:T(2,128)(2,1)S(1)}, u32[]{:S(2)}, u32[]{:S(2)}) collective-permute-start(bf16[2,192]{1,0:T(2,128)(2,1)S(1)} %get-tuple-element.6), channel_id=1, source_target_pairs={{8,0},{16,8},{24,16},{32,24},{40,32},{48,40},{56,48},{64,56},{72,6... | collective-permute-start | bytes 2312 | tf_op jit(solution)/shard_map/ppermute | solution.py:15
  48.5 6.3 %collective-permute-start.3 = (bf16[2,192]{1,0:T(2,128)(2,1)S(1)}, bf16[2,192]{1,0:T(2,128)(2,1)S(1)}, u32[]{:S(2)}, u32[]{:S(2)}) collective-permute-start(bf16[2,192]{1,0:T(2,128)(2,1)S(1)} %get-tuple-element.7), channel_id=1, source_target_pairs={{0,8},{8,16},{16,24},{24,32},{32,40},{40,48},{48,56},{56,64},{64,7... | collective-permute-start | bytes 2312 | tf_op jit(solution)/shard_map/ppermute | solution.py:12
  59.8 66.4 %all-to-all-start.2 = ((bf16[8,160,640]{2,1,0:T(8,128)(2,1)}), bf16[8,160,640]{2,1,0:T(8,128)(2,1)S(1)}, u32[]{:S(2)}, u32[]{:S(2)}) async-start(bf16[8,160,640]{2,1,0:T(8,128)(2,1)} %bitcast.54), calls=%async_computation.3 | async-start | bytes 3276800 | tf_op jit(solution)/shard_map/all_to_all | solution.py:119
  127.1 12.9 %all-to-all-start.1 = ((bf16[4,60,1280]{2,1,0:T(8,128)(2,1)}), bf16[4,60,1280]{2,1,0:T(8,128)(2,1)S(1)}, u32[]{:S(2)}, u32[]{:S(2)}) async-start(bf16[4,60,1280]{2,1,0:T(8,128)(2,1)} %broadcast_in_dim.15), calls=%async_computation.2 | async-start | bytes 1310720 | tf_op jit(solution)/shard_map/all_to_all | solution.py:101
Sparse Core Ops, SparseCore 0:
  46.4 78.8 reduce-scatter.1

commit v6 on v5

--- a/solution.py
+++ b/solution.py
@@ -71,32 +71,29 @@
     in_ch = kernel.shape[2]
     n_section = lax.axis_size("section")
     rows = trunk_grad.shape[1]
-    grouped = trunk_grad[0].reshape(rows, n_section, out_ch).transpose(1, 0, 2)
-    pooled = lax.all_to_all(grouped, "section", 0, 0, tiled=True).reshape(rows * n_section, out_ch)
+    grouped = jnp.repeat(trunk_grad[0].reshape(rows, n_section, out_ch), 2, axis=0).transpose(1, 0, 2)
+    upsampled = lax.all_to_all(grouped, "section", 0, 0, tiled=True).reshape(2 * rows * n_section, out_ch)
     padded = extended(local_signal, (("seq", 0),), 2)
     stacked = kernel.transpose(1, 0, 2).reshape(taps_count * out_ch, in_ch)
     per_tap = jnp.einsum("tc,jc->tj", padded, stacked, preferred_element_type=jnp.float32)
     linear = per_tap[0:length, 0:out_ch]
     for k in range(1, taps_count):
         linear = linear + per_tap[k : k + length, k * out_ch : (k + 1) * out_ch]
-    grad_hidden = 0.5 * jnp.repeat(pooled.astype(jnp.float32), 2, axis=0)
+    grad_hidden = 0.5 * upsampled.astype(jnp.float32)
     grad_pre = (grad_hidden * gelu_slope(linear)).astype(jnp.bfloat16)
     grad_ext = extended(grad_pre, (("seq", 0),), 2)
     grad_middle = grad_ext[2 : 2 + length]
     n_seq = lax.axis_size("seq")
-    chunk = out_ch // n_seq * taps_count
-    chunk_rows = -(-chunk // 16) * 16
-    shifted = jnp.stack(
-        [jnp.pad(grad_middle.T, ((0, 0), (k, taps_count - 1 - k))) for k in range(taps_count)],
+    own = out_ch // n_seq
+    own_rows = -(-own // 16) * 16
+    spread = jnp.pad(grad_middle.T.reshape(n_seq, own, length), ((0, 0), (0, own_rows - own), (0, 0)))
+    banded = jnp.concatenate(
+        [jnp.pad(spread, ((0, 0), (0, 0), (k, taps_count - 1 - k))) for k in range(taps_count)],
         axis=1,
-    ).reshape(n_seq, chunk, length + taps_count - 1)
-    banded = jnp.pad(shifted, ((0, 0), (0, chunk_rows - chunk), (0, 0))).reshape(
-        n_seq * chunk_rows, length + taps_count - 1
-    )
+    ).reshape(n_seq * taps_count * own_rows, length + taps_count - 1)
     partial = jnp.dot(banded, padded, preferred_element_type=jnp.float32).astype(jnp.bfloat16)
-    weight_part = lax.psum_scatter(
-        partial.reshape(n_seq, chunk_rows, in_ch), "seq", scatter_dimension=0, tiled=True
-    )[0, :chunk]
+    partial = partial.reshape(n_seq, taps_count * own_rows, in_ch)
+    weight_part = lax.psum_scatter(partial, "seq", scatter_dimension=0, tiled=True)[0]
     n_dp = lax.axis_size("dp")
     copies = lax.all_to_all(
         jnp.broadcast_to(weight_part[None], (n_dp,) + weight_part.shape), "dp", 0, 0, tiled=True
@@ -104,7 +101,7 @@
     total = copies[0]
     for j in range(1, n_dp):
         total = total + copies[j]
-    weight_grad = total.reshape(-1, taps_count, in_ch)
+    weight_grad = total.reshape(taps_count, own_rows, in_ch)[:, :own].transpose(1, 0, 2)
     summed = jnp.einsum(
         "lo,oc->cl", grad_ext[4 : 4 + length], kernel[:, 0, :], preferred_element_type=jnp.float32
     )

time: 149 us -> 141 us (0.946)
  blocking collectives: 0 us -> 26 us
  waiting for transfers between devices: 68.7 us -> 53.5 us
  local copies, waits for them, and re-layouts: 22.5 us -> 9.74 us
  starting transfers between devices: 27.8 us -> 22.4 us
    all_to_all x0 -> x1, blocking collectives: none -> 26 us  [shards(): received = lax.all_to_all(groups, 'section', 0, 0, tiled=True)]
    reduce_scatter x1, waiting for transfers between devices: 59.8 us -> 42 us  [shards(): lax.psum_scatter(partial, 'seq', scatter_dimension=0, tiled=True)[0]]
    all_to_all x1 -> x0, starting transfers between devices: 5.6 us -> none  [shards(): received = lax.all_to_all(groups, 'section', 0, 0, tiled=True)]
    another operation x4 -> x2, local copies, waits for them, and re-layouts: 6.05 us -> 1.12 us  [shards(): trunk_grad[0].reshape(rows, n_section, out_ch)]
    unnamed x9 -> x8, local copies, waits for them, and re-layouts: 4.49 us -> 1.34 us
    mul x1 -> x0, local copies, waits for them, and re-layouts: 2.39 us -> none  [shards(): grad_hidden = 0.5 * jnp.repeat(pooled.astype(jnp.float32), 2, axis=0)]
    all_to_all x1, waiting for transfers between devices: 0.26 us -> 2.02 us  [shards(): lax.all_to_all(grouped, 'section', 0, 0, tiled=True)]
    pad x1, local copies, waits for them, and re-layouts: 1.72 us -> 0.03 us  [shards(): jnp.pad(grad_middle.T.reshape(n_seq, own, length), ((0, 0), (0, own_rows...]
  transfers between devices with their start and end apart: 8 -> 7, of which waited for: 4 -> 4; matrix products, arithmetic and copies ran while one was open for 9% -> 10% of each run, Pallas kernels for 0% -> 0%
where the time goes in v6:
time: 141 us; the launch traced here: 140 us
  waiting for transfers between devices  53.5 us (38%)
  blocking collectives  26 us (18%)
  starting transfers between devices  22.4 us (16%)
  between operations  14.2 us (10%)
  matrix products  12.3 us (9%)
  local copies, waits for them, and re-layouts  9.74 us (7%)
  other arithmetic  1.85 us (1%)
    reduce_scatter x1, waiting for transfers between devices, shards(): lax.psum_scatter(partial, 'seq', scatter_dimension=0, tiled=True)[0]  42 us
    all_to_all x1, blocking collectives, shards(): received = lax.all_to_all(groups, 'section', 0, 0, tiled=True)  26 us
    ppermute x2, starting transfers between devices, extended(): lax.ppermute(lax.slice_in_dim(block, block.shape[dim] - width, None, axis...  8.79 us
    all_to_all x1, waiting for transfers between devices, shards(): lax.all_to_all(jnp.broadcast_to(weight_part[None], (n_dp,) + weight_part....  8.73 us
    all_to_all x1, starting transfers between devices, shards(): lax.all_to_all(grouped, 'section', 0, 0, tiled=True)  6.69 us
    all_to_all x1, starting transfers between devices, shards(): lax.all_to_all(jnp.broadcast_to(weight_part[None], (n_dp,) + weight_part....  4.2 us
    dot_general x1, matrix products, shards(): jnp.dot(banded, padded, preferred_element_type=jnp.float32)  4.18 us
    dot_general x1, matrix products, shards(): jnp.einsum('tc,jc->tj', padded, stacked, preferred_element_type=jnp.float32)  4.11 us
  transfers between devices with their start and end apart: 7, of which 4 were waited for; matrix products, arithmetic and copies ran while one was open for 10% of the time, Pallas kernels for 0%

profile of v6, /device:TPU:6, one launch (start us, length us, event | category | flops | bytes accessed | tf_op | source)
XLA Modules:
  0.0 140.0 jit_solution(15872551042198493747)
XLA Ops:
  7.2 0.8 slice_bitcast_fusion.2
  7.9 3.8 %collective-permute-start = (bf16[2,1280]{1,0:T(2,128)(2,1)S(1)}, bf16[2,1280]{1,0:T(2,128)(2,1)S(1)}, u32[]{:S(2)}, u32[]{:S(2)}) collective-permute-start(bf16[2,1280]{1,0:T(2,128)(2,1)S(1)} %get-tuple-element.2), channel_id=1, source_target_pairs={{0,8},{8,16},{16,24},{24,32},{32,40},{40,48},{48,56},{56,64},{64,7... | collective-permute-start | bytes 15368 | tf_op jit(solution)/shard_map/ppermute | solution.py:12
  11.8 1.3 collective-permute-start.1
  13.1 1.1 reshape_squeeze.3
  14.2 0.2 broadcast_in_dim.13
  14.4 1.0 reshape.36
  15.4 6.7 %all-to-all-start = ((bf16[8,80,192]{2,1,0:T(8,128)(2,1)}), bf16[8,80,192]{2,1,0:T(8,128)(2,1)S(1)}, u32[]{:S(2)}, u32[]{:S(2)}) async-start(bf16[8,80,192]{2,1,0:T(8,128)(2,1)} %bitcast), calls=%async_computation | async-start | bytes 655360 | tf_op jit(solution)/shard_map/all_to_all | solution.py:75
  22.1 4.1 %fusion.4 = f32[644,960]{1,0:T(8,128)S(1)} fusion(bf16[960,1280]{1,0:T(8,128)(2,1)} %bitcast.45, bf16[2,1280]{1,0:T(2,128)(2,1)S(1)} %collective-permute-done.1, bf16[640,1280]{1,0:T(8,128)(2,1)} %bitcast.50, bf16[2,1280]{1,0:T(2,128)(2,1)S(1)} %collective-permute-done), kind=kOutput, calls=%fused_computation.9 | convolution fusion | flops 1587640320 | bytes 6579200 | tf_op jit(solution)/shard_map/tc,jc->tj/dot_general | solution.py:78
  26.2 2.0 %all-to-all-done = bf16[8,80,192]{2,1,0:T(8,128)(2,1)S(1)} async-done(((bf16[8,80,192]{2,1,0:T(8,128)(2,1)}), bf16[8,80,192]{2,1,0:T(8,128)(2,1)S(1)}, u32[]{:S(2)}, u32[]{:S(2)}) %all-to-all-start) | async-done | bytes 245792 | tf_op jit(solution)/shard_map/all_to_all | solution.py:75
  28.3 0.7 fusion.10
  29.0 0.2 copy.7
  29.3 0.2 pad_dynamic-update-slice_fusion.3
  29.5 0.2 pad_dynamic-update-slice_fusion.2
  30.0 0.6 copy-done.1
  30.6 4.2 %convolution_convert_fusion = bf16[1280,1280]{1,0:T(8,128)(2,1)} fusion(bf16[1280,644]{1,0:T(8,128)(2,1)S(1)} %bitcast.49, bf16[2,1280]{1,0:T(2,128)(2,1)S(1)} %collective-permute-done.1, bf16[640,1280]{1,0:T(8,128)(2,1)S(1)} %bitcast.51, bf16[2,1280]{1,0:T(2,128)(2,1)S(1)} %collective-permute-done), kind=kOutput, calls=%fused_computation | convolution fusion | flops 2116843520 | bytes 6574080 | tf_op jit(solution)/shard_map/dot_general | solution.py:94
  34.8 1.4 %collective-permute-start.2 = (bf16[2,192]{1,0:T(2,128)(2,1)S(1)}, bf16[2,192]{1,0:T(2,128)(2,1)S(1)}, u32[]{:S(2)}, u32[]{:S(2)}) collective-permute-start(bf16[2,192]{1,0:T(2,128)(2,1)S(1)} %get-tuple-element.4), channel_id=1, source_target_pairs={{8,0},{16,8},{24,16},{32,24},{40,32},{48,40},{56,48},{64,56},{72,6... | collective-permute-start | bytes 2312 | tf_op jit(solution)/shard_map/ppermute | solution.py:15
  36.2 0.2 copy-done
  36.5 0.6 fusion.14
  37.0 5.0 %collective-permute-start.3 = (bf16[2,192]{1,0:T(2,128)(2,1)S(1)}, bf16[2,192]{1,0:T(2,128)(2,1)S(1)}, u32[]{:S(2)}, u32[]{:S(2)}) collective-permute-start(bf16[2,192]{1,0:T(2,128)(2,1)S(1)} %get-tuple-element.5), channel_id=1, source_target_pairs={{0,8},{8,16},{16,24},{24,32},{32,40},{40,48},{48,56},{56,64},{64,7... | collective-permute-start | bytes 2312 | tf_op jit(solution)/shard_map/ppermute | solution.py:12
  42.0 0.6 fusion.16
  42.6 0.7 collective-permute-done.3
  43.3 0.6 fusion.11
  43.9 0.7 fusion.1
  44.6 1.6 %fusion.3 = bf16[1280,640]{0,1:T(8,128)(2,1)S(1)} fusion(f32[640,1280]{1,0:T(8,128)S(1)} %fusion.11, f32[640,1280]{1,0:T(8,128)S(1)} %fusion.1, bf16[192,5,1280]{2,0,1:T(8,128)(2,1)} %param.4, bf16[2,192]{1,0:T(2,128)(2,1)S(1)} %collective-permute-done.3, bf16[640,192]{1,0:T(8,128)(2,1)S(1)} %fusion.10), kind=kOutput, calls=%fused_computation.6 | convolution fusion | flops 317521920 | bytes 8930048 | tf_op jit(solution)/shard_map/lo,oc->cl/dot_general | solution.py:109
  46.2 2.2 %copy.8 = bf16[1280,640]{1,0:T(8,128)(2,1)} copy(bf16[1280,640]{0,1:T(8,128)(2,1)S(1)} %fusion.3) | data formatting | bytes 3276800 | tf_op jit(solution)/shard_map/add | solution.py:109
  48.4 26.0 %all_to_all.15 = bf16[8,160,640]{2,1,0:T(8,128)(2,1)S(1)} all-to-all(bf16[8,160,640]{2,1,0:T(8,128)(2,1)} %bitcast.43), channel_id=1, replica_groups=mesh['dp'=4,'seq'=16,'section'=8] {'section'}, dimensions={0} | all-to-all | bytes 3276800 | tf_op jit(solution)/shard_map/all_to_all | solution.py:116
  74.4 42.0 %reduce-scatter.2.cloned.1.call-done = bf16[1,80,1280]{2,1,0:T(8,128)(2,1)} async-done(((bf16[16,80,1280]{2,1,0:T(8,128)(2,1)}), bf16[1,80,1280]{2,1,0:T(8,128)(2,1)}) %reduce-scatter.2.cloned.1.call-update) | async-done | bytes 204816 | tf_op jit(solution)/shard_map/reduce_scatter | solution.py:96
  116.5 1.9 %broadcast_in_dim.15 = bf16[4,80,1280]{2,1,0:T(8,128)(2,1)} broadcast(bf16[80,1280]{1,0:T(8,128)(2,1)} %bitcast.47), dimensions={1,2} | broadcast | bytes 1024000 | tf_op jit(solution)/shard_map/broadcast_in_dim | solution.py:99
  118.3 4.2 %all-to-all-start.1 = ((bf16[4,80,1280]{2,1,0:T(8,128)(2,1)}), bf16[4,80,1280]{2,1,0:T(8,128)(2,1)S(1)}, u32[]{:S(2)}, u32[]{:S(2)}) async-start(bf16[4,80,1280]{2,1,0:T(8,128)(2,1)} %broadcast_in_dim.15), calls=%async_computation.2 | async-start | bytes 1638400 | tf_op jit(solution)/shard_map/all_to_all | solution.py:98
  122.5 0.9 reduce_sum.12
  123.5 8.7 %all-to-all-done.1 = bf16[4,80,1280]{2,1,0:T(8,128)(2,1)S(1)} async-done(((bf16[4,80,1280]{2,1,0:T(8,128)(2,1)}), bf16[4,80,1280]{2,1,0:T(8,128)(2,1)S(1)}, u32[]{:S(2)}, u32[]{:S(2)}) %all-to-all-start.1) | async-done | bytes 819232 | tf_op jit(solution)/shard_map/all_to_all | solution.py:98
  132.4 0.8 slice_bitcast_fusion
  (17 shorter events, 0.8 us)
Async XLA Ops:
  7.9 14.2 %collective-permute-start = (bf16[2,1280]{1,0:T(2,128)(2,1)S(1)}, bf16[2,1280]{1,0:T(2,128)(2,1)S(1)}, u32[]{:S(2)}, u32[]{:S(2)}) collective-permute-start(bf16[2,1280]{1,0:T(2,128)(2,1)S(1)} %get-tuple-element.2), channel_id=1, source_target_pairs={{0,8},{8,16},{16,24},{24,32},{32,40},{40,48},{48,56},{56,64},{64,7... | collective-permute-start | bytes 15368 | tf_op jit(solution)/shard_map/ppermute | solution.py:12
  11.8 10.3 %collective-permute-start.1 = (bf16[2,1280]{1,0:T(2,128)(2,1)S(1)}, bf16[2,1280]{1,0:T(2,128)(2,1)S(1)}, u32[]{:S(2)}, u32[]{:S(2)}) collective-permute-start(bf16[2,1280]{1,0:T(2,128)(2,1)S(1)} %get-tuple-element.3), channel_id=1, source_target_pairs={{8,0},{16,8},{24,16},{32,24},{40,32},{48,40},{56,48},{64,56},{72,6... | collective-permute-start | bytes 15368 | tf_op jit(solution)/shard_map/ppermute | solution.py:15
  15.4 12.8 %all-to-all-start = ((bf16[8,80,192]{2,1,0:T(8,128)(2,1)}), bf16[8,80,192]{2,1,0:T(8,128)(2,1)S(1)}, u32[]{:S(2)}, u32[]{:S(2)}) async-start(bf16[8,80,192]{2,1,0:T(8,128)(2,1)} %bitcast), calls=%async_computation | async-start | bytes 655360 | tf_op jit(solution)/shard_map/all_to_all | solution.py:75
  22.1 94.4 %reduce-scatter.2.cloned.1.call-start = ((), (), s32[]{:S(2)}) async-start(), calls=%async_computation.4 | async-start | bytes 3481600 | tf_op jit(solution)/shard_map/reduce_scatter | solution.py:96
  29.1 1.4 %copy-start.1 = (bf16[1,640,1280]{2,1,0:T(8,128)(2,1)S(1)}, bf16[1,640,1280]{2,1,0:T(8,128)(2,1)}, u32[]{:S(2)}) copy-start(bf16[1,640,1280]{2,1,0:T(8,128)(2,1)} %param.3) | copy-start | bytes 4915204
  34.8 1.7 %copy-start = (bf16[192,5,1280]{2,0,1:T(8,128)(2,1)S(1)}, bf16[192,5,1280]{2,0,1:T(8,128)(2,1)}, u32[]{:S(2)}) copy-start(bf16[192,5,1280]{2,0,1:T(8,128)(2,1)} %param.4) | copy-start | bytes 7372804
  34.8 7.2 %collective-permute-start.2 = (bf16[2,192]{1,0:T(2,128)(2,1)S(1)}, bf16[2,192]{1,0:T(2,128)(2,1)S(1)}, u32[]{:S(2)}, u32[]{:S(2)}) collective-permute-start(bf16[2,192]{1,0:T(2,128)(2,1)S(1)} %get-tuple-element.4), channel_id=1, source_target_pairs={{8,0},{16,8},{24,16},{32,24},{40,32},{48,40},{56,48},{64,56},{72,6... | collective-permute-start | bytes 2312 | tf_op jit(solution)/shard_map/ppermute | solution.py:15
  37.0 6.3 %collective-permute-start.3 = (bf16[2,192]{1,0:T(2,128)(2,1)S(1)}, bf16[2,192]{1,0:T(2,128)(2,1)S(1)}, u32[]{:S(2)}, u32[]{:S(2)}) collective-permute-start(bf16[2,192]{1,0:T(2,128)(2,1)S(1)} %get-tuple-element.5), channel_id=1, source_target_pairs={{0,8},{8,16},{16,24},{24,32},{32,40},{40,48},{48,56},{56,64},{64,7... | collective-permute-start | bytes 2312 | tf_op jit(solution)/shard_map/ppermute | solution.py:12
  118.3 13.9 %all-to-all-start.1 = ((bf16[4,80,1280]{2,1,0:T(8,128)(2,1)}), bf16[4,80,1280]{2,1,0:T(8,128)(2,1)S(1)}, u32[]{:S(2)}, u32[]{:S(2)}) async-start(bf16[4,80,1280]{2,1,0:T(8,128)(2,1)} %broadcast_in_dim.15), calls=%async_computation.2 | async-start | bytes 1638400 | tf_op jit(solution)/shard_map/all_to_all | solution.py:98
Sparse Core Ops, SparseCore 0:
  34.9 81.5 reduce-scatter.1

commit v7 on v6

--- a/solution.py
+++ b/solution.py
@@ -95,9 +95,7 @@
     partial = partial.reshape(n_seq, taps_count * own_rows, in_ch)
     weight_part = lax.psum_scatter(partial, "seq", scatter_dimension=0, tiled=True)[0]
     n_dp = lax.axis_size("dp")
-    copies = lax.all_to_all(
-        jnp.broadcast_to(weight_part[None], (n_dp,) + weight_part.shape), "dp", 0, 0, tiled=True
-    ).astype(jnp.float32)
+    copies = lax.all_gather(weight_part, "dp", axis=0, tiled=False).astype(jnp.float32)
     total = copies[0]
     for j in range(1, n_dp):
         total = total + copies[j]

time: 141 us -> 139 us (0.986)
  blocking collectives: 26 us -> 39.9 us
  waiting for transfers between devices: 53.5 us -> 43.8 us
  starting transfers between devices: 22.4 us -> 18.2 us
  local copies, waits for them, and re-layouts: 9.74 us -> 7.84 us
    all_gather x0 -> x1, blocking collectives: none -> 13.9 us  [shards(): lax.all_gather(weight_part, 'dp', axis=0, tiled=False).astype(jnp.float32)]
    all_to_all x1 -> x0, waiting for transfers between devices: 8.73 us -> none  [shards(): lax.all_to_all(jnp.broadcast_to(weight_part[None], (n_dp,) + weight_part....]
    all_to_all x1 -> x0, starting transfers between devices: 4.2 us -> none  [shards(): lax.all_to_all(jnp.broadcast_to(weight_part[None], (n_dp,) + weight_part....]
    broadcast_in_dim x1 -> x0, local copies, waits for them, and re-layouts: 1.88 us -> none  [shards(): jnp.broadcast_to(weight_part[None], (n_dp,) + weight_part.shape)]
  transfers between devices with their start and end apart: 7 -> 6, of which waited for: 4 -> 3; matrix products, arithmetic and copies ran while one was open for 10% -> 10% of each run, Pallas kernels for 0% -> 0%
where the time goes in v7:
time: 139 us; the launch traced here: 138 us
  waiting for transfers between devices  43.8 us (32%)
  blocking collectives  39.9 us (29%)
  starting transfers between devices  18.2 us (13%)
  between operations  14.2 us (10%)
  matrix products  12.3 us (9%)
  local copies, waits for them, and re-layouts  7.84 us (6%)
  other arithmetic  1.85 us (1%)
    reduce_scatter x1, waiting for transfers between devices, shards(): lax.psum_scatter(partial, 'seq', scatter_dimension=0, tiled=True)[0]  41.1 us
    all_to_all x1, blocking collectives, shards(): received = lax.all_to_all(groups, 'section', 0, 0, tiled=True)  26 us
    all_gather x1, blocking collectives, shards(): lax.all_gather(weight_part, 'dp', axis=0, tiled=False).astype(jnp.float32)  13.9 us
    ppermute x2, starting transfers between devices, extended(): lax.ppermute(lax.slice_in_dim(block, block.shape[dim] - width, None, axis...  8.79 us
    all_to_all x1, starting transfers between devices, shards(): lax.all_to_all(grouped, 'section', 0, 0, tiled=True)  6.69 us
    dot_general x1, matrix products, shards(): jnp.dot(banded, padded, preferred_element_type=jnp.float32)  4.18 us
    dot_general x1, matrix products, shards(): jnp.einsum('tc,jc->tj', padded, stacked, preferred_element_type=jnp.float32)  4.11 us
    dot_general x4, matrix products, shards(): jnp.einsum('lo,oc->cl', grad_ext[4 - offset:4 - offset + length], kernel[...  3.38 us
  transfers between devices with their start and end apart: 6, of which 3 were waited for; matrix products, arithmetic and copies ran while one was open for 10% of the time, Pallas kernels for 0%

profile of v7, /device:TPU:6, one launch (start us, length us, event | category | flops | bytes accessed | tf_op | source)
XLA Modules:
  0.0 138.1 jit_solution(17063829890906662635)
XLA Ops:
  7.2 0.8 slice_bitcast_fusion.2
  7.9 3.8 %collective-permute-start = (bf16[2,1280]{1,0:T(2,128)(2,1)S(1)}, bf16[2,1280]{1,0:T(2,128)(2,1)S(1)}, u32[]{:S(2)}, u32[]{:S(2)}) collective-permute-start(bf16[2,1280]{1,0:T(2,128)(2,1)S(1)} %get-tuple-element.2), channel_id=1, source_target_pairs={{0,8},{8,16},{16,24},{24,32},{32,40},{40,48},{48,56},{56,64},{64,7... | collective-permute-start | bytes 15368 | tf_op jit(solution)/shard_map/ppermute | solution.py:12
  11.8 1.3 collective-permute-start.1
  13.1 1.1 reshape_squeeze.3
  14.2 0.2 broadcast_in_dim.6
  14.4 1.0 reshape.36
  15.4 6.7 %all-to-all-start = ((bf16[8,80,192]{2,1,0:T(8,128)(2,1)}), bf16[8,80,192]{2,1,0:T(8,128)(2,1)S(1)}, u32[]{:S(2)}, u32[]{:S(2)}) async-start(bf16[8,80,192]{2,1,0:T(8,128)(2,1)} %bitcast), calls=%async_computation | async-start | bytes 655360 | tf_op jit(solution)/shard_map/all_to_all | solution.py:75
  22.1 4.1 %fusion.4 = f32[644,960]{1,0:T(8,128)S(1)} fusion(bf16[960,1280]{1,0:T(8,128)(2,1)} %bitcast.44, bf16[2,1280]{1,0:T(2,128)(2,1)S(1)} %collective-permute-done.1, bf16[640,1280]{1,0:T(8,128)(2,1)} %bitcast.48, bf16[2,1280]{1,0:T(2,128)(2,1)S(1)} %collective-permute-done), kind=kOutput, calls=%fused_computation.9 | convolution fusion | flops 1587640320 | bytes 6579200 | tf_op jit(solution)/shard_map/tc,jc->tj/dot_general | solution.py:78
  26.2 2.0 %all-to-all-done = bf16[8,80,192]{2,1,0:T(8,128)(2,1)S(1)} async-done(((bf16[8,80,192]{2,1,0:T(8,128)(2,1)}), bf16[8,80,192]{2,1,0:T(8,128)(2,1)S(1)}, u32[]{:S(2)}, u32[]{:S(2)}) %all-to-all-start) | async-done | bytes 245792 | tf_op jit(solution)/shard_map/all_to_all | solution.py:75
  28.3 0.7 fusion.10
  29.0 0.2 copy.10
  29.3 0.2 pad_dynamic-update-slice_fusion.3
  29.5 0.2 pad_dynamic-update-slice_fusion.2
  29.7 0.2 pad_dynamic-update-slice_fusion.1
  29.8 0.2 pad_dynamic-update-slice_fusion
  30.0 0.6 copy-done.1
  30.6 4.2 %convolution_convert_fusion = bf16[1280,1280]{1,0:T(8,128)(2,1)} fusion(bf16[1280,644]{1,0:T(8,128)(2,1)S(1)} %bitcast.47, bf16[2,1280]{1,0:T(2,128)(2,1)S(1)} %collective-permute-done.1, bf16[640,1280]{1,0:T(8,128)(2,1)S(1)} %bitcast.49, bf16[2,1280]{1,0:T(2,128)(2,1)S(1)} %collective-permute-done), kind=kOutput, calls=%fused_computation | convolution fusion | flops 2116843520 | bytes 6574080 | tf_op jit(solution)/shard_map/dot_general | solution.py:94
  34.8 1.4 %collective-permute-start.2 = (bf16[2,192]{1,0:T(2,128)(2,1)S(1)}, bf16[2,192]{1,0:T(2,128)(2,1)S(1)}, u32[]{:S(2)}, u32[]{:S(2)}) collective-permute-start(bf16[2,192]{1,0:T(2,128)(2,1)S(1)} %get-tuple-element.4), channel_id=1, source_target_pairs={{8,0},{16,8},{24,16},{32,24},{40,32},{48,40},{56,48},{64,56},{72,6... | collective-permute-start | bytes 2312 | tf_op jit(solution)/shard_map/ppermute | solution.py:15
  36.2 0.2 copy-done
  36.4 0.6 fusion.14
  37.0 5.0 %collective-permute-start.3 = (bf16[2,192]{1,0:T(2,128)(2,1)S(1)}, bf16[2,192]{1,0:T(2,128)(2,1)S(1)}, u32[]{:S(2)}, u32[]{:S(2)}) collective-permute-start(bf16[2,192]{1,0:T(2,128)(2,1)S(1)} %get-tuple-element.5), channel_id=1, source_target_pairs={{0,8},{8,16},{16,24},{24,32},{32,40},{40,48},{48,56},{56,64},{64,7... | collective-permute-start | bytes 2312 | tf_op jit(solution)/shard_map/ppermute | solution.py:12
  42.0 0.6 fusion.16
  42.6 0.7 collective-permute-done.3
  43.3 0.6 fusion.11
  43.9 0.7 fusion.1
  44.6 1.6 %fusion.3 = bf16[1280,640]{0,1:T(8,128)(2,1)S(1)} fusion(f32[640,1280]{1,0:T(8,128)S(1)} %fusion.11, f32[640,1280]{1,0:T(8,128)S(1)} %fusion.1, bf16[192,5,1280]{2,0,1:T(8,128)(2,1)} %param.4, bf16[2,192]{1,0:T(2,128)(2,1)S(1)} %collective-permute-done.3, bf16[640,192]{1,0:T(8,128)(2,1)S(1)} %fusion.10), kind=kOutput, calls=%fused_computation.6 | convolution fusion | flops 317521920 | bytes 8930048 | tf_op jit(solution)/shard_map/lo,oc->cl/dot_general | solution.py:107
  46.2 2.2 %copy.11 = bf16[1280,640]{1,0:T(8,128)(2,1)} copy(bf16[1280,640]{0,1:T(8,128)(2,1)S(1)} %fusion.3) | data formatting | bytes 3276800 | tf_op jit(solution)/shard_map/add | solution.py:107
  48.4 26.0 %all_to_all.10 = bf16[8,160,640]{2,1,0:T(8,128)(2,1)S(1)} all-to-all(bf16[8,160,640]{2,1,0:T(8,128)(2,1)} %bitcast.42), channel_id=1, replica_groups=mesh['dp'=4,'seq'=16,'section'=8] {'section'}, dimensions={0} | all-to-all | bytes 3276800 | tf_op jit(solution)/shard_map/all_to_all | solution.py:114
  74.4 0.9 reduce_sum.12
  75.3 41.1 %reduce-scatter.2.cloned.1.call-done = bf16[1,80,1280]{2,1,0:T(8,128)(2,1)} async-done(((bf16[16,80,1280]{2,1,0:T(8,128)(2,1)}), bf16[1,80,1280]{2,1,0:T(8,128)(2,1)}) %reduce-scatter.2.cloned.1.call-update) | async-done | bytes 204816 | tf_op jit(solution)/shard_map/reduce_scatter | solution.py:96
  116.4 13.9 %all_gather.3 = bf16[4,80,1280]{2,1,0:T(8,128)(2,1)S(1)} all-gather(bf16[1,80,1280]{2,1,0:T(8,128)(2,1)} %reduce-scatter.2.cloned.1.call-done), channel_id=1, replica_groups=mesh['dp'=4,'seq'=16,'section'=8] {'dp'}, dimensions={0}, use_global_device_ids=true | all-gather | bytes 1024000 | tf_op jit(solution)/shard_map/all_gather | solution.py:98
  130.5 0.8 slice_bitcast_fusion
  (15 shorter events, 0.4 us)
Async XLA Ops:
  7.9 14.2 %collective-permute-start = (bf16[2,1280]{1,0:T(2,128)(2,1)S(1)}, bf16[2,1280]{1,0:T(2,128)(2,1)S(1)}, u32[]{:S(2)}, u32[]{:S(2)}) collective-permute-start(bf16[2,1280]{1,0:T(2,128)(2,1)S(1)} %get-tuple-element.2), channel_id=1, source_target_pairs={{0,8},{8,16},{16,24},{24,32},{32,40},{40,48},{48,56},{56,64},{64,7... | collective-permute-start | bytes 15368 | tf_op jit(solution)/shard_map/ppermute | solution.py:12
  11.8 10.3 %collective-permute-start.1 = (bf16[2,1280]{1,0:T(2,128)(2,1)S(1)}, bf16[2,1280]{1,0:T(2,128)(2,1)S(1)}, u32[]{:S(2)}, u32[]{:S(2)}) collective-permute-start(bf16[2,1280]{1,0:T(2,128)(2,1)S(1)} %get-tuple-element.3), channel_id=1, source_target_pairs={{8,0},{16,8},{24,16},{32,24},{40,32},{48,40},{56,48},{64,56},{72,6... | collective-permute-start | bytes 15368 | tf_op jit(solution)/shard_map/ppermute | solution.py:15
  15.4 12.8 %all-to-all-start = ((bf16[8,80,192]{2,1,0:T(8,128)(2,1)}), bf16[8,80,192]{2,1,0:T(8,128)(2,1)S(1)}, u32[]{:S(2)}, u32[]{:S(2)}) async-start(bf16[8,80,192]{2,1,0:T(8,128)(2,1)} %bitcast), calls=%async_computation | async-start | bytes 655360 | tf_op jit(solution)/shard_map/all_to_all | solution.py:75
  22.1 94.3 %reduce-scatter.2.cloned.1.call-start = ((), (), s32[]{:S(2)}) async-start(), calls=%async_computation.3 | async-start | bytes 3481600 | tf_op jit(solution)/shard_map/reduce_scatter | solution.py:96
  29.1 1.4 %copy-start.1 = (bf16[1,640,1280]{2,1,0:T(8,128)(2,1)S(1)}, bf16[1,640,1280]{2,1,0:T(8,128)(2,1)}, u32[]{:S(2)}) copy-start(bf16[1,640,1280]{2,1,0:T(8,128)(2,1)} %param.3) | copy-start | bytes 4915204
  34.8 1.7 %copy-start = (bf16[192,5,1280]{2,0,1:T(8,128)(2,1)S(1)}, bf16[192,5,1280]{2,0,1:T(8,128)(2,1)}, u32[]{:S(2)}) copy-start(bf16[192,5,1280]{2,0,1:T(8,128)(2,1)} %param.4) | copy-start | bytes 7372804
  34.8 7.2 %collective-permute-start.2 = (bf16[2,192]{1,0:T(2,128)(2,1)S(1)}, bf16[2,192]{1,0:T(2,128)(2,1)S(1)}, u32[]{:S(2)}, u32[]{:S(2)}) collective-permute-start(bf16[2,192]{1,0:T(2,128)(2,1)S(1)} %get-tuple-element.4), channel_id=1, source_target_pairs={{8,0},{16,8},{24,16},{32,24},{40,32},{48,40},{56,48},{64,56},{72,6... | collective-permute-start | bytes 2312 | tf_op jit(solution)/shard_map/ppermute | solution.py:15
  37.0 6.3 %collective-permute-start.3 = (bf16[2,192]{1,0:T(2,128)(2,1)S(1)}, bf16[2,192]{1,0:T(2,128)(2,1)S(1)}, u32[]{:S(2)}, u32[]{:S(2)}) collective-permute-start(bf16[2,192]{1,0:T(2,128)(2,1)S(1)} %get-tuple-element.5), channel_id=1, source_target_pairs={{0,8},{8,16},{16,24},{24,32},{32,40},{40,48},{48,56},{56,64},{64,7... | collective-permute-start | bytes 2312 | tf_op jit(solution)/shard_map/ppermute | solution.py:12
Sparse Core Ops, SparseCore 0:
  34.9 81.4 reduce-scatter.1

commit v8 on v7

--- a/solution.py
+++ b/solution.py
@@ -85,21 +85,21 @@
     grad_middle = grad_ext[2 : 2 + length]
     n_seq = lax.axis_size("seq")
     own = out_ch // n_seq
-    own_rows = -(-own // 16) * 16
-    spread = jnp.pad(grad_middle.T.reshape(n_seq, own, length), ((0, 0), (0, own_rows - own), (0, 0)))
-    banded = jnp.concatenate(
-        [jnp.pad(spread, ((0, 0), (0, 0), (k, taps_count - 1 - k))) for k in range(taps_count)],
-        axis=1,
-    ).reshape(n_seq * taps_count * own_rows, length + taps_count - 1)
+    chunk = own * taps_count
+    chunk_rows = -(-chunk // 16) * 16
+    spread = grad_middle.T.reshape(n_seq, own, length)
+    blocks = [jnp.pad(spread, ((0, 0), (0, 0), (k, taps_count - 1 - k))) for k in range(taps_count)]
+    blocks.append(jnp.zeros((n_seq, chunk_rows - chunk, length + taps_count - 1), spread.dtype))
+    banded = jnp.concatenate(blocks, axis=1).reshape(n_seq * chunk_rows, length + taps_count - 1)
     partial = jnp.dot(banded, padded, preferred_element_type=jnp.float32).astype(jnp.bfloat16)
-    partial = partial.reshape(n_seq, taps_count * own_rows, in_ch)
+    partial = partial.reshape(n_seq, chunk_rows, in_ch)
     weight_part = lax.psum_scatter(partial, "seq", scatter_dimension=0, tiled=True)[0]
     n_dp = lax.axis_size("dp")
     copies = lax.all_gather(weight_part, "dp", axis=0, tiled=False).astype(jnp.float32)
     total = copies[0]
     for j in range(1, n_dp):
         total = total + copies[j]
-    weight_grad = total.reshape(taps_count, own_rows, in_ch)[:, :own].transpose(1, 0, 2)
+    weight_grad = total[:chunk].reshape(taps_count, own, in_ch).transpose(1, 0, 2)
     summed = jnp.einsum(
         "lo,oc->cl", grad_ext[4 : 4 + length], kernel[:, 0, :], preferred_element_type=jnp.float32
     )

time: 139 us -> 142 us (1.022)
  local copies, waits for them, and re-layouts: 7.84 us -> 13.4 us
  waiting for transfers between devices: 43.8 us -> 40.8 us
    concatenate x1, local copies, waits for them, and re-layouts: 0.17 us -> 4.84 us  [shards(): jnp.concatenate(blocks, axis=1)]
    reduce_scatter x1, waiting for transfers between devices: 41.1 us -> 38 us  [shards(): lax.psum_scatter(partial, 'seq', scatter_dimension=0, tiled=True)[0]]
where the time goes in v8:
time: 142 us; the launch traced here: 141 us
  waiting for transfers between devices  40.8 us (29%)
  blocking collectives  39.8 us (28%)
  starting transfers between devices  18.2 us (13%)
  between operations  14.2 us (10%)
  local copies, waits for them, and re-layouts  13.4 us (9%)
  matrix products  13.3 us (9%)
  other arithmetic  1.71 us (1%)
    reduce_scatter x1, waiting for transfers between devices, shards(): lax.psum_scatter(partial, 'seq', scatter_dimension=0, tiled=True)[0]  38 us
    all_to_all x1, blocking collectives, shards(): received = lax.all_to_all(groups, 'section', 0, 0, tiled=True)  26 us
    all_gather x1, blocking collectives, shards(): lax.all_gather(weight_part, 'dp', axis=0, tiled=False).astype(jnp.float32)  13.8 us
    ppermute x2, starting transfers between devices, extended(): lax.ppermute(lax.slice_in_dim(block, block.shape[dim] - width, None, axis...  8.79 us
    all_to_all x1, starting transfers between devices, shards(): lax.all_to_all(grouped, 'section', 0, 0, tiled=True)  6.69 us
    dot_general x1, matrix products, shards(): jnp.dot(banded, padded, preferred_element_type=jnp.float32)  5.19 us
    concatenate x1, local copies, waits for them, and re-layouts, shards(): jnp.concatenate(blocks, axis=1)  4.84 us
    dot_general x1, matrix products, shards(): jnp.einsum('tc,jc->tj', padded, stacked, preferred_element_type=jnp.float32)  4.11 us
  transfers between devices with their start and end apart: 6, of which 3 were waited for; matrix products, arithmetic and copies ran while one was open for 10% of the time, Pallas kernels for 0%

profile of v8, /device:TPU:6, one launch (start us, length us, event | category | flops | bytes accessed | tf_op | source)
XLA Modules:
  0.0 141.4 jit_solution(3836949625123367771)
XLA Ops:
  7.2 0.8 slice_bitcast_fusion.1
  7.9 3.8 %collective-permute-start = (bf16[2,1280]{1,0:T(2,128)(2,1)S(1)}, bf16[2,1280]{1,0:T(2,128)(2,1)S(1)}, u32[]{:S(2)}, u32[]{:S(2)}) collective-permute-start(bf16[2,1280]{1,0:T(2,128)(2,1)S(1)} %get-tuple-element.2), channel_id=1, source_target_pairs={{0,8},{8,16},{16,24},{24,32},{32,40},{40,48},{48,56},{56,64},{64,7... | collective-permute-start | bytes 15368 | tf_op jit(solution)/shard_map/ppermute | solution.py:12
  11.8 1.3 collective-permute-start.1
  13.1 1.1 reshape_squeeze.3
  14.2 0.2 broadcast_in_dim.9
  14.4 1.0 reshape.36
  15.4 6.7 %all-to-all-start = ((bf16[8,80,192]{2,1,0:T(8,128)(2,1)}), bf16[8,80,192]{2,1,0:T(8,128)(2,1)S(1)}, u32[]{:S(2)}, u32[]{:S(2)}) async-start(bf16[8,80,192]{2,1,0:T(8,128)(2,1)} %bitcast), calls=%async_computation | async-start | bytes 655360 | tf_op jit(solution)/shard_map/all_to_all | solution.py:75
  22.1 4.1 %fusion.4 = f32[644,960]{1,0:T(8,128)S(1)} fusion(bf16[960,1280]{1,0:T(8,128)(2,1)} %bitcast.42, bf16[2,1280]{1,0:T(2,128)(2,1)S(1)} %collective-permute-done.1, bf16[640,1280]{1,0:T(8,128)(2,1)} %bitcast.46, bf16[2,1280]{1,0:T(2,128)(2,1)S(1)} %collective-permute-done), kind=kOutput, calls=%fused_computation.9 | convolution fusion | flops 1587640320 | bytes 6579200 | tf_op jit(solution)/shard_map/tc,jc->tj/dot_general | solution.py:78
  26.2 2.0 %all-to-all-done = bf16[8,80,192]{2,1,0:T(8,128)(2,1)S(1)} async-done(((bf16[8,80,192]{2,1,0:T(8,128)(2,1)}), bf16[8,80,192]{2,1,0:T(8,128)(2,1)S(1)}, u32[]{:S(2)}, u32[]{:S(2)}) %all-to-all-start) | async-done | bytes 245792 | tf_op jit(solution)/shard_map/all_to_all | solution.py:75
  28.3 0.7 fusion.10
  29.0 0.2 copy.10
  29.2 1.3 fusion.38
  30.5 0.7 broadcast_in_dim.10
  31.2 4.8 %concatenate.16 = bf16[16,64,644]{2,1,0:T(8,128)(2,1)S(1)} concatenate(bf16[16,12,644]{2,1,0:T(8,128)(2,1)} %get-tuple-element.14, bf16[16,12,644]{2,1,0:T(8,128)(2,1)S(1)} %get-tuple-element.13, bf16[16,12,644]{2,1,0:T(8,128)(2,1)S(1)} %get-tuple-element.12, bf16[16,12,644]{2,1,0:T(8,128)(2,1)S(1)} %get-tuple-element.11, bf16[16,12,644]{2,1,0:T(8,128)(2,1)S(1)} %get-tuple-element.10, ...), dimensions={1} | concatenate | bytes 2637824 | tf_op jit(solution)/shard_map/concatenate | solution.py:93
  36.0 5.2 %convolution_convert_fusion = bf16[1024,1280]{1,0:T(8,128)(2,1)} fusion(bf16[1024,644]{1,0:T(8,128)(2,1)S(1)} %bitcast.43, bf16[2,1280]{1,0:T(2,128)(2,1)S(1)} %collective-permute-done.1, bf16[640,1280]{1,0:T(8,128)(2,1)} %bitcast.47, bf16[2,1280]{1,0:T(2,128)(2,1)S(1)} %collective-permute-done), kind=kOutput, calls=%fused_computation | convolution fusion | flops 1694464000 | bytes 5588992 | tf_op jit(solution)/shard_map/dot_general | solution.py:94
  41.2 1.4 %collective-permute-start.2 = (bf16[2,192]{1,0:T(2,128)(2,1)S(1)}, bf16[2,192]{1,0:T(2,128)(2,1)S(1)}, u32[]{:S(2)}, u32[]{:S(2)}) collective-permute-start(bf16[2,192]{1,0:T(2,128)(2,1)S(1)} %get-tuple-element.8), channel_id=1, source_target_pairs={{8,0},{16,8},{24,16},{32,24},{40,32},{48,40},{56,48},{64,56},{72,6... | collective-permute-start | bytes 2312 | tf_op jit(solution)/shard_map/ppermute | solution.py:15
  42.7 0.2 copy-done
  42.9 0.6 fusion.14
  43.5 5.0 %collective-permute-start.3 = (bf16[2,192]{1,0:T(2,128)(2,1)S(1)}, bf16[2,192]{1,0:T(2,128)(2,1)S(1)}, u32[]{:S(2)}, u32[]{:S(2)}) collective-permute-start(bf16[2,192]{1,0:T(2,128)(2,1)S(1)} %get-tuple-element.9), channel_id=1, source_target_pairs={{0,8},{8,16},{16,24},{24,32},{32,40},{40,48},{48,56},{56,64},{64,7... | collective-permute-start | bytes 2312 | tf_op jit(solution)/shard_map/ppermute | solution.py:12
  48.5 0.6 fusion.16
  49.0 0.7 collective-permute-done.3
  49.7 0.6 fusion.11
  50.3 0.6 fusion.1
  50.9 1.7 %fusion.3 = bf16[1280,640]{0,1:T(8,128)(2,1)S(1)} fusion(f32[640,1280]{1,0:T(8,128)S(1)} %fusion.11, f32[640,1280]{1,0:T(8,128)S(1)} %fusion.1, bf16[192,5,1280]{2,0,1:T(8,128)(2,1)} %param.4, bf16[2,192]{1,0:T(2,128)(2,1)S(1)} %collective-permute-done.3, bf16[640,192]{1,0:T(8,128)(2,1)S(1)} %fusion.10), kind=kOutput, calls=%fused_computation.6 | convolution fusion | flops 317521920 | bytes 8930048 | tf_op jit(solution)/shard_map/lo,oc->cl/dot_general | solution.py:107
  52.6 2.2 %copy.11 = bf16[1280,640]{1,0:T(8,128)(2,1)} copy(bf16[1280,640]{0,1:T(8,128)(2,1)S(1)} %fusion.3) | data formatting | bytes 3276800 | tf_op jit(solution)/shard_map/add | solution.py:107
  54.8 26.0 %all_to_all.10 = bf16[8,160,640]{2,1,0:T(8,128)(2,1)S(1)} all-to-all(bf16[8,160,640]{2,1,0:T(8,128)(2,1)} %bitcast.40), channel_id=1, replica_groups=mesh['dp'=4,'seq'=16,'section'=8] {'section'}, dimensions={0} | all-to-all | bytes 3276800 | tf_op jit(solution)/shard_map/all_to_all | solution.py:114
  80.8 0.9 reduce_sum.12
  81.7 38.0 %reduce-scatter.2.cloned.1.call-done = bf16[1,64,1280]{2,1,0:T(8,128)(2,1)} async-done(((bf16[16,64,1280]{2,1,0:T(8,128)(2,1)}), bf16[1,64,1280]{2,1,0:T(8,128)(2,1)}) %reduce-scatter.2.cloned.1.call-update) | async-done | bytes 163856 | tf_op jit(solution)/shard_map/reduce_scatter | solution.py:96
  119.8 13.8 %all_gather.3 = bf16[4,64,1280]{2,1,0:T(8,128)(2,1)S(1)} all-gather(bf16[1,64,1280]{2,1,0:T(8,128)(2,1)} %reduce-scatter.2.cloned.1.call-done), channel_id=1, replica_groups=mesh['dp'=4,'seq'=16,'section'=8] {'dp'}, dimensions={0}, use_global_device_ids=true | all-gather | bytes 819200 | tf_op jit(solution)/shard_map/all_gather | solution.py:98
  133.6 0.1 fusion.36
  133.7 0.1 slice_add_fusion.4
  133.7 0.8 reshape.41
  (10 shorter events, 0.2 us)
Async XLA Ops:
  7.9 14.2 %collective-permute-start = (bf16[2,1280]{1,0:T(2,128)(2,1)S(1)}, bf16[2,1280]{1,0:T(2,128)(2,1)S(1)}, u32[]{:S(2)}, u32[]{:S(2)}) collective-permute-start(bf16[2,1280]{1,0:T(2,128)(2,1)S(1)} %get-tuple-element.2), channel_id=1, source_target_pairs={{0,8},{8,16},{16,24},{24,32},{32,40},{40,48},{48,56},{56,64},{64,7... | collective-permute-start | bytes 15368 | tf_op jit(solution)/shard_map/ppermute | solution.py:12
  11.8 10.3 %collective-permute-start.1 = (bf16[2,1280]{1,0:T(2,128)(2,1)S(1)}, bf16[2,1280]{1,0:T(2,128)(2,1)S(1)}, u32[]{:S(2)}, u32[]{:S(2)}) collective-permute-start(bf16[2,1280]{1,0:T(2,128)(2,1)S(1)} %get-tuple-element.3), channel_id=1, source_target_pairs={{8,0},{16,8},{24,16},{32,24},{40,32},{48,40},{56,48},{64,56},{72,6... | collective-permute-start | bytes 15368 | tf_op jit(solution)/shard_map/ppermute | solution.py:15
  15.4 12.8 %all-to-all-start = ((bf16[8,80,192]{2,1,0:T(8,128)(2,1)}), bf16[8,80,192]{2,1,0:T(8,128)(2,1)S(1)}, u32[]{:S(2)}, u32[]{:S(2)}) async-start(bf16[8,80,192]{2,1,0:T(8,128)(2,1)} %bitcast), calls=%async_computation | async-start | bytes 655360 | tf_op jit(solution)/shard_map/all_to_all | solution.py:75
  22.1 97.7 %reduce-scatter.2.cloned.1.call-start = ((), (), s32[]{:S(2)}) async-start(), calls=%async_computation.3 | async-start | bytes 2785280 | tf_op jit(solution)/shard_map/reduce_scatter | solution.py:96
  41.2 1.7 %copy-start = (bf16[192,5,1280]{2,0,1:T(8,128)(2,1)S(1)}, bf16[192,5,1280]{2,0,1:T(8,128)(2,1)}, u32[]{:S(2)}) copy-start(bf16[192,5,1280]{2,0,1:T(8,128)(2,1)} %param.4) | copy-start | bytes 7372804
  41.2 7.2 %collective-permute-start.2 = (bf16[2,192]{1,0:T(2,128)(2,1)S(1)}, bf16[2,192]{1,0:T(2,128)(2,1)S(1)}, u32[]{:S(2)}, u32[]{:S(2)}) collective-permute-start(bf16[2,192]{1,0:T(2,128)(2,1)S(1)} %get-tuple-element.8), channel_id=1, source_target_pairs={{8,0},{16,8},{24,16},{32,24},{40,32},{48,40},{56,48},{64,56},{72,6... | collective-permute-start | bytes 2312 | tf_op jit(solution)/shard_map/ppermute | solution.py:15
  43.5 6.3 %collective-permute-start.3 = (bf16[2,192]{1,0:T(2,128)(2,1)S(1)}, bf16[2,192]{1,0:T(2,128)(2,1)S(1)}, u32[]{:S(2)}, u32[]{:S(2)}) collective-permute-start(bf16[2,192]{1,0:T(2,128)(2,1)S(1)} %get-tuple-element.9), channel_id=1, source_target_pairs={{0,8},{8,16},{16,24},{24,32},{32,40},{40,48},{48,56},{56,64},{64,7... | collective-permute-start | bytes 2312 | tf_op jit(solution)/shard_map/ppermute | solution.py:12
Sparse Core Ops, SparseCore 0:
  41.4 78.3 reduce-scatter.1

commit v9 on v7

--- a/solution.py
+++ b/solution.py
@@ -21,46 +21,6 @@
     normal_cdf = 0.5 * (1.0 + jax.scipy.special.erf(values * 0.7071067811865476))
     density = jnp.exp(-0.5 * values * values) * 0.3989422804014327
     return normal_cdf + values * density
-
-
-def convolve(padded, kernel, out_rows):
-    linear = jnp.einsum(
-        "lc,oc->lo", padded[0:out_rows], kernel[:, 0, :], preferred_element_type=jnp.float32
-    )
-    for offset in range(1, kernel.shape[1]):
-        linear = linear + jnp.einsum(
-            "lc,oc->lo",
-            padded[offset : offset + out_rows],
-            kernel[:, offset, :],
-            preferred_element_type=jnp.float32,
-        )
-    return linear
-
-
-def butterfly_sum(block, axis):
-    count = lax.axis_size(axis)
-    if count & (count - 1):
-        return lax.psum(block.astype(jnp.float32), axis)
-    total = block.astype(jnp.float32)
-    step = 1
-    while step < count:
-        other = lax.ppermute(block if step == 1 else total, axis, [(i, i ^ step) for i in range(count)])
-        total = total + other.astype(jnp.float32)
-        step *= 2
-    return total
-
-
-def symmetric_sum(block, axis):
-    count = lax.axis_size(axis)
-    if count & (count - 1):
-        return lax.psum(block.astype(jnp.float32), axis)
-    parts = [block] + [
-        lax.ppermute(block, axis, [(i, i ^ step) for i in range(count)]) for step in range(1, count)
-    ]
-    parts = [part.astype(jnp.float32) for part in parts]
-    while len(parts) > 1:
-        parts = [parts[i] + parts[i + 1] for i in range(0, len(parts), 2)]
-    return parts[0]
 
 
 def shards(signal, kernel, trunk_grad):

time: 139 us -> 139 us (level)
  no operation moved by 1% of the time
where the time goes in v9:
time: 139 us; the launch traced here: 138 us
  waiting for transfers between devices  43.8 us (32%)
  blocking collectives  39.9 us (29%)
  starting transfers between devices  18.2 us (13%)
  between operations  14.2 us (10%)
  matrix products  12.3 us (9%)
  local copies, waits for them, and re-layouts  7.84 us (6%)
  other arithmetic  1.85 us (1%)
    reduce_scatter x1, waiting for transfers between devices, shards(): lax.psum_scatter(partial, 'seq', scatter_dimension=0, tiled=True)[0]  41.1 us
    all_to_all x1, blocking collectives, shards(): received = lax.all_to_all(groups, 'section', 0, 0, tiled=True)  26 us
    all_gather x1, blocking collectives, shards(): lax.all_gather(weight_part, 'dp', axis=0, tiled=False).astype(jnp.float32)  13.9 us
    ppermute x2, starting transfers between devices, extended(): lax.ppermute(lax.slice_in_dim(block, block.shape[dim] - width, None, axis...  8.79 us
    all_to_all x1, starting transfers between devices, shards(): lax.all_to_all(grouped, 'section', 0, 0, tiled=True)  6.69 us
    dot_general x1, matrix products, shards(): jnp.dot(banded, padded, preferred_element_type=jnp.float32)  4.18 us
    dot_general x1, matrix products, shards(): jnp.einsum('tc,jc->tj', padded, stacked, preferred_element_type=jnp.float32)  4.11 us
    dot_general x4, matrix products, shards(): jnp.einsum('lo,oc->cl', grad_ext[4 - offset:4 - offset + length], kernel[...  3.38 us
  transfers between devices with their start and end apart: 6, of which 3 were waited for; matrix products, arithmetic and copies ran while one was open for 10% of the time, Pallas kernels for 0%

profile of v9, /device:TPU:6, one launch (start us, length us, event | category | flops | bytes accessed | tf_op | source)
XLA Modules:
  0.0 138.1 jit_solution(17063829890906662635)
XLA Ops:
  7.2 0.8 slice_bitcast_fusion.2
  7.9 3.8 %collective-permute-start = (bf16[2,1280]{1,0:T(2,128)(2,1)S(1)}, bf16[2,1280]{1,0:T(2,128)(2,1)S(1)}, u32[]{:S(2)}, u32[]{:S(2)}) collective-permute-start(bf16[2,1280]{1,0:T(2,128)(2,1)S(1)} %get-tuple-element.2), channel_id=1, source_target_pairs={{0,8},{8,16},{16,24},{24,32},{32,40},{40,48},{48,56},{56,64},{64,7... | collective-permute-start | bytes 15368 | tf_op jit(solution)/shard_map/ppermute | solution.py:12
  11.8 1.3 collective-permute-start.1
  13.1 1.1 reshape_squeeze.3
  14.2 0.2 broadcast_in_dim.6
  14.4 1.0 reshape.36
  15.4 6.7 %all-to-all-start = ((bf16[8,80,192]{2,1,0:T(8,128)(2,1)}), bf16[8,80,192]{2,1,0:T(8,128)(2,1)S(1)}, u32[]{:S(2)}, u32[]{:S(2)}) async-start(bf16[8,80,192]{2,1,0:T(8,128)(2,1)} %bitcast), calls=%async_computation | async-start | bytes 655360 | tf_op jit(solution)/shard_map/all_to_all | solution.py:35
  22.1 4.1 %fusion.4 = f32[644,960]{1,0:T(8,128)S(1)} fusion(bf16[960,1280]{1,0:T(8,128)(2,1)} %bitcast.44, bf16[2,1280]{1,0:T(2,128)(2,1)S(1)} %collective-permute-done.1, bf16[640,1280]{1,0:T(8,128)(2,1)} %bitcast.48, bf16[2,1280]{1,0:T(2,128)(2,1)S(1)} %collective-permute-done), kind=kOutput, calls=%fused_computation.9 | convolution fusion | flops 1587640320 | bytes 6579200 | tf_op jit(solution)/shard_map/tc,jc->tj/dot_general | solution.py:38
  26.2 2.0 %all-to-all-done = bf16[8,80,192]{2,1,0:T(8,128)(2,1)S(1)} async-done(((bf16[8,80,192]{2,1,0:T(8,128)(2,1)}), bf16[8,80,192]{2,1,0:T(8,128)(2,1)S(1)}, u32[]{:S(2)}, u32[]{:S(2)}) %all-to-all-start) | async-done | bytes 245792 | tf_op jit(solution)/shard_map/all_to_all | solution.py:35
  28.3 0.7 fusion.10
  29.0 0.2 copy.10
  29.3 0.2 pad_dynamic-update-slice_fusion.3
  29.5 0.2 pad_dynamic-update-slice_fusion.2
  29.7 0.2 pad_dynamic-update-slice_fusion.1
  29.8 0.2 pad_dynamic-update-slice_fusion
  30.0 0.6 copy-done.1
  30.6 4.2 %convolution_convert_fusion = bf16[1280,1280]{1,0:T(8,128)(2,1)} fusion(bf16[1280,644]{1,0:T(8,128)(2,1)S(1)} %bitcast.47, bf16[2,1280]{1,0:T(2,128)(2,1)S(1)} %collective-permute-done.1, bf16[640,1280]{1,0:T(8,128)(2,1)S(1)} %bitcast.49, bf16[2,1280]{1,0:T(2,128)(2,1)S(1)} %collective-permute-done), kind=kOutput, calls=%fused_computation | convolution fusion | flops 2116843520 | bytes 6574080 | tf_op jit(solution)/shard_map/dot_general | solution.py:54
  34.8 1.4 %collective-permute-start.2 = (bf16[2,192]{1,0:T(2,128)(2,1)S(1)}, bf16[2,192]{1,0:T(2,128)(2,1)S(1)}, u32[]{:S(2)}, u32[]{:S(2)}) collective-permute-start(bf16[2,192]{1,0:T(2,128)(2,1)S(1)} %get-tuple-element.4), channel_id=1, source_target_pairs={{8,0},{16,8},{24,16},{32,24},{40,32},{48,40},{56,48},{64,56},{72,6... | collective-permute-start | bytes 2312 | tf_op jit(solution)/shard_map/ppermute | solution.py:15
  36.2 0.2 copy-done
  36.4 0.6 fusion.14
  37.0 5.0 %collective-permute-start.3 = (bf16[2,192]{1,0:T(2,128)(2,1)S(1)}, bf16[2,192]{1,0:T(2,128)(2,1)S(1)}, u32[]{:S(2)}, u32[]{:S(2)}) collective-permute-start(bf16[2,192]{1,0:T(2,128)(2,1)S(1)} %get-tuple-element.5), channel_id=1, source_target_pairs={{0,8},{8,16},{16,24},{24,32},{32,40},{40,48},{48,56},{56,64},{64,7... | collective-permute-start | bytes 2312 | tf_op jit(solution)/shard_map/ppermute | solution.py:12
  42.0 0.6 fusion.16
  42.6 0.7 collective-permute-done.3
  43.3 0.6 fusion.11
  43.9 0.7 fusion.1
  44.6 1.6 %fusion.3 = bf16[1280,640]{0,1:T(8,128)(2,1)S(1)} fusion(f32[640,1280]{1,0:T(8,128)S(1)} %fusion.11, f32[640,1280]{1,0:T(8,128)S(1)} %fusion.1, bf16[192,5,1280]{2,0,1:T(8,128)(2,1)} %param.4, bf16[2,192]{1,0:T(2,128)(2,1)S(1)} %collective-permute-done.3, bf16[640,192]{1,0:T(8,128)(2,1)S(1)} %fusion.10), kind=kOutput, calls=%fused_computation.6 | convolution fusion | flops 317521920 | bytes 8930048 | tf_op jit(solution)/shard_map/lo,oc->cl/dot_general | solution.py:67
  46.2 2.2 %copy.11 = bf16[1280,640]{1,0:T(8,128)(2,1)} copy(bf16[1280,640]{0,1:T(8,128)(2,1)S(1)} %fusion.3) | data formatting | bytes 3276800 | tf_op jit(solution)/shard_map/add | solution.py:67
  48.4 26.0 %all_to_all.10 = bf16[8,160,640]{2,1,0:T(8,128)(2,1)S(1)} all-to-all(bf16[8,160,640]{2,1,0:T(8,128)(2,1)} %bitcast.42), channel_id=1, replica_groups=mesh['dp'=4,'seq'=16,'section'=8] {'section'}, dimensions={0} | all-to-all | bytes 3276800 | tf_op jit(solution)/shard_map/all_to_all | solution.py:74
  74.4 0.9 reduce_sum.12
  75.3 41.1 %reduce-scatter.2.cloned.1.call-done = bf16[1,80,1280]{2,1,0:T(8,128)(2,1)} async-done(((bf16[16,80,1280]{2,1,0:T(8,128)(2,1)}), bf16[1,80,1280]{2,1,0:T(8,128)(2,1)}) %reduce-scatter.2.cloned.1.call-update) | async-done | bytes 204816 | tf_op jit(solution)/shard_map/reduce_scatter | solution.py:56
  116.4 13.9 %all_gather.3 = bf16[4,80,1280]{2,1,0:T(8,128)(2,1)S(1)} all-gather(bf16[1,80,1280]{2,1,0:T(8,128)(2,1)} %reduce-scatter.2.cloned.1.call-done), channel_id=1, replica_groups=mesh['dp'=4,'seq'=16,'section'=8] {'dp'}, dimensions={0}, use_global_device_ids=true | all-gather | bytes 1024000 | tf_op jit(solution)/shard_map/all_gather | solution.py:58
  130.5 0.8 slice_bitcast_fusion
  (15 shorter events, 0.4 us)
Async XLA Ops:
  7.9 14.2 %collective-permute-start = (bf16[2,1280]{1,0:T(2,128)(2,1)S(1)}, bf16[2,1280]{1,0:T(2,128)(2,1)S(1)}, u32[]{:S(2)}, u32[]{:S(2)}) collective-permute-start(bf16[2,1280]{1,0:T(2,128)(2,1)S(1)} %get-tuple-element.2), channel_id=1, source_target_pairs={{0,8},{8,16},{16,24},{24,32},{32,40},{40,48},{48,56},{56,64},{64,7... | collective-permute-start | bytes 15368 | tf_op jit(solution)/shard_map/ppermute | solution.py:12
  11.8 10.3 %collective-permute-start.1 = (bf16[2,1280]{1,0:T(2,128)(2,1)S(1)}, bf16[2,1280]{1,0:T(2,128)(2,1)S(1)}, u32[]{:S(2)}, u32[]{:S(2)}) collective-permute-start(bf16[2,1280]{1,0:T(2,128)(2,1)S(1)} %get-tuple-element.3), channel_id=1, source_target_pairs={{8,0},{16,8},{24,16},{32,24},{40,32},{48,40},{56,48},{64,56},{72,6... | collective-permute-start | bytes 15368 | tf_op jit(solution)/shard_map/ppermute | solution.py:15
  15.4 12.8 %all-to-all-start = ((bf16[8,80,192]{2,1,0:T(8,128)(2,1)}), bf16[8,80,192]{2,1,0:T(8,128)(2,1)S(1)}, u32[]{:S(2)}, u32[]{:S(2)}) async-start(bf16[8,80,192]{2,1,0:T(8,128)(2,1)} %bitcast), calls=%async_computation | async-start | bytes 655360 | tf_op jit(solution)/shard_map/all_to_all | solution.py:35
  22.1 94.3 %reduce-scatter.2.cloned.1.call-start = ((), (), s32[]{:S(2)}) async-start(), calls=%async_computation.3 | async-start | bytes 3481600 | tf_op jit(solution)/shard_map/reduce_scatter | solution.py:56
  29.1 1.4 %copy-start.1 = (bf16[1,640,1280]{2,1,0:T(8,128)(2,1)S(1)}, bf16[1,640,1280]{2,1,0:T(8,128)(2,1)}, u32[]{:S(2)}) copy-start(bf16[1,640,1280]{2,1,0:T(8,128)(2,1)} %param.3) | copy-start | bytes 4915204
  34.8 1.7 %copy-start = (bf16[192,5,1280]{2,0,1:T(8,128)(2,1)S(1)}, bf16[192,5,1280]{2,0,1:T(8,128)(2,1)}, u32[]{:S(2)}) copy-start(bf16[192,5,1280]{2,0,1:T(8,128)(2,1)} %param.4) | copy-start | bytes 7372804
  34.8 7.2 %collective-permute-start.2 = (bf16[2,192]{1,0:T(2,128)(2,1)S(1)}, bf16[2,192]{1,0:T(2,128)(2,1)S(1)}, u32[]{:S(2)}, u32[]{:S(2)}) collective-permute-start(bf16[2,192]{1,0:T(2,128)(2,1)S(1)} %get-tuple-element.4), channel_id=1, source_target_pairs={{8,0},{16,8},{24,16},{32,24},{40,32},{48,40},{56,48},{64,56},{72,6... | collective-permute-start | bytes 2312 | tf_op jit(solution)/shard_map/ppermute | solution.py:15
  37.0 6.3 %collective-permute-start.3 = (bf16[2,192]{1,0:T(2,128)(2,1)S(1)}, bf16[2,192]{1,0:T(2,128)(2,1)S(1)}, u32[]{:S(2)}, u32[]{:S(2)}) collective-permute-start(bf16[2,192]{1,0:T(2,128)(2,1)S(1)} %get-tuple-element.5), channel_id=1, source_target_pairs={{0,8},{8,16},{16,24},{24,32},{32,40},{40,48},{48,56},{56,64},{64,7... | collective-permute-start | bytes 2312 | tf_op jit(solution)/shard_map/ppermute | solution.py:12
Sparse Core Ops, SparseCore 0:
  34.9 81.4 reduce-scatter.1

commit v10 on v9

--- a/solution.py
+++ b/solution.py
@@ -32,7 +32,8 @@
     n_section = lax.axis_size("section")
     rows = trunk_grad.shape[1]
     grouped = jnp.repeat(trunk_grad[0].reshape(rows, n_section, out_ch), 2, axis=0).transpose(1, 0, 2)
-    upsampled = lax.all_to_all(grouped, "section", 0, 0, tiled=True).reshape(2 * rows * n_section, out_ch)
+    dense = grouped.reshape(n_section, -1, 128)
+    upsampled = lax.all_to_all(dense, "section", 0, 0, tiled=True).reshape(2 * rows * n_section, out_ch)
     padded = extended(local_signal, (("seq", 0),), 2)
     stacked = kernel.transpose(1, 0, 2).reshape(taps_count * out_ch, in_ch)
     per_tap = jnp.einsum("tc,jc->tj", padded, stacked, preferred_element_type=jnp.float32)

time: 139 us -> 140 us (level)
  no operation moved by 1% of the time
where the time goes in v10:
time: 140 us; the launch traced here: 139 us
  waiting for transfers between devices  43.1 us (31%)
  blocking collectives  39.6 us (28%)
  starting transfers between devices  18.2 us (13%)
  between operations  14.2 us (10%)
  matrix products  12.3 us (9%)
  local copies, waits for them, and re-layouts  9.22 us (7%)
  other arithmetic  2.9 us (2%)
    reduce_scatter x1, waiting for transfers between devices, shards(): lax.psum_scatter(partial, 'seq', scatter_dimension=0, tiled=True)[0]  41.2 us
    all_to_all x1, blocking collectives, shards(): received = lax.all_to_all(groups, 'section', 0, 0, tiled=True)  26 us
    all_gather x1, blocking collectives, shards(): lax.all_gather(weight_part, 'dp', axis=0, tiled=False).astype(jnp.float32)  13.6 us
    ppermute x2, starting transfers between devices, extended(): lax.ppermute(lax.slice_in_dim(block, block.shape[dim] - width, None, axis...  8.79 us
    all_to_all x1, starting transfers between devices, shards(): lax.all_to_all(dense, 'section', 0, 0, tiled=True)  6.66 us
    dot_general x1, matrix products, shards(): jnp.dot(banded, padded, preferred_element_type=jnp.float32)  4.18 us
    dot_general x1, matrix products, shards(): jnp.einsum('tc,jc->tj', padded, stacked, preferred_element_type=jnp.float32)  4.11 us
    dot_general x4, matrix products, shards(): jnp.einsum('lo,oc->cl', grad_ext[4 - offset:4 - offset + length], kernel[...  3.4 us
  transfers between devices with their start and end apart: 6, of which 3 were waited for; matrix products, arithmetic and copies ran while one was open for 10% of the time, Pallas kernels for 0%

profile of v10, /device:TPU:6, one launch (start us, length us, event | category | flops | bytes accessed | tf_op | source)
XLA Modules:
  0.0 139.5 jit_solution(7016052224853749002)
XLA Ops:
  7.2 0.8 slice_bitcast_fusion.2
  7.9 3.8 %collective-permute-start = (bf16[2,1280]{1,0:T(2,128)(2,1)S(1)}, bf16[2,1280]{1,0:T(2,128)(2,1)S(1)}, u32[]{:S(2)}, u32[]{:S(2)}) collective-permute-start(bf16[2,1280]{1,0:T(2,128)(2,1)S(1)} %get-tuple-element.2), channel_id=1, source_target_pairs={{0,8},{8,16},{16,24},{24,32},{32,40},{40,48},{48,56},{56,64},{64,7... | collective-permute-start | bytes 15368 | tf_op jit(solution)/shard_map/ppermute | solution.py:12
  11.8 1.3 collective-permute-start.1
  13.1 1.1 reshape_squeeze.3
  14.2 0.2 broadcast_in_dim.6
  14.4 0.3 reshape.39
  14.7 1.1 reshape.40
  15.8 6.7 %all-to-all-start = ((bf16[8,120,128]{2,1,0:T(8,128)(2,1)}), bf16[8,120,128]{2,1,0:T(8,128)(2,1)S(1)}, u32[]{:S(2)}, u32[]{:S(2)}) async-start(bf16[8,120,128]{2,1,0:T(8,128)(2,1)} %reshape.40), calls=%async_computation | async-start | bytes 491520 | tf_op jit(solution)/shard_map/all_to_all | solution.py:36
  22.5 4.1 %fusion.4 = f32[644,960]{1,0:T(8,128)S(1)} fusion(bf16[960,1280]{1,0:T(8,128)(2,1)} %bitcast.42, bf16[2,1280]{1,0:T(2,128)(2,1)S(1)} %collective-permute-done.1, bf16[640,1280]{1,0:T(8,128)(2,1)} %bitcast.47, bf16[2,1280]{1,0:T(2,128)(2,1)S(1)} %collective-permute-done), kind=kOutput, calls=%fused_computation.9 | convolution fusion | flops 1587640320 | bytes 6579200 | tf_op jit(solution)/shard_map/tc,jc->tj/dot_general | solution.py:39
  26.6 1.1 all-to-all-done
  27.8 1.0 mul.37
  28.8 1.7 %fusion.10 = bf16[640,192]{1,0:T(8,128)(2,1)S(1)} fusion(f32[640,192]{1,0:T(8,128)} %mul.37, f32[644,960]{1,0:T(8,128)S(1)} %fusion.4), kind=kLoop, calls=%fused_computation.15 | loop fusion | flops 1720320 | bytes 3194880 | tf_op jit(solution)/shard_map/convert_element_type | solution.py:44
  30.5 0.2 copy.10
  31.0 0.2 pad_dynamic-update-slice_fusion.2
  31.2 0.2 pad_dynamic-update-slice_fusion.1
  31.5 0.6 copy-done.1
  32.1 4.2 %convolution_convert_fusion = bf16[1280,1280]{1,0:T(8,128)(2,1)} fusion(bf16[1280,644]{1,0:T(8,128)(2,1)S(1)} %bitcast.46, bf16[2,1280]{1,0:T(2,128)(2,1)S(1)} %collective-permute-done.1, bf16[640,1280]{1,0:T(8,128)(2,1)S(1)} %bitcast.48, bf16[2,1280]{1,0:T(2,128)(2,1)S(1)} %collective-permute-done), kind=kOutput, calls=%fused_computation | convolution fusion | flops 2116843520 | bytes 6574080 | tf_op jit(solution)/shard_map/dot_general | solution.py:55
  36.3 1.4 %collective-permute-start.2 = (bf16[2,192]{1,0:T(2,128)(2,1)S(1)}, bf16[2,192]{1,0:T(2,128)(2,1)S(1)}, u32[]{:S(2)}, u32[]{:S(2)}) collective-permute-start(bf16[2,192]{1,0:T(2,128)(2,1)S(1)} %get-tuple-element.4), channel_id=1, source_target_pairs={{8,0},{16,8},{24,16},{32,24},{40,32},{48,40},{56,48},{64,56},{72,6... | collective-permute-start | bytes 2312 | tf_op jit(solution)/shard_map/ppermute | solution.py:15
  37.8 0.2 copy-done
  38.0 0.6 fusion.14
  38.6 5.0 %collective-permute-start.3 = (bf16[2,192]{1,0:T(2,128)(2,1)S(1)}, bf16[2,192]{1,0:T(2,128)(2,1)S(1)}, u32[]{:S(2)}, u32[]{:S(2)}) collective-permute-start(bf16[2,192]{1,0:T(2,128)(2,1)S(1)} %get-tuple-element.5), channel_id=1, source_target_pairs={{0,8},{8,16},{16,24},{24,32},{32,40},{40,48},{48,56},{56,64},{64,7... | collective-permute-start | bytes 2312 | tf_op jit(solution)/shard_map/ppermute | solution.py:12
  43.5 0.6 fusion.16
  44.1 0.7 collective-permute-done.3
  44.8 0.6 fusion.11
  45.4 0.6 fusion.1
  46.0 1.7 %fusion.3 = bf16[1280,640]{0,1:T(8,128)(2,1)S(1)} fusion(f32[640,1280]{1,0:T(8,128)S(1)} %fusion.11, f32[640,1280]{1,0:T(8,128)S(1)} %fusion.1, bf16[192,5,1280]{2,0,1:T(8,128)(2,1)} %param.4, bf16[2,192]{1,0:T(2,128)(2,1)S(1)} %collective-permute-done.3, bf16[640,192]{1,0:T(8,128)(2,1)S(1)} %fusion.10), kind=kOutput, calls=%fused_computation.6 | convolution fusion | flops 317521920 | bytes 8930048 | tf_op jit(solution)/shard_map/lo,oc->cl/dot_general | solution.py:68
  47.7 2.2 %copy.11 = bf16[1280,640]{1,0:T(8,128)(2,1)} copy(bf16[1280,640]{0,1:T(8,128)(2,1)S(1)} %fusion.3) | data formatting | bytes 3276800 | tf_op jit(solution)/shard_map/add | solution.py:68
  49.9 26.0 %all_to_all.10 = bf16[8,160,640]{2,1,0:T(8,128)(2,1)S(1)} all-to-all(bf16[8,160,640]{2,1,0:T(8,128)(2,1)} %bitcast.40), channel_id=1, replica_groups=mesh['dp'=4,'seq'=16,'section'=8] {'section'}, dimensions={0} | all-to-all | bytes 3276800 | tf_op jit(solution)/shard_map/all_to_all | solution.py:75
  75.9 0.9 reduce_sum.12
  76.8 41.2 %reduce-scatter.2.cloned.1.call-done = bf16[1,80,1280]{2,1,0:T(8,128)(2,1)} async-done(((bf16[16,80,1280]{2,1,0:T(8,128)(2,1)}), bf16[1,80,1280]{2,1,0:T(8,128)(2,1)}) %reduce-scatter.2.cloned.1.call-update) | async-done | bytes 204816 | tf_op jit(solution)/shard_map/reduce_scatter | solution.py:57
  118.0 13.6 %all_gather.3 = bf16[4,80,1280]{2,1,0:T(8,128)(2,1)S(1)} all-gather(bf16[1,80,1280]{2,1,0:T(8,128)(2,1)} %reduce-scatter.2.cloned.1.call-done), channel_id=1, replica_groups=mesh['dp'=4,'seq'=16,'section'=8] {'dp'}, dimensions={0}, use_global_device_ids=true | all-gather | bytes 1024000 | tf_op jit(solution)/shard_map/all_gather | solution.py:59
  131.8 0.8 slice_bitcast_fusion
  (17 shorter events, 0.8 us)
Async XLA Ops:
  7.9 14.5 %collective-permute-start = (bf16[2,1280]{1,0:T(2,128)(2,1)S(1)}, bf16[2,1280]{1,0:T(2,128)(2,1)S(1)}, u32[]{:S(2)}, u32[]{:S(2)}) collective-permute-start(bf16[2,1280]{1,0:T(2,128)(2,1)S(1)} %get-tuple-element.2), channel_id=1, source_target_pairs={{0,8},{8,16},{16,24},{24,32},{32,40},{40,48},{48,56},{56,64},{64,7... | collective-permute-start | bytes 15368 | tf_op jit(solution)/shard_map/ppermute | solution.py:12
  11.8 10.7 %collective-permute-start.1 = (bf16[2,1280]{1,0:T(2,128)(2,1)S(1)}, bf16[2,1280]{1,0:T(2,128)(2,1)S(1)}, u32[]{:S(2)}, u32[]{:S(2)}) collective-permute-start(bf16[2,1280]{1,0:T(2,128)(2,1)S(1)} %get-tuple-element.3), channel_id=1, source_target_pairs={{8,0},{16,8},{24,16},{32,24},{40,32},{48,40},{56,48},{64,56},{72,6... | collective-permute-start | bytes 15368 | tf_op jit(solution)/shard_map/ppermute | solution.py:15
  15.8 11.9 %all-to-all-start = ((bf16[8,120,128]{2,1,0:T(8,128)(2,1)}), bf16[8,120,128]{2,1,0:T(8,128)(2,1)S(1)}, u32[]{:S(2)}, u32[]{:S(2)}) async-start(bf16[8,120,128]{2,1,0:T(8,128)(2,1)} %reshape.40), calls=%async_computation | async-start | bytes 491520 | tf_op jit(solution)/shard_map/all_to_all | solution.py:36
  22.4 95.6 %reduce-scatter.2.cloned.1.call-start = ((), (), s32[]{:S(2)}) async-start(), calls=%async_computation.3 | async-start | bytes 3481600 | tf_op jit(solution)/shard_map/reduce_scatter | solution.py:57
  30.7 1.4 %copy-start.1 = (bf16[1,640,1280]{2,1,0:T(8,128)(2,1)S(1)}, bf16[1,640,1280]{2,1,0:T(8,128)(2,1)}, u32[]{:S(2)}) copy-start(bf16[1,640,1280]{2,1,0:T(8,128)(2,1)} %param.3) | copy-start | bytes 4915204
  36.3 1.7 %copy-start = (bf16[192,5,1280]{2,0,1:T(8,128)(2,1)S(1)}, bf16[192,5,1280]{2,0,1:T(8,128)(2,1)}, u32[]{:S(2)}) copy-start(bf16[192,5,1280]{2,0,1:T(8,128)(2,1)} %param.4) | copy-start | bytes 7372804
  36.3 7.2 %collective-permute-start.2 = (bf16[2,192]{1,0:T(2,128)(2,1)S(1)}, bf16[2,192]{1,0:T(2,128)(2,1)S(1)}, u32[]{:S(2)}, u32[]{:S(2)}) collective-permute-start(bf16[2,192]{1,0:T(2,128)(2,1)S(1)} %get-tuple-element.4), channel_id=1, source_target_pairs={{8,0},{16,8},{24,16},{32,24},{40,32},{48,40},{56,48},{64,56},{72,6... | collective-permute-start | bytes 2312 | tf_op jit(solution)/shard_map/ppermute | solution.py:15
  38.6 6.3 %collective-permute-start.3 = (bf16[2,192]{1,0:T(2,128)(2,1)S(1)}, bf16[2,192]{1,0:T(2,128)(2,1)S(1)}, u32[]{:S(2)}, u32[]{:S(2)}) collective-permute-start(bf16[2,192]{1,0:T(2,128)(2,1)S(1)} %get-tuple-element.5), channel_id=1, source_target_pairs={{0,8},{8,16},{16,24},{24,32},{32,40},{40,48},{48,56},{56,64},{64,7... | collective-permute-start | bytes 2312 | tf_op jit(solution)/shard_map/ppermute | solution.py:12
Sparse Core Ops, SparseCore 0:
  36.4 81.5 reduce-scatter.1

commit v11 on v9

--- a/solution.py
+++ b/solution.py
@@ -35,18 +35,18 @@
     upsampled = lax.all_to_all(grouped, "section", 0, 0, tiled=True).reshape(2 * rows * n_section, out_ch)
     padded = extended(local_signal, (("seq", 0),), 2)
     stacked = kernel.transpose(1, 0, 2).reshape(taps_count * out_ch, in_ch)
-    per_tap = jnp.einsum("tc,jc->tj", padded, stacked, preferred_element_type=jnp.float32)
-    linear = per_tap[0:length, 0:out_ch]
+    per_tap = jnp.einsum("jc,tc->jt", stacked, padded, preferred_element_type=jnp.float32)
+    linear = per_tap[0:out_ch, 0:length]
     for k in range(1, taps_count):
-        linear = linear + per_tap[k : k + length, k * out_ch : (k + 1) * out_ch]
-    grad_hidden = 0.5 * upsampled.astype(jnp.float32)
-    grad_pre = (grad_hidden * gelu_slope(linear)).astype(jnp.bfloat16)
+        linear = linear + per_tap[k * out_ch : (k + 1) * out_ch, k : k + length]
+    grad_hidden = 0.5 * upsampled.T.astype(jnp.float32)
+    grad_flip = (grad_hidden * gelu_slope(linear)).astype(jnp.bfloat16)
+    grad_pre = grad_flip.T
     grad_ext = extended(grad_pre, (("seq", 0),), 2)
-    grad_middle = grad_ext[2 : 2 + length]
     n_seq = lax.axis_size("seq")
     own = out_ch // n_seq
     own_rows = -(-own // 16) * 16
-    spread = jnp.pad(grad_middle.T.reshape(n_seq, own, length), ((0, 0), (0, own_rows - own), (0, 0)))
+    spread = jnp.pad(grad_flip.reshape(n_seq, own, length), ((0, 0), (0, own_rows - own), (0, 0)))
     banded = jnp.concatenate(
         [jnp.pad(spread, ((0, 0), (0, 0), (k, taps_count - 1 - k))) for k in range(taps_count)],
         axis=1,

time: 139 us -> 139 us (level)
  no operation moved by 1% of the time
where the time goes in v11:
time: 139 us; the launch traced here: 138 us
  waiting for transfers between devices  43.8 us (32%)
  blocking collectives  39.9 us (29%)
  starting transfers between devices  18.2 us (13%)
  between operations  14.2 us (10%)
  matrix products  12.3 us (9%)
  local copies, waits for them, and re-layouts  7.84 us (6%)
  other arithmetic  1.85 us (1%)
    reduce_scatter x1, waiting for transfers between devices, shards(): lax.psum_scatter(partial, 'seq', scatter_dimension=0, tiled=True)[0]  41.1 us
    all_to_all x1, blocking collectives, shards(): received = lax.all_to_all(groups, 'section', 0, 0, tiled=True)  26 us
    all_gather x1, blocking collectives, shards(): lax.all_gather(weight_part, 'dp', axis=0, tiled=False).astype(jnp.float32)  13.9 us
    ppermute x2, starting transfers between devices, extended(): lax.ppermute(lax.slice_in_dim(block, block.shape[dim] - width, None, axis...  8.79 us
    all_to_all x1, starting transfers between devices, shards(): lax.all_to_all(grouped, 'section', 0, 0, tiled=True)  6.69 us
    dot_general x1, matrix products, shards(): jnp.dot(banded, padded, preferred_element_type=jnp.float32)  4.18 us
    dot_general x1, matrix products, shards(): jnp.einsum('jc,tc->jt', stacked, padded, preferred_element_type=jnp.float32)  4.11 us
    dot_general x4, matrix products, shards(): jnp.einsum('lo,oc->cl', grad_ext[4 - offset:4 - offset + length], kernel[...  3.38 us
  transfers between devices with their start and end apart: 6, of which 3 were waited for; matrix products, arithmetic and copies ran while one was open for 10% of the time, Pallas kernels for 0%

profile of v11, /device:TPU:6, one launch (start us, length us, event | category | flops | bytes accessed | tf_op | source)
XLA Modules:
  0.0 138.1 jit_solution(17063829890906662635)
XLA Ops:
  7.2 0.8 slice_bitcast_fusion.2
  7.9 3.8 %collective-permute-start = (bf16[2,1280]{1,0:T(2,128)(2,1)S(1)}, bf16[2,1280]{1,0:T(2,128)(2,1)S(1)}, u32[]{:S(2)}, u32[]{:S(2)}) collective-permute-start(bf16[2,1280]{1,0:T(2,128)(2,1)S(1)} %get-tuple-element.2), channel_id=1, source_target_pairs={{0,8},{8,16},{16,24},{24,32},{32,40},{40,48},{48,56},{56,64},{64,7... | collective-permute-start | bytes 15368 | tf_op jit(solution)/shard_map/ppermute | solution.py:12
  11.8 1.3 collective-permute-start.1
  13.1 1.1 reshape_squeeze.3
  14.2 0.2 broadcast_in_dim.6
  14.4 1.0 reshape.36
  15.4 6.7 %all-to-all-start = ((bf16[8,80,192]{2,1,0:T(8,128)(2,1)}), bf16[8,80,192]{2,1,0:T(8,128)(2,1)S(1)}, u32[]{:S(2)}, u32[]{:S(2)}) async-start(bf16[8,80,192]{2,1,0:T(8,128)(2,1)} %bitcast), calls=%async_computation | async-start | bytes 655360 | tf_op jit(solution)/shard_map/all_to_all | solution.py:35
  22.1 4.1 %convolution_bitcast_fusion = f32[960,644]{0,1:T(8,128)S(1)} fusion(bf16[960,1280]{1,0:T(8,128)(2,1)} %bitcast.52, bf16[2,1280]{1,0:T(2,128)(2,1)S(1)} %collective-permute-done.1, bf16[640,1280]{1,0:T(8,128)(2,1)} %bitcast.56, bf16[2,1280]{1,0:T(2,128)(2,1)S(1)} %collective-permute-done), kind=kOutput, calls=%fused_computation.7 | convolution fusion | flops 1587640320 | bytes 6579200 | tf_op jit(solution)/shard_map/jc,tc->jt/dot_general | solution.py:38
  26.2 2.0 %all-to-all-done = bf16[8,80,192]{2,1,0:T(8,128)(2,1)S(1)} async-done(((bf16[8,80,192]{2,1,0:T(8,128)(2,1)}), bf16[8,80,192]{2,1,0:T(8,128)(2,1)S(1)}, u32[]{:S(2)}, u32[]{:S(2)}) %all-to-all-start) | async-done | bytes 245792 | tf_op jit(solution)/shard_map/all_to_all | solution.py:35
  28.3 0.7 fusion.9
  29.0 0.2 copy.10
  29.3 0.2 pad_dynamic-update-slice_fusion.3
  29.5 0.2 pad_dynamic-update-slice_fusion.2
  29.7 0.2 pad_dynamic-update-slice_fusion.1
  29.8 0.2 pad_dynamic-update-slice_fusion
  30.0 0.6 copy-done.1
  30.6 4.2 %convolution_convert_fusion = bf16[1280,1280]{1,0:T(8,128)(2,1)} fusion(bf16[1280,644]{1,0:T(8,128)(2,1)S(1)} %bitcast.55, bf16[2,1280]{1,0:T(2,128)(2,1)S(1)} %collective-permute-done.1, bf16[640,1280]{1,0:T(8,128)(2,1)S(1)} %bitcast.57, bf16[2,1280]{1,0:T(2,128)(2,1)S(1)} %collective-permute-done), kind=kOutput, calls=%fused_computation | convolution fusion | flops 2116843520 | bytes 6574080 | tf_op jit(solution)/shard_map/dot_general | solution.py:54
  34.8 1.4 %collective-permute-start.2 = (bf16[2,192]{1,0:T(2,128)(2,1)S(1)}, bf16[2,192]{1,0:T(2,128)(2,1)S(1)}, u32[]{:S(2)}, u32[]{:S(2)}) collective-permute-start(bf16[2,192]{1,0:T(2,128)(2,1)S(1)} %get-tuple-element.4), channel_id=1, source_target_pairs={{8,0},{16,8},{24,16},{32,24},{40,32},{48,40},{56,48},{64,56},{72,6... | collective-permute-start | bytes 2312 | tf_op jit(solution)/shard_map/ppermute | solution.py:15
  36.2 0.2 copy-done
  36.4 0.6 fusion.13
  37.0 5.0 %collective-permute-start.3 = (bf16[2,192]{1,0:T(2,128)(2,1)S(1)}, bf16[2,192]{1,0:T(2,128)(2,1)S(1)}, u32[]{:S(2)}, u32[]{:S(2)}) collective-permute-start(bf16[2,192]{1,0:T(2,128)(2,1)S(1)} %get-tuple-element.5), channel_id=1, source_target_pairs={{0,8},{8,16},{16,24},{24,32},{32,40},{40,48},{48,56},{56,64},{64,7... | collective-permute-start | bytes 2312 | tf_op jit(solution)/shard_map/ppermute | solution.py:12
  42.0 0.6 fusion.15
  42.6 0.7 collective-permute-done.3
  43.3 0.6 fusion.10
  43.9 0.7 fusion.1
  44.6 1.6 %fusion.3 = bf16[1280,640]{0,1:T(8,128)(2,1)S(1)} fusion(f32[640,1280]{1,0:T(8,128)S(1)} %fusion.10, f32[640,1280]{1,0:T(8,128)S(1)} %fusion.1, bf16[192,5,1280]{2,0,1:T(8,128)(2,1)} %param.4, bf16[2,192]{1,0:T(2,128)(2,1)S(1)} %collective-permute-done.3, bf16[640,192]{1,0:T(8,128)(2,1)S(1)} %bitcast.49), kind=kOutput, calls=%fused_computation.6 | convolution fusion | flops 317521920 | bytes 8930048 | tf_op jit(solution)/shard_map/lo,oc->cl/dot_general | solution.py:67
  46.2 2.2 %copy.11 = bf16[1280,640]{1,0:T(8,128)(2,1)} copy(bf16[1280,640]{0,1:T(8,128)(2,1)S(1)} %fusion.3) | data formatting | bytes 3276800 | tf_op jit(solution)/shard_map/add | solution.py:67
  48.4 26.0 %all_to_all.10 = bf16[8,160,640]{2,1,0:T(8,128)(2,1)S(1)} all-to-all(bf16[8,160,640]{2,1,0:T(8,128)(2,1)} %bitcast.50), channel_id=1, replica_groups=mesh['dp'=4,'seq'=16,'section'=8] {'section'}, dimensions={0} | all-to-all | bytes 3276800 | tf_op jit(solution)/shard_map/all_to_all | solution.py:74
  74.4 0.9 reduce_sum.12
  75.3 41.1 %reduce-scatter.2.cloned.1.call-done = bf16[1,80,1280]{2,1,0:T(8,128)(2,1)} async-done(((bf16[16,80,1280]{2,1,0:T(8,128)(2,1)}), bf16[1,80,1280]{2,1,0:T(8,128)(2,1)}) %reduce-scatter.2.cloned.1.call-update) | async-done | bytes 204816 | tf_op jit(solution)/shard_map/reduce_scatter | solution.py:56
  116.4 13.9 %all_gather.3 = bf16[4,80,1280]{2,1,0:T(8,128)(2,1)S(1)} all-gather(bf16[1,80,1280]{2,1,0:T(8,128)(2,1)} %reduce-scatter.2.cloned.1.call-done), channel_id=1, replica_groups=mesh['dp'=4,'seq'=16,'section'=8] {'dp'}, dimensions={0}, use_global_device_ids=true | all-gather | bytes 1024000 | tf_op jit(solution)/shard_map/all_gather | solution.py:58
  130.5 0.8 slice_bitcast_fusion
  (15 shorter events, 0.4 us)
Async XLA Ops:
  7.9 14.2 %collective-permute-start = (bf16[2,1280]{1,0:T(2,128)(2,1)S(1)}, bf16[2,1280]{1,0:T(2,128)(2,1)S(1)}, u32[]{:S(2)}, u32[]{:S(2)}) collective-permute-start(bf16[2,1280]{1,0:T(2,128)(2,1)S(1)} %get-tuple-element.2), channel_id=1, source_target_pairs={{0,8},{8,16},{16,24},{24,32},{32,40},{40,48},{48,56},{56,64},{64,7... | collective-permute-start | bytes 15368 | tf_op jit(solution)/shard_map/ppermute | solution.py:12
  11.8 10.3 %collective-permute-start.1 = (bf16[2,1280]{1,0:T(2,128)(2,1)S(1)}, bf16[2,1280]{1,0:T(2,128)(2,1)S(1)}, u32[]{:S(2)}, u32[]{:S(2)}) collective-permute-start(bf16[2,1280]{1,0:T(2,128)(2,1)S(1)} %get-tuple-element.3), channel_id=1, source_target_pairs={{8,0},{16,8},{24,16},{32,24},{40,32},{48,40},{56,48},{64,56},{72,6... | collective-permute-start | bytes 15368 | tf_op jit(solution)/shard_map/ppermute | solution.py:15
  15.4 12.8 %all-to-all-start = ((bf16[8,80,192]{2,1,0:T(8,128)(2,1)}), bf16[8,80,192]{2,1,0:T(8,128)(2,1)S(1)}, u32[]{:S(2)}, u32[]{:S(2)}) async-start(bf16[8,80,192]{2,1,0:T(8,128)(2,1)} %bitcast), calls=%async_computation | async-start | bytes 655360 | tf_op jit(solution)/shard_map/all_to_all | solution.py:35
  22.1 94.3 %reduce-scatter.2.cloned.1.call-start = ((), (), s32[]{:S(2)}) async-start(), calls=%async_computation.3 | async-start | bytes 3481600 | tf_op jit(solution)/shard_map/reduce_scatter | solution.py:56
  29.1 1.4 %copy-start.1 = (bf16[1,640,1280]{2,1,0:T(8,128)(2,1)S(1)}, bf16[1,640,1280]{2,1,0:T(8,128)(2,1)}, u32[]{:S(2)}) copy-start(bf16[1,640,1280]{2,1,0:T(8,128)(2,1)} %param.3) | copy-start | bytes 4915204
  34.8 1.7 %copy-start = (bf16[192,5,1280]{2,0,1:T(8,128)(2,1)S(1)}, bf16[192,5,1280]{2,0,1:T(8,128)(2,1)}, u32[]{:S(2)}) copy-start(bf16[192,5,1280]{2,0,1:T(8,128)(2,1)} %param.4) | copy-start | bytes 7372804
  34.8 7.2 %collective-permute-start.2 = (bf16[2,192]{1,0:T(2,128)(2,1)S(1)}, bf16[2,192]{1,0:T(2,128)(2,1)S(1)}, u32[]{:S(2)}, u32[]{:S(2)}) collective-permute-start(bf16[2,192]{1,0:T(2,128)(2,1)S(1)} %get-tuple-element.4), channel_id=1, source_target_pairs={{8,0},{16,8},{24,16},{32,24},{40,32},{48,40},{56,48},{64,56},{72,6... | collective-permute-start | bytes 2312 | tf_op jit(solution)/shard_map/ppermute | solution.py:15
  37.0 6.3 %collective-permute-start.3 = (bf16[2,192]{1,0:T(2,128)(2,1)S(1)}, bf16[2,192]{1,0:T(2,128)(2,1)S(1)}, u32[]{:S(2)}, u32[]{:S(2)}) collective-permute-start(bf16[2,192]{1,0:T(2,128)(2,1)S(1)} %get-tuple-element.5), channel_id=1, source_target_pairs={{0,8},{8,16},{16,24},{24,32},{32,40},{40,48},{48,56},{56,64},{64,7... | collective-permute-start | bytes 2312 | tf_op jit(solution)/shard_map/ppermute | solution.py:12
Sparse Core Ops, SparseCore 0:
  34.9 81.4 reduce-scatter.1

commit v12 on v9

--- a/solution.py
+++ b/solution.py
@@ -33,7 +33,8 @@
     rows = trunk_grad.shape[1]
     grouped = jnp.repeat(trunk_grad[0].reshape(rows, n_section, out_ch), 2, axis=0).transpose(1, 0, 2)
     upsampled = lax.all_to_all(grouped, "section", 0, 0, tiled=True).reshape(2 * rows * n_section, out_ch)
-    padded = extended(local_signal, (("seq", 0),), 2)
+    anchor = (grouped[0, 0, 0] * 0).astype(local_signal.dtype)
+    padded = extended(local_signal + anchor, (("seq", 0),), 2)
     stacked = kernel.transpose(1, 0, 2).reshape(taps_count * out_ch, in_ch)
     per_tap = jnp.einsum("tc,jc->tj", padded, stacked, preferred_element_type=jnp.float32)
     linear = per_tap[0:length, 0:out_ch]

time: 139 us -> 139 us (level)
  matrix products: 12.3 us -> 10.1 us
  waiting for transfers between devices: 43.8 us -> 45.4 us
    ppermute x2, waiting for transfers between devices: 0.01 us -> 4.08 us  [extended(): lax.ppermute(lax.slice_in_dim(block, 0, width, axis=dim), axis, backward)]
    ppermute x2, starting transfers between devices: 8.79 us -> 5.76 us  [extended(): lax.ppermute(lax.slice_in_dim(block, block.shape[dim] - width, None, axis...]
    all_to_all x1, starting transfers between devices: 6.69 us -> 9.22 us  [shards(): lax.all_to_all(grouped, 'section', 0, 0, tiled=True)]
    dot_general x1, matrix products: 4.11 us -> 1.92 us  [shards(): jnp.einsum('tc,jc->tj', padded, stacked, preferred_element_type=jnp.float32)]
    all_to_all x1, waiting for transfers between devices: 2.02 us -> 0.01 us  [shards(): lax.all_to_all(grouped, 'section', 0, 0, tiled=True)]
  transfers between devices with their start and end apart: 6 -> 6, of which waited for: 3 -> 3; matrix products, arithmetic and copies ran while one was open for 10% -> 8% of each run, Pallas kernels for 0% -> 0%
where the time goes in v12:
time: 139 us; the launch traced here: 138 us
  waiting for transfers between devices  45.4 us (33%)
  blocking collectives  39.2 us (28%)
  starting transfers between devices  17.7 us (13%)
  between operations  14.9 us (11%)
  matrix products  10.1 us (7%)
  local copies, waits for them, and re-layouts  8.58 us (6%)
  other arithmetic  2.07 us (1%)
    reduce_scatter x1, waiting for transfers between devices, shards(): lax.psum_scatter(partial, 'seq', scatter_dimension=0, tiled=True)[0]  40.6 us
    all_to_all x1, blocking collectives, shards(): received = lax.all_to_all(groups, 'section', 0, 0, tiled=True)  25.2 us
    all_gather x1, blocking collectives, shards(): lax.all_gather(weight_part, 'dp', axis=0, tiled=False).astype(jnp.float32)  14 us
    all_to_all x1, starting transfers between devices, shards(): lax.all_to_all(grouped, 'section', 0, 0, tiled=True)  9.22 us
    ppermute x2, starting transfers between devices, extended(): lax.ppermute(lax.slice_in_dim(block, block.shape[dim] - width, None, axis...  5.76 us
    dot_general x1, matrix products, shards(): jnp.dot(banded, padded, preferred_element_type=jnp.float32)  4.16 us
    ppermute x2, waiting for transfers between devices, extended(): lax.ppermute(lax.slice_in_dim(block, 0, width, axis=dim), axis, backward)  4.08 us
    dot_general x4, matrix products, shards(): jnp.einsum('lo,oc->cl', grad_ext[4 - offset:4 - offset + length], kernel[...  3.4 us
  transfers between devices with their start and end apart: 6, of which 3 were waited for; matrix products, arithmetic and copies ran while one was open for 8% of the time, Pallas kernels for 0%

profile of v12, /device:TPU:6, one launch (start us, length us, event | category | flops | bytes accessed | tf_op | source)
XLA Modules:
  0.0 138.0 jit_solution(958501960996733346)
XLA Ops:
  7.2 1.2 reshape_squeeze.3
  8.4 0.2 broadcast_in_dim.6
  8.6 1.0 reshape.40
  9.6 9.2 %all-to-all-start = ((bf16[8,80,192]{2,1,0:T(8,128)(2,1)}), bf16[8,80,192]{2,1,0:T(8,128)(2,1)S(1)}, u32[]{:S(2)}, u32[]{:S(2)}) async-start(bf16[8,80,192]{2,1,0:T(8,128)(2,1)} %bitcast), calls=%async_computation | async-start | bytes 655360 | tf_op jit(solution)/shard_map/all_to_all | solution.py:35
  18.9 1.2 slice.108
  20.9 1.4 %collective-permute-start = (bf16[2,1280]{1,0:T(2,128)(2,1)S(1)}, bf16[2,1280]{1,0:T(2,128)(2,1)S(1)}, u32[]{:S(2)}, u32[]{:S(2)}) collective-permute-start(bf16[2,1280]{1,0:T(2,128)(2,1)S(1)} %get-tuple-element.2), channel_id=1, source_target_pairs={{0,8},{8,16},{16,24},{24,32},{32,40},{40,48},{48,56},{56,64},{64,7... | collective-permute-start | bytes 15368 | tf_op jit(solution)/shard_map/ppermute | solution.py:12
  22.3 1.3 collective-permute-start.1
  23.8 4.1 %collective-permute-done.1 = bf16[2,1280]{1,0:T(2,128)(2,1)S(1)} collective-permute-done((bf16[2,1280]{1,0:T(2,128)(2,1)S(1)}, bf16[2,1280]{1,0:T(2,128)(2,1)S(1)}, u32[]{:S(2)}, u32[]{:S(2)}) %collective-permute-start.1) | collective-permute-done | bytes 5152 | tf_op jit(solution)/shard_map/ppermute | solution.py:15
  27.9 1.9 %fusion.4 = f32[644,960]{1,0:T(8,128)S(1)} fusion(bf16[960,1280]{1,0:T(8,128)(2,1)S(1)} %bitcast.46, bf16[2,1280]{1,0:T(2,128)(2,1)S(1)} %collective-permute-done.1, bf16[640,1280]{1,0:T(8,128)(2,1)S(1)} %fusion.40, bf16[2,1280]{1,0:T(2,128)(2,1)S(1)} %collective-permute-done), kind=kOutput, calls=%fused_computation.10 | convolution fusion | flops 1587640320 | bytes 6579200 | tf_op jit(solution)/shard_map/tc,jc->tj/dot_general | solution.py:39
  29.9 0.7 fusion.10
  30.5 0.2 copy.10
  30.8 0.2 pad_dynamic-update-slice_fusion.3
  31.0 0.2 pad_dynamic-update-slice_fusion.2
  31.2 0.2 pad_dynamic-update-slice_fusion.1
  31.4 0.2 pad_dynamic-update-slice_fusion
  31.6 0.7 copy-done.4
  32.2 4.2 %convolution_convert_fusion = bf16[1280,1280]{1,0:T(8,128)(2,1)} fusion(bf16[1280,644]{1,0:T(8,128)(2,1)S(1)} %bitcast.49, bf16[2,1280]{1,0:T(2,128)(2,1)S(1)} %collective-permute-done.1, bf16[640,1280]{1,0:T(8,128)(2,1)S(1)} %copy-done.4, bf16[2,1280]{1,0:T(2,128)(2,1)S(1)} %collective-permute-done), kind=kOutput, calls=%fused_computation | convolution fusion | flops 2116843520 | bytes 6574080 | tf_op jit(solution)/shard_map/dot_general | solution.py:55
  36.4 1.4 %collective-permute-start.2 = (bf16[2,192]{1,0:T(2,128)(2,1)S(1)}, bf16[2,192]{1,0:T(2,128)(2,1)S(1)}, u32[]{:S(2)}, u32[]{:S(2)}) collective-permute-start(bf16[2,192]{1,0:T(2,128)(2,1)S(1)} %get-tuple-element.4), channel_id=1, source_target_pairs={{8,0},{16,8},{24,16},{32,24},{40,32},{48,40},{56,48},{64,56},{72,6... | collective-permute-start | bytes 2312 | tf_op jit(solution)/shard_map/ppermute | solution.py:15
  37.9 0.2 copy-done.2
  38.1 0.6 fusion.14
  38.7 4.3 %collective-permute-start.3 = (bf16[2,192]{1,0:T(2,128)(2,1)S(1)}, bf16[2,192]{1,0:T(2,128)(2,1)S(1)}, u32[]{:S(2)}, u32[]{:S(2)}) collective-permute-start(bf16[2,192]{1,0:T(2,128)(2,1)S(1)} %get-tuple-element.5), channel_id=1, source_target_pairs={{0,8},{8,16},{16,24},{24,32},{32,40},{40,48},{48,56},{56,64},{64,7... | collective-permute-start | bytes 2312 | tf_op jit(solution)/shard_map/ppermute | solution.py:12
  43.0 0.6 fusion.16
  43.6 0.7 collective-permute-done.3
  44.3 0.6 fusion.11
  44.9 0.6 fusion.1
  45.5 1.7 %fusion.3 = bf16[1280,640]{0,1:T(8,128)(2,1)S(1)} fusion(f32[640,1280]{1,0:T(8,128)S(1)} %fusion.11, f32[640,1280]{1,0:T(8,128)S(1)} %fusion.1, bf16[192,5,1280]{2,0,1:T(8,128)(2,1)} %param.4, bf16[2,192]{1,0:T(2,128)(2,1)S(1)} %collective-permute-done.3, bf16[640,192]{1,0:T(8,128)(2,1)S(1)} %fusion.10), kind=kOutput, calls=%fused_computation.6 | convolution fusion | flops 317521920 | bytes 8930048 | tf_op jit(solution)/shard_map/lo,oc->cl/dot_general | solution.py:68
  47.2 2.2 %copy.11 = bf16[1280,640]{1,0:T(8,128)(2,1)} copy(bf16[1280,640]{0,1:T(8,128)(2,1)S(1)} %fusion.3) | data formatting | bytes 3276800 | tf_op jit(solution)/shard_map/add | solution.py:68
  49.4 25.2 %all_to_all.10 = bf16[8,160,640]{2,1,0:T(8,128)(2,1)S(1)} all-to-all(bf16[8,160,640]{2,1,0:T(8,128)(2,1)} %bitcast.44), channel_id=1, replica_groups=mesh['dp'=4,'seq'=16,'section'=8] {'section'}, dimensions={0} | all-to-all | bytes 3276800 | tf_op jit(solution)/shard_map/all_to_all | solution.py:75
  74.6 0.9 reduce_sum.12
  75.6 40.6 %reduce-scatter.2.cloned.1.call-done = bf16[1,80,1280]{2,1,0:T(8,128)(2,1)} async-done(((bf16[16,80,1280]{2,1,0:T(8,128)(2,1)}), bf16[1,80,1280]{2,1,0:T(8,128)(2,1)}) %reduce-scatter.2.cloned.1.call-update) | async-done | bytes 204816 | tf_op jit(solution)/shard_map/reduce_scatter | solution.py:57
  116.2 14.0 %all_gather.3 = bf16[4,80,1280]{2,1,0:T(8,128)(2,1)S(1)} all-gather(bf16[1,80,1280]{2,1,0:T(8,128)(2,1)} %reduce-scatter.2.cloned.1.call-done), channel_id=1, replica_groups=mesh['dp'=4,'seq'=16,'section'=8] {'dp'}, dimensions={0}, use_global_device_ids=true | all-gather | bytes 1024000 | tf_op jit(solution)/shard_map/all_gather | solution.py:59
  130.4 0.8 slice_bitcast_fusion
  (24 shorter events, 0.7 us)
Async XLA Ops:
  7.2 13.6 %copy-start = (bf16[1,640,1280]{2,1,0:T(8,128)(2,1)S(1)}, bf16[1,640,1280]{2,1,0:T(8,128)(2,1)}, u32[]{:S(2)}) copy-start(bf16[1,640,1280]{2,1,0:T(8,128)(2,1)} %param.3) | copy-start | bytes 4915204
  9.6 20.1 %all-to-all-start = ((bf16[8,80,192]{2,1,0:T(8,128)(2,1)}), bf16[8,80,192]{2,1,0:T(8,128)(2,1)S(1)}, u32[]{:S(2)}, u32[]{:S(2)}) async-start(bf16[8,80,192]{2,1,0:T(8,128)(2,1)} %bitcast), calls=%async_computation | async-start | bytes 655360 | tf_op jit(solution)/shard_map/all_to_all | solution.py:35
  18.9 97.4 %reduce-scatter.2.cloned.1.call-start = ((), (), s32[]{:S(2)}) async-start(), calls=%async_computation.3 | async-start | bytes 3481600 | tf_op jit(solution)/shard_map/reduce_scatter | solution.py:57
  20.9 7.0 %copy-start.1 = (bf16[192,5,1280]{2,0,1:T(8,128)(2,1)S(1)}, bf16[192,5,1280]{2,0,1:T(8,128)(2,1)}, u32[]{:S(2)}) copy-start(bf16[192,5,1280]{2,0,1:T(8,128)(2,1)} %param.4) | copy-start | bytes 7372804
  20.9 2.9 %collective-permute-start = (bf16[2,1280]{1,0:T(2,128)(2,1)S(1)}, bf16[2,1280]{1,0:T(2,128)(2,1)S(1)}, u32[]{:S(2)}, u32[]{:S(2)}) collective-permute-start(bf16[2,1280]{1,0:T(2,128)(2,1)S(1)} %get-tuple-element.2), channel_id=1, source_target_pairs={{0,8},{8,16},{16,24},{24,32},{32,40},{40,48},{48,56},{56,64},{64,7... | collective-permute-start | bytes 15368 | tf_op jit(solution)/shard_map/ppermute | solution.py:12
  22.3 5.5 %collective-permute-start.1 = (bf16[2,1280]{1,0:T(2,128)(2,1)S(1)}, bf16[2,1280]{1,0:T(2,128)(2,1)S(1)}, u32[]{:S(2)}, u32[]{:S(2)}) collective-permute-start(bf16[2,1280]{1,0:T(2,128)(2,1)S(1)} %get-tuple-element.3), channel_id=1, source_target_pairs={{8,0},{16,8},{24,16},{32,24},{40,32},{48,40},{56,48},{64,56},{72,6... | collective-permute-start | bytes 15368 | tf_op jit(solution)/shard_map/ppermute | solution.py:15
  23.8 4.1 %copy-start.3 = (bf16[640,1280]{1,0:T(8,128)(2,1)}, bf16[640,1280]{1,0:T(8,128)(2,1)S(1)}, u32[]{:S(2)}) copy-start(bf16[640,1280]{1,0:T(8,128)(2,1)S(1)} %fusion.40) | copy-start | bytes 4915204
  30.8 1.4 %copy-start.4 = (bf16[640,1280]{1,0:T(8,128)(2,1)S(1)}, bf16[640,1280]{1,0:T(8,128)(2,1)}, u32[]{:S(2)}) copy-start(bf16[640,1280]{1,0:T(8,128)(2,1)} %copy-done.3) | copy-start | bytes 4915204
  36.4 1.7 %copy-start.2 = (bf16[192,5,1280]{2,0,1:T(8,128)(2,1)S(1)}, bf16[192,5,1280]{2,0,1:T(8,128)(2,1)}, u32[]{:S(2)}) copy-start(bf16[192,5,1280]{2,0,1:T(8,128)(2,1)} %param.4) | copy-start | bytes 7372804
  36.4 6.6 %collective-permute-start.2 = (bf16[2,192]{1,0:T(2,128)(2,1)S(1)}, bf16[2,192]{1,0:T(2,128)(2,1)S(1)}, u32[]{:S(2)}, u32[]{:S(2)}) collective-permute-start(bf16[2,192]{1,0:T(2,128)(2,1)S(1)} %get-tuple-element.4), channel_id=1, source_target_pairs={{8,0},{16,8},{24,16},{32,24},{40,32},{48,40},{56,48},{64,56},{72,6... | collective-permute-start | bytes 2312 | tf_op jit(solution)/shard_map/ppermute | solution.py:15
  38.7 5.6 %collective-permute-start.3 = (bf16[2,192]{1,0:T(2,128)(2,1)S(1)}, bf16[2,192]{1,0:T(2,128)(2,1)S(1)}, u32[]{:S(2)}, u32[]{:S(2)}) collective-permute-start(bf16[2,192]{1,0:T(2,128)(2,1)S(1)} %get-tuple-element.5), channel_id=1, source_target_pairs={{0,8},{8,16},{16,24},{24,32},{32,40},{40,48},{48,56},{56,64},{64,7... | collective-permute-start | bytes 2312 | tf_op jit(solution)/shard_map/ppermute | solution.py:12
Sparse Core Ops, SparseCore 0:
  36.5 79.6 reduce-scatter.1

commit v13 on v12

--- a/solution.py
+++ b/solution.py
@@ -4,15 +4,17 @@
 from jax.sharding import PartitionSpec as P
 
 
-def extended(block, sides, width):
+def extended(block, sides, width, anchor=None):
     for axis, dim in sides:
         count = lax.axis_size(axis)
         forward = [(i, i + 1) for i in range(count - 1)]
         backward = [(target, source) for source, target in forward]
-        low = lax.ppermute(
-            lax.slice_in_dim(block, block.shape[dim] - width, None, axis=dim), axis, forward
-        )
-        high = lax.ppermute(lax.slice_in_dim(block, 0, width, axis=dim), axis, backward)
+        tail = lax.slice_in_dim(block, block.shape[dim] - width, None, axis=dim)
+        head = lax.slice_in_dim(block, 0, width, axis=dim)
+        if anchor is not None:
+            tail, head = tail + anchor, head + anchor
+        low = lax.ppermute(tail, axis, forward)
+        high = lax.ppermute(head, axis, backward)
         block = jnp.concatenate([low, block, high], axis=dim)
     return block
 
@@ -34,12 +36,34 @@
     grouped = jnp.repeat(trunk_grad[0].reshape(rows, n_section, out_ch), 2, axis=0).transpose(1, 0, 2)
     upsampled = lax.all_to_all(grouped, "section", 0, 0, tiled=True).reshape(2 * rows * n_section, out_ch)
     anchor = (grouped[0, 0, 0] * 0).astype(local_signal.dtype)
-    padded = extended(local_signal + anchor, (("seq", 0),), 2)
+    padded = extended(local_signal, (("seq", 0),), 2, anchor)
     stacked = kernel.transpose(1, 0, 2).reshape(taps_count * out_ch, in_ch)
-    per_tap = jnp.einsum("tc,jc->tj", padded, stacked, preferred_element_type=jnp.float32)
+    half = (taps_count - 1) // 2
+    per_tap = jnp.pad(
+        jnp.einsum("tc,jc->tj", local_signal, stacked, preferred_element_type=jnp.float32),
+        ((half, half), (0, 0)),
+    )
+    edges = jnp.concatenate([padded[:half], padded[length + half :]], axis=0)
+    edge_taps = jnp.einsum("tc,jc->tj", edges, stacked, preferred_element_type=jnp.float32)
+    top = []
+    for r in range(half):
+        top.append(sum(edge_taps[r + k, k * out_ch : (k + 1) * out_ch] for k in range(half - r)))
+    bottom = []
+    for r in range(half):
+        t = length - half + r
+        terms = [
+            edge_taps[half + (t + k - (length + half)), k * out_ch : (k + 1) * out_ch]
+            for k in range(taps_count)
+            if t + k >= length + half
+        ]
+        bottom.append(sum(terms))
+    correction = jnp.concatenate(
+        [jnp.stack(top), jnp.zeros((length - 2 * half, out_ch), jnp.float32), jnp.stack(bottom)], axis=0
+    )
     linear = per_tap[0:length, 0:out_ch]
     for k in range(1, taps_count):
         linear = linear + per_tap[k : k + length, k * out_ch : (k + 1) * out_ch]
+    linear = linear + correction
     grad_hidden = 0.5 * upsampled.astype(jnp.float32)
     grad_pre = (grad_hidden * gelu_slope(linear)).astype(jnp.bfloat16)
     grad_ext = extended(grad_pre, (("seq", 0),), 2)

time: 139 us -> 145 us (1.043)
  matrix products: 10.1 us -> 15.7 us
  waiting for transfers between devices: 45.4 us -> 41 us
  other arithmetic: 2.07 us -> 5.63 us
    dot_general x1 -> x2, matrix products: 1.92 us -> 6.67 us  [the longest x1 5.9 us: shards(): jnp.einsum('tc,jc->tj', local_signal, stacked, preferred_element_type=jnp...]
    ppermute x4, waiting for transfers between devices: 4.76 us -> 0.97 us  [the longest x2 0.97 us: extended(): low = lax.ppermute(tail, axis, forward)]
    ppermute x4, starting transfers between devices: 8.47 us -> 11.6 us  [the longest x2 9 us: extended(): low = lax.ppermute(tail, axis, forward)]
    all_to_all x1, starting transfers between devices: 9.22 us -> 7.31 us  [shards(): lax.all_to_all(grouped, 'section', 0, 0, tiled=True)]
    convert_element_type x1, other arithmetic: 0.66 us -> 2.51 us  [shards(): grad_pre = (grad_hidden * gelu_slope(linear)).astype(jnp.bfloat16)]
  transfers between devices with their start and end apart: 6 -> 6, of which waited for: 3 -> 2; matrix products, arithmetic and copies ran while one was open for 8% -> 12% of each run, Pallas kernels for 0% -> 0%
where the time goes in v13:
time: 145 us
  waiting for transfers between devices  41 us (28%)
  blocking collectives  39 us (27%)
  starting transfers between devices  18.9 us (13%)
  matrix products  15.7 us (11%)
  between operations  14.9 us (10%)
  local copies, waits for them, and re-layouts  9.67 us (7%)
  other arithmetic  5.63 us (4%)
    reduce_scatter x1, waiting for transfers between devices, shards(): lax.psum_scatter(partial, 'seq', scatter_dimension=0, tiled=True)[0]  40 us
    all_to_all x1, blocking collectives, shards(): received = lax.all_to_all(groups, 'section', 0, 0, tiled=True)  25 us
    all_gather x1, blocking collectives, shards(): lax.all_gather(weight_part, 'dp', axis=0, tiled=False).astype(jnp.float32)  14 us
    ppermute x2, starting transfers between devices, extended(): low = lax.ppermute(tail, axis, forward)  9 us
    all_to_all x1, starting transfers between devices, shards(): lax.all_to_all(grouped, 'section', 0, 0, tiled=True)  7.31 us
    dot_general x1, matrix products, shards(): jnp.einsum('tc,jc->tj', local_signal, stacked, preferred_element_type=jnp...  5.9 us
    dot_general x1, matrix products, shards(): jnp.dot(banded, padded, preferred_element_type=jnp.float32)  4.17 us
    dot_general x4, matrix products, shards(): jnp.einsum('lo,oc->cl', grad_ext[4 - offset:4 - offset + length], kernel[...  4.1 us
  transfers between devices with their start and end apart: 6, of which 2 were waited for; matrix products, arithmetic and copies ran while one was open for 12% of the time, Pallas kernels for 0%

profile of v13, /device:TPU:6, one launch (start us, length us, event | category | flops | bytes accessed | tf_op | source)
XLA Modules:
  0.0 144.8 jit_solution(2929871705028580231)
XLA Ops:
  7.2 1.1 reshape_squeeze.3
  8.3 0.5 slice.128
  9.5 0.8 add_bitcast_fusion.1
  10.2 3.8 %collective-permute-start = (bf16[2,1280]{1,0:T(2,128)(2,1)S(1)}, bf16[2,1280]{1,0:T(2,128)(2,1)S(1)}, u32[]{:S(2)}, u32[]{:S(2)}) collective-permute-start(bf16[2,1280]{1,0:T(2,128)(2,1)S(1)} %get-tuple-element.2), channel_id=1, source_target_pairs={{0,8},{8,16},{16,24},{24,32},{32,40},{40,48},{48,56},{56,64},{64,7... | collective-permute-start | bytes 15368 | tf_op jit(solution)/shard_map/ppermute | solution.py:16
  14.1 1.3 collective-permute-start.1
  15.4 0.8 copy.21
  16.1 7.3 %all-to-all-start = ((bf16[8,80,192]{2,1,0:T(8,128)(2,1)}), bf16[8,80,192]{2,1,0:T(8,128)(2,1)}, u32[]{:S(2)}, u32[]{:S(2)}) async-start(bf16[8,80,192]{2,1,0:T(8,128)(2,1)} %copy.21), calls=%async_computation | async-start | bytes 655360 | tf_op jit(solution)/shard_map/all_to_all | solution.py:37
  23.5 5.9 %fusion.49 = f32[640,960]{0,1:T(8,128)} fusion(bf16[960,1280]{1,0:T(8,128)(2,1)} %bitcast.45, bf16[1,640,1280]{2,1,0:T(8,128)(2,1)} %param.3), kind=kOutput, calls=%fused_computation.75 | convolution fusion | flops 1572864000 | bytes 6553600 | tf_op jit(solution)/shard_map/tc,jc->tj/dot_general | solution.py:43
  29.4 0.8 fusion.39
  30.1 0.2 slice_add_fusion.3
  30.4 1.1 concatenate.22
  31.4 1.0 convert_multiply_fusion
  32.5 1.0 copy.28
  33.5 2.5 %fusion.14 = bf16[640,192]{0,1:T(8,128)(2,1)S(1)} fusion(f32[640,192]{0,1:T(8,128)} %copy.28, f32[640,192]{0,1:T(8,128)} %concatenate.22, f32[640,960]{0,1:T(8,128)} %fusion.49), kind=kLoop, calls=%fused_computation.23 | loop fusion | flops 1843200 | bytes 4177920 | tf_op jit(solution)/shard_map/convert_element_type | solution.py:68
  36.2 0.2 pad_dynamic-update-slice_fusion.3
  36.3 0.2 pad_dynamic-update-slice_fusion.2
  36.9 0.6 copy-done.1
  37.5 4.2 %convolution_convert_fusion = bf16[1280,1280]{1,0:T(8,128)(2,1)} fusion(bf16[1280,644]{1,0:T(8,128)(2,1)S(1)} %bitcast.54, bf16[2,1280]{1,0:T(2,128)(2,1)S(1)} %collective-permute-done.1, bf16[640,1280]{1,0:T(8,128)(2,1)S(1)} %bitcast.55, bf16[2,1280]{1,0:T(2,128)(2,1)S(1)} %collective-permute-done), kind=kOutput, calls=%fused_computation | convolution fusion | flops 2116843520 | bytes 6574080 | tf_op jit(solution)/shard_map/dot_general | solution.py:79
  41.8 1.3 collective-permute-start.2
  43.1 0.6 fusion.23
  43.7 5.2 %collective-permute-start.3 = (bf16[2,192]{0,1:T(8,128)(2,1)S(1)}, bf16[2,192]{0,1:T(8,128)(2,1)S(1)}, u32[]{:S(2)}, u32[]{:S(2)}) collective-permute-start(bf16[2,192]{0,1:T(8,128)(2,1)S(1)} %get-tuple-element.9), channel_id=1, source_target_pairs={{0,8},{8,16},{16,24},{24,32},{32,40},{40,48},{48,56},{56,64},{64,7... | collective-permute-start | bytes 2312 | tf_op jit(solution)/shard_map/ppermute | solution.py:16
  48.9 0.8 fusion.25
  49.7 1.0 collective-permute-done.3
  50.7 0.7 fusion.20
  51.4 0.8 fusion.1
  52.2 2.0 %fusion.3 = bf16[1280,640]{0,1:T(8,128)(2,1)} fusion(f32[640,1280]{1,0:T(8,128)S(1)} %fusion.20, f32[640,1280]{1,0:T(8,128)S(1)} %fusion.1, bf16[192,5,1280]{2,0,1:T(8,128)(2,1)S(1)} %copy-done, bf16[2,192]{0,1:T(8,128)(2,1)S(1)} %collective-permute-done.3, bf16[640,192]{0,1:T(8,128)(2,1)S(1)} %fusion.14), kind=kOutput, calls=%fused_computation.10 | convolution fusion | flops 317521920 | bytes 8978432 | tf_op jit(solution)/shard_map/lo,oc->cl/dot_general | solution.py:92
  54.1 2.8 %copy.29 = bf16[1280,640]{1,0:T(8,128)(2,1)S(1)} copy(bf16[1280,640]{0,1:T(8,128)(2,1)} %fusion.3) | data formatting | bytes 3276800 | tf_op jit(solution)/shard_map/add | solution.py:92
  57.0 25.0 %all_to_all.10 = bf16[8,160,640]{2,1,0:T(8,128)(2,1)S(1)} all-to-all(bf16[8,160,640]{2,1,0:T(8,128)(2,1)S(1)} %bitcast.47), channel_id=1, replica_groups=mesh['dp'=4,'seq'=16,'section'=8] {'section'}, dimensions={0} | all-to-all | bytes 3276800 | tf_op jit(solution)/shard_map/all_to_all | solution.py:99
  82.0 0.9 reduce_sum.12
  83.0 40.0 %reduce-scatter.2.cloned.1.call-done = bf16[1,80,1280]{2,1,0:T(8,128)(2,1)} async-done(((bf16[16,80,1280]{2,1,0:T(8,128)(2,1)}), bf16[1,80,1280]{2,1,0:T(8,128)(2,1)}) %reduce-scatter.2.cloned.1.call-update) | async-done | bytes 204816 | tf_op jit(solution)/shard_map/reduce_scatter | solution.py:81
  123.0 14.0 %all_gather.3 = bf16[4,80,1280]{2,1,0:T(8,128)(2,1)S(1)} all-gather(bf16[1,80,1280]{2,1,0:T(8,128)(2,1)} %reduce-scatter.2.cloned.1.call-done), channel_id=1, replica_groups=mesh['dp'=4,'seq'=16,'section'=8] {'dp'}, dimensions={0}, use_global_device_ids=true | all-gather | bytes 1024000 | tf_op jit(solution)/shard_map/all_gather | solution.py:83
  137.2 0.8 slice_bitcast_fusion
  (19 shorter events, 0.8 us)
Async XLA Ops:
  10.2 19.1 %collective-permute-start = (bf16[2,1280]{1,0:T(2,128)(2,1)S(1)}, bf16[2,1280]{1,0:T(2,128)(2,1)S(1)}, u32[]{:S(2)}, u32[]{:S(2)}) collective-permute-start(bf16[2,1280]{1,0:T(2,128)(2,1)S(1)} %get-tuple-element.2), channel_id=1, source_target_pairs={{0,8},{8,16},{16,24},{24,32},{32,40},{40,48},{48,56},{56,64},{64,7... | collective-permute-start | bytes 15368 | tf_op jit(solution)/shard_map/ppermute | solution.py:16
  14.1 15.3 %collective-permute-start.1 = (bf16[2,1280]{1,0:T(2,128)(2,1)S(1)}, bf16[2,1280]{1,0:T(2,128)(2,1)S(1)}, u32[]{:S(2)}, u32[]{:S(2)}) collective-permute-start(bf16[2,1280]{1,0:T(2,128)(2,1)S(1)} %get-tuple-element.3), channel_id=1, source_target_pairs={{8,0},{16,8},{24,16},{32,24},{40,32},{48,40},{56,48},{64,56},{72,6... | collective-permute-start | bytes 15368 | tf_op jit(solution)/shard_map/ppermute | solution.py:17
  16.1 15.3 %all-to-all-start = ((bf16[8,80,192]{2,1,0:T(8,128)(2,1)}), bf16[8,80,192]{2,1,0:T(8,128)(2,1)}, u32[]{:S(2)}, u32[]{:S(2)}) async-start(bf16[8,80,192]{2,1,0:T(8,128)(2,1)} %copy.21), calls=%async_computation | async-start | bytes 655360 | tf_op jit(solution)/shard_map/all_to_all | solution.py:37
  23.4 99.5 %reduce-scatter.2.cloned.1.call-start = ((), (), s32[]{:S(2)}) async-start(), calls=%async_computation.3 | async-start | bytes 3481600 | tf_op jit(solution)/shard_map/reduce_scatter | solution.py:81
  23.5 5.9 %copy-start = (bf16[192,5,1280]{2,0,1:T(8,128)(2,1)S(1)}, bf16[192,5,1280]{2,0,1:T(8,128)(2,1)}, u32[]{:S(2)}) copy-start(bf16[192,5,1280]{2,0,1:T(8,128)(2,1)} %param.4) | copy-start | bytes 7372804
  36.1 1.4 copy-start.1
  41.8 7.1 %collective-permute-start.2 = (bf16[2,192]{0,1:T(8,128)(2,1)S(1)}, bf16[2,192]{0,1:T(8,128)(2,1)S(1)}, u32[]{:S(2)}, u32[]{:S(2)}) collective-permute-start(bf16[2,192]{0,1:T(8,128)(2,1)S(1)} %get-tuple-element.8), channel_id=1, source_target_pairs={{8,0},{16,8},{24,16},{32,24},{40,32},{48,40},{56,48},{64,56},{72,6... | collective-permute-start | bytes 2312 | tf_op jit(solution)/shard_map/ppermute | solution.py:17
  43.7 6.9 %collective-permute-start.3 = (bf16[2,192]{0,1:T(8,128)(2,1)S(1)}, bf16[2,192]{0,1:T(8,128)(2,1)S(1)}, u32[]{:S(2)}, u32[]{:S(2)}) collective-permute-start(bf16[2,192]{0,1:T(8,128)(2,1)S(1)} %get-tuple-element.9), channel_id=1, source_target_pairs={{0,8},{8,16},{16,24},{24,32},{32,40},{40,48},{48,56},{56,64},{64,7... | collective-permute-start | bytes 2312 | tf_op jit(solution)/shard_map/ppermute | solution.py:16
Sparse Core Ops, SparseCore 0:
  41.8 81.0 reduce-scatter.1

commit v14 on v9

--- a/solution.py
+++ b/solution.py
@@ -31,7 +31,7 @@
     in_ch = kernel.shape[2]
     n_section = lax.axis_size("section")
     rows = trunk_grad.shape[1]
-    grouped = jnp.repeat(trunk_grad[0].reshape(rows, n_section, out_ch), 2, axis=0).transpose(1, 0, 2)
+    grouped = jnp.repeat(trunk_grad[0], 2, axis=0).reshape(2 * rows, n_section, out_ch).transpose(1, 0, 2)
     upsampled = lax.all_to_all(grouped, "section", 0, 0, tiled=True).reshape(2 * rows * n_section, out_ch)
     padded = extended(local_signal, (("seq", 0),), 2)
     stacked = kernel.transpose(1, 0, 2).reshape(taps_count * out_ch, in_ch)

time: 139 us -> 139 us (level)
  no operation moved by 1% of the time
where the time goes in v14:
time: 139 us; the launch traced here: 138 us
  waiting for transfers between devices  43.9 us (32%)
  blocking collectives  39.9 us (29%)
  starting transfers between devices  18.2 us (13%)
  between operations  14.2 us (10%)
  matrix products  12.3 us (9%)
  local copies, waits for them, and re-layouts  7.65 us (6%)
  other arithmetic  1.85 us (1%)
    reduce_scatter x1, waiting for transfers between devices, shards(): lax.psum_scatter(partial, 'seq', scatter_dimension=0, tiled=True)[0]  41.1 us
    all_to_all x1, blocking collectives, shards(): received = lax.all_to_all(groups, 'section', 0, 0, tiled=True)  26 us
    all_gather x1, blocking collectives, shards(): lax.all_gather(weight_part, 'dp', axis=0, tiled=False).astype(jnp.float32)  13.9 us
    ppermute x2, starting transfers between devices, extended(): lax.ppermute(lax.slice_in_dim(block, block.shape[dim] - width, None, axis...  8.79 us
    all_to_all x1, starting transfers between devices, shards(): lax.all_to_all(grouped, 'section', 0, 0, tiled=True)  6.69 us
    dot_general x1, matrix products, shards(): jnp.dot(banded, padded, preferred_element_type=jnp.float32)  4.18 us
    dot_general x1, matrix products, shards(): jnp.einsum('tc,jc->tj', padded, stacked, preferred_element_type=jnp.float32)  4.1 us
    dot_general x4, matrix products, shards(): jnp.einsum('lo,oc->cl', grad_ext[4 - offset:4 - offset + length], kernel[...  3.38 us
  transfers between devices with their start and end apart: 6, of which 3 were waited for; matrix products, arithmetic and copies ran while one was open for 10% of the time, Pallas kernels for 0%

profile of v14, /device:TPU:6, one launch (start us, length us, event | category | flops | bytes accessed | tf_op | source)
XLA Modules:
  0.0 138.0 jit_solution(10787459043167057891)
XLA Ops:
  7.2 0.8 slice_bitcast_fusion.2
  7.9 3.8 %collective-permute-start = (bf16[2,1280]{1,0:T(2,128)(2,1)S(1)}, bf16[2,1280]{1,0:T(2,128)(2,1)S(1)}, u32[]{:S(2)}, u32[]{:S(2)}) collective-permute-start(bf16[2,1280]{1,0:T(2,128)(2,1)S(1)} %get-tuple-element.2), channel_id=1, source_target_pairs={{0,8},{8,16},{16,24},{24,32},{32,40},{40,48},{48,56},{56,64},{64,7... | collective-permute-start | bytes 15368 | tf_op jit(solution)/shard_map/ppermute | solution.py:12
  11.8 1.3 collective-permute-start.1
  13.1 1.0 broadcast_in_dim.6
  14.1 0.3 reshape_reshape.3
  14.4 0.8 copy.8
  15.2 6.7 %all-to-all-start = ((bf16[8,80,192]{2,1,0:T(8,128)(2,1)}), bf16[8,80,192]{2,1,0:T(8,128)(2,1)S(1)}, u32[]{:S(2)}, u32[]{:S(2)}) async-start(bf16[8,80,192]{2,1,0:T(8,128)(2,1)} %copy.8), calls=%async_computation | async-start | bytes 655360 | tf_op jit(solution)/shard_map/all_to_all | solution.py:35
  21.9 4.1 %fusion.4 = f32[644,960]{1,0:T(8,128)S(1)} fusion(bf16[960,1280]{1,0:T(8,128)(2,1)} %bitcast.43, bf16[2,1280]{1,0:T(2,128)(2,1)S(1)} %collective-permute-done.1, bf16[640,1280]{1,0:T(8,128)(2,1)} %bitcast.49, bf16[2,1280]{1,0:T(2,128)(2,1)S(1)} %collective-permute-done), kind=kOutput, calls=%fused_computation.9 | convolution fusion | flops 1587640320 | bytes 6579200 | tf_op jit(solution)/shard_map/tc,jc->tj/dot_general | solution.py:38
  26.0 2.0 %all-to-all-done = bf16[8,80,192]{2,1,0:T(8,128)(2,1)S(1)} async-done(((bf16[8,80,192]{2,1,0:T(8,128)(2,1)}), bf16[8,80,192]{2,1,0:T(8,128)(2,1)S(1)}, u32[]{:S(2)}, u32[]{:S(2)}) %all-to-all-start) | async-done | bytes 245792 | tf_op jit(solution)/shard_map/all_to_all | solution.py:35
  28.1 0.7 fusion.10
  28.8 0.2 copy.9
  29.1 0.2 pad_dynamic-update-slice_fusion.3
  29.3 0.2 pad_dynamic-update-slice_fusion.2
  29.4 0.2 pad_dynamic-update-slice_fusion.1
  29.6 0.2 pad_dynamic-update-slice_fusion
  29.8 0.6 copy-done.1
  30.4 4.2 %convolution_convert_fusion = bf16[1280,1280]{1,0:T(8,128)(2,1)} fusion(bf16[1280,644]{1,0:T(8,128)(2,1)S(1)} %bitcast.48, bf16[2,1280]{1,0:T(2,128)(2,1)S(1)} %collective-permute-done.1, bf16[640,1280]{1,0:T(8,128)(2,1)S(1)} %bitcast.50, bf16[2,1280]{1,0:T(2,128)(2,1)S(1)} %collective-permute-done), kind=kOutput, calls=%fused_computation | convolution fusion | flops 2116843520 | bytes 6574080 | tf_op jit(solution)/shard_map/dot_general | solution.py:54
  34.6 1.4 %collective-permute-start.2 = (bf16[2,192]{1,0:T(2,128)(2,1)S(1)}, bf16[2,192]{1,0:T(2,128)(2,1)S(1)}, u32[]{:S(2)}, u32[]{:S(2)}) collective-permute-start(bf16[2,192]{1,0:T(2,128)(2,1)S(1)} %get-tuple-element.4), channel_id=1, source_target_pairs={{8,0},{16,8},{24,16},{32,24},{40,32},{48,40},{56,48},{64,56},{72,6... | collective-permute-start | bytes 2312 | tf_op jit(solution)/shard_map/ppermute | solution.py:15
  36.0 0.2 copy-done
  36.2 0.6 fusion.14
  36.8 5.0 %collective-permute-start.3 = (bf16[2,192]{1,0:T(2,128)(2,1)S(1)}, bf16[2,192]{1,0:T(2,128)(2,1)S(1)}, u32[]{:S(2)}, u32[]{:S(2)}) collective-permute-start(bf16[2,192]{1,0:T(2,128)(2,1)S(1)} %get-tuple-element.5), channel_id=1, source_target_pairs={{0,8},{8,16},{16,24},{24,32},{32,40},{40,48},{48,56},{56,64},{64,7... | collective-permute-start | bytes 2312 | tf_op jit(solution)/shard_map/ppermute | solution.py:12
  41.8 0.6 fusion.16
  42.4 0.7 collective-permute-done.3
  43.1 0.6 fusion.11
  43.7 0.7 fusion.1
  44.3 1.6 %fusion.3 = bf16[1280,640]{0,1:T(8,128)(2,1)S(1)} fusion(f32[640,1280]{1,0:T(8,128)S(1)} %fusion.11, f32[640,1280]{1,0:T(8,128)S(1)} %fusion.1, bf16[192,5,1280]{2,0,1:T(8,128)(2,1)} %param.4, bf16[2,192]{1,0:T(2,128)(2,1)S(1)} %collective-permute-done.3, bf16[640,192]{1,0:T(8,128)(2,1)S(1)} %fusion.10), kind=kOutput, calls=%fused_computation.6 | convolution fusion | flops 317521920 | bytes 8930048 | tf_op jit(solution)/shard_map/lo,oc->cl/dot_general | solution.py:67
  46.0 2.2 %copy.10 = bf16[1280,640]{1,0:T(8,128)(2,1)} copy(bf16[1280,640]{0,1:T(8,128)(2,1)S(1)} %fusion.3) | data formatting | bytes 3276800 | tf_op jit(solution)/shard_map/add | solution.py:67
  48.2 26.0 %all_to_all.10 = bf16[8,160,640]{2,1,0:T(8,128)(2,1)S(1)} all-to-all(bf16[8,160,640]{2,1,0:T(8,128)(2,1)} %bitcast.41), channel_id=1, replica_groups=mesh['dp'=4,'seq'=16,'section'=8] {'section'}, dimensions={0} | all-to-all | bytes 3276800 | tf_op jit(solution)/shard_map/all_to_all | solution.py:74
  74.2 0.9 reduce_sum.12
  75.1 41.1 %reduce-scatter.2.cloned.1.call-done = bf16[1,80,1280]{2,1,0:T(8,128)(2,1)} async-done(((bf16[16,80,1280]{2,1,0:T(8,128)(2,1)}), bf16[1,80,1280]{2,1,0:T(8,128)(2,1)}) %reduce-scatter.2.cloned.1.call-update) | async-done | bytes 204816 | tf_op jit(solution)/shard_map/reduce_scatter | solution.py:56
  116.2 13.9 %all_gather.3 = bf16[4,80,1280]{2,1,0:T(8,128)(2,1)S(1)} all-gather(bf16[1,80,1280]{2,1,0:T(8,128)(2,1)} %reduce-scatter.2.cloned.1.call-done), channel_id=1, replica_groups=mesh['dp'=4,'seq'=16,'section'=8] {'dp'}, dimensions={0}, use_global_device_ids=true | all-gather | bytes 1024000 | tf_op jit(solution)/shard_map/all_gather | solution.py:58
  130.4 0.8 slice_bitcast_fusion
  (14 shorter events, 0.4 us)
Async XLA Ops:
  7.9 14.0 %collective-permute-start = (bf16[2,1280]{1,0:T(2,128)(2,1)S(1)}, bf16[2,1280]{1,0:T(2,128)(2,1)S(1)}, u32[]{:S(2)}, u32[]{:S(2)}) collective-permute-start(bf16[2,1280]{1,0:T(2,128)(2,1)S(1)} %get-tuple-element.2), channel_id=1, source_target_pairs={{0,8},{8,16},{16,24},{24,32},{32,40},{40,48},{48,56},{56,64},{64,7... | collective-permute-start | bytes 15368 | tf_op jit(solution)/shard_map/ppermute | solution.py:12
  11.8 10.1 %collective-permute-start.1 = (bf16[2,1280]{1,0:T(2,128)(2,1)S(1)}, bf16[2,1280]{1,0:T(2,128)(2,1)S(1)}, u32[]{:S(2)}, u32[]{:S(2)}) collective-permute-start(bf16[2,1280]{1,0:T(2,128)(2,1)S(1)} %get-tuple-element.3), channel_id=1, source_target_pairs={{8,0},{16,8},{24,16},{32,24},{40,32},{48,40},{56,48},{64,56},{72,6... | collective-permute-start | bytes 15368 | tf_op jit(solution)/shard_map/ppermute | solution.py:15
  15.2 12.8 %all-to-all-start = ((bf16[8,80,192]{2,1,0:T(8,128)(2,1)}), bf16[8,80,192]{2,1,0:T(8,128)(2,1)S(1)}, u32[]{:S(2)}, u32[]{:S(2)}) async-start(bf16[8,80,192]{2,1,0:T(8,128)(2,1)} %copy.8), calls=%async_computation | async-start | bytes 655360 | tf_op jit(solution)/shard_map/all_to_all | solution.py:35
  21.9 94.4 %reduce-scatter.2.cloned.1.call-start = ((), (), s32[]{:S(2)}) async-start(), calls=%async_computation.3 | async-start | bytes 3481600 | tf_op jit(solution)/shard_map/reduce_scatter | solution.py:56
  28.9 1.4 %copy-start.1 = (bf16[1,640,1280]{2,1,0:T(8,128)(2,1)S(1)}, bf16[1,640,1280]{2,1,0:T(8,128)(2,1)}, u32[]{:S(2)}) copy-start(bf16[1,640,1280]{2,1,0:T(8,128)(2,1)} %param.3) | copy-start | bytes 4915204
  34.5 1.7 %copy-start = (bf16[192,5,1280]{2,0,1:T(8,128)(2,1)S(1)}, bf16[192,5,1280]{2,0,1:T(8,128)(2,1)}, u32[]{:S(2)}) copy-start(bf16[192,5,1280]{2,0,1:T(8,128)(2,1)} %param.4) | copy-start | bytes 7372804
  34.6 7.2 %collective-permute-start.2 = (bf16[2,192]{1,0:T(2,128)(2,1)S(1)}, bf16[2,192]{1,0:T(2,128)(2,1)S(1)}, u32[]{:S(2)}, u32[]{:S(2)}) collective-permute-start(bf16[2,192]{1,0:T(2,128)(2,1)S(1)} %get-tuple-element.4), channel_id=1, source_target_pairs={{8,0},{16,8},{24,16},{32,24},{40,32},{48,40},{56,48},{64,56},{72,6... | collective-permute-start | bytes 2312 | tf_op jit(solution)/shard_map/ppermute | solution.py:15
  36.8 6.3 %collective-permute-start.3 = (bf16[2,192]{1,0:T(2,128)(2,1)S(1)}, bf16[2,192]{1,0:T(2,128)(2,1)S(1)}, u32[]{:S(2)}, u32[]{:S(2)}) collective-permute-start(bf16[2,192]{1,0:T(2,128)(2,1)S(1)} %get-tuple-element.5), channel_id=1, source_target_pairs={{0,8},{8,16},{16,24},{24,32},{32,40},{40,48},{48,56},{56,64},{64,7... | collective-permute-start | bytes 2312 | tf_op jit(solution)/shard_map/ppermute | solution.py:12
Sparse Core Ops, SparseCore 0:
  34.7 81.5 reduce-scatter.1
